TPU v7x, 128 devices: a whole 4x4x4 slice. The times are simulated.
128 devices in a mesh: seq: 16 (over y, x), expert: 4 (over z), mp: 2 (over core).
Axes of the slice: x: 4, y: 4, z: 4, core: 2. Of those that a mesh axis runs over, the one named last changes fastest.
Arguments:
- activations: bfloat16 [16384, 4096], P('seq', ('expert', 'mp')), may hold values from -6 to 6
- output_gradient: bfloat16 [16384, 4096], P('seq', ('expert', 'mp')), may hold values from -1.5 to 1.5
- input_state_map: bfloat16 [16384, 16], P('seq'), may hold values from -3 to 3
- output_state_map: bfloat16 [16384, 16], P('seq'), may hold values from -3 to 3
- head_decay_speed: float32 [64], P(('expert', 'mp')), may hold values from 3.0517578e-06 to 0.05, as said below
- spike_decay_level: int32 [16384], P('seq'), may hold values from 0 to 2, as said below
- assign: int32 [128], replicated, may hold values from 0 to 15, as said below
- expert_up_weight: bfloat16 [4, 4096, 12288], P('expert', 'mp', 'seq'), may hold values from -0.09375 to 0.09375
- expert_down_weight: bfloat16 [4, 12288, 4096], P('expert', 'seq', 'mp'), may hold values from -0.0546875 to 0.0546875
Outputs:
- grad_x: float32 [16384, 4096], P('seq', ('expert', 'mp'))
- grad_w_up: float32 [4, 4096, 12288], P('expert', 'mp', 'seq')
- grad_w_down: float32 [4, 12288, 4096], P('expert', 'seq', 'mp')
Inputs may be any that keep to these rules, and one draw needn't show every extreme that they name: `head_decay_speed`: some of the heads keep a tenth or more of their state over the whole sequence, the others lose it within some tens of tokens. `spike_decay_level`: at most three tokens of the sequence have a nonzero level. `assign`: numbers below 4 are the window's experts: the 8 blocks of one index of seq hold at most one block of each of them, each takes at most 8 blocks in all, and one takes exactly 8.
All inputs are finite; a program needn't handle non-finite values.
Results may differ from a plain program's by a relative error of at most 0.019.
Values may be sent and summed in bfloat16 or wider, within the bound.
No kernel may reach another device: no remote copies, remote signals or barrier semaphores. Data moves between devices by JAX's collectives and lax.ppermute only.
A program may use at most 128 MiB of HBM per device.

v0:
```python
import jax
import jax.numpy as jnp
from jax import lax
from jax.sharding import PartitionSpec as P

HEAD = 64
STATE = 16
BLOCK = 128


spike_position_step = 0.3
highest = lax.Precision.HIGHEST


def from_behind(value, axis, steps):
    count = lax.axis_size(axis)
    first, last = (max(0, -steps), min(count, count - steps))
    return lax.ppermute(value, axis, [(source, source + steps) for source in range(first, last)])


def rounded(rounded_in):
    return lax.optimization_barrier(rounded_in.astype(jnp.bfloat16)).astype(jnp.float32)


def split_parts(values):
    high_part = values.astype(jnp.bfloat16)
    low_part = (values - high_part.astype(jnp.float32)).astype(jnp.bfloat16)
    return (high_part, low_part)


def mixing(cum_block, scores, causal):
    spread = cum_block.T[:, :, None] - cum_block.T[:, None, :]
    spread = jnp.where(causal[None], spread, -jnp.inf)
    return jnp.exp(spread) * scores[None]


def narrow(gathered, exp_index, mp_index, half_width):
    row_set = lax.dynamic_index_in_dim(gathered, exp_index, 0, keepdims=False)
    return lax.dynamic_slice_in_dim(row_set, mp_index * half_width, half_width, 1)


def compact(select, gathered, half_width):
    shaped = gathered.reshape(select.shape[1], -1, half_width)
    rows_out = jnp.einsum("js,srf->jrf", select, shaped, preferred_element_type=jnp.float32)
    return rows_out.astype(jnp.bfloat16).reshape(-1, half_width)


def per_device(
    activations,
    output_gradient,
    input_state_map,
    output_state_map,
    head_decay_speed,
    spike_decay_level,
    assign,
    expert_up_weight,
    expert_down_weight,
):
    tokens, slice_width = activations.shape
    heads_dev = slice_width // HEAD
    seq_count = lax.axis_size("seq")
    exp_count = lax.axis_size("expert")
    mp_count = lax.axis_size("mp")
    seq_index = lax.axis_index("seq")
    exp_index = lax.axis_index("expert")
    mp_index = lax.axis_index("mp")
    my_slice = exp_index * mp_count + mp_index
    slice_half = my_slice // exp_count
    half_width = slice_width * exp_count
    slot_total = seq_count // 2
    input_scale = jnp.sqrt(1.0 - jnp.exp(-2.0 * head_decay_speed))
    cum_level = jnp.cumsum(
        -head_decay_speed[None, :]
        - spike_position_step * spike_decay_level.astype(jnp.float32)[:, None],
        axis=0,
    )
    b_float = input_state_map.astype(jnp.float32)
    c_float = output_state_map.astype(jnp.float32)
    act_heads = activations.reshape(tokens, heads_dev, HEAD)
    scaled = act_heads.astype(jnp.float32) * input_scale[None, :, None]
    span_rows = min(512, tokens)
    span_count = tokens // span_rows
    causal = jnp.arange(span_rows)[:, None] >= jnp.arange(span_rows)[None, :]
    zero_level = jnp.zeros((heads_dev,), jnp.float32)
    carry_state = jnp.zeros((heads_dev, HEAD, STATE), jnp.float32)
    pieces = []
    for position in range(span_count):
        first_row = position * span_rows
        last_row = first_row + span_rows
        cum_block = cum_level[first_row:last_row]
        start_level = cum_level[first_row - 1] if position > 0 else zero_level
        scores = jnp.dot(
            output_state_map[first_row:last_row],
            input_state_map[first_row:last_row].T,
            preferred_element_type=jnp.float32,
        )
        weights = mixing(cum_block, scores, causal)
        weight_high, weight_low = split_parts(weights)
        x_span = act_heads[first_row:last_row]
        inner_part = jnp.einsum(
            "hts,shp->thp", weight_high, x_span, preferred_element_type=jnp.float32
        )
        inner_part = inner_part + jnp.einsum(
            "hts,shp->thp", weight_low, x_span, preferred_element_type=jnp.float32
        )
        inner_part = inner_part * input_scale[None, :, None]
        carried = jnp.exp(cum_block - start_level[None, :])[:, :, None] * jnp.einsum(
            "tn,hpn->thp", c_float[first_row:last_row], carry_state, precision=highest
        )
        pieces.append(inner_part + carried)
        end_level = cum_block[-1]
        tail_decay = jnp.exp(end_level[None, :] - cum_block)
        carry_state = jnp.exp(end_level - start_level)[:, None, None] * carry_state + jnp.einsum(
            "shp,sn->hpn",
            scaled[first_row:last_row] * tail_decay[:, :, None],
            b_float[first_row:last_row],
            precision=highest,
        )
    device_decay = jnp.exp(cum_level[-1])
    flat_state = carry_state.reshape(heads_dev, HEAD * STATE)

    def relay_state(rounds, carried_in):
        return from_behind(
            (device_decay[:, None] * carried_in + flat_state).astype(jnp.bfloat16), "seq", 1
        ).astype(jnp.float32)

    incoming = lax.fori_loop(0, seq_count - 1, relay_state, jnp.zeros_like(flat_state))
    incoming = incoming.reshape(heads_dev, HEAD, STATE)
    outputs = jnp.concatenate(pieces, axis=0) + jnp.exp(cum_level)[:, :, None] * jnp.einsum(
        "tn,hpn->thp", c_float, incoming, precision=highest
    )
    mixed_out = (activations.astype(jnp.float32) + outputs.reshape(tokens, slice_width)).astype(
        jnp.bfloat16
    )
    blocks_dev = tokens // BLOCK
    route_table = assign.reshape(seq_count, blocks_dev)
    own_row = lax.dynamic_index_in_dim(route_table, seq_index, 0, keepdims=False)
    chosen = (own_row[None, :] == jnp.arange(exp_count)[:, None]).astype(jnp.bfloat16)
    h_pick = jnp.einsum(
        "eb,brf->erf",
        chosen,
        mixed_out.reshape(blocks_dev, BLOCK, slice_width),
        preferred_element_type=jnp.float32,
    ).astype(jnp.bfloat16)
    g_pick = jnp.einsum(
        "eb,brf->erf",
        chosen,
        output_gradient.reshape(blocks_dev, BLOCK, slice_width),
        preferred_element_type=jnp.float32,
    ).astype(jnp.bfloat16)
    h_full, g_full = (
        lax.all_gather(h_pick, ("expert", "mp"), axis=2, tiled=True),
        lax.all_gather(g_pick, ("expert", "mp"), axis=2, tiled=True),
    )
    h_block = narrow(h_full, exp_index, mp_index, half_width)
    g_block = narrow(g_full, exp_index, mp_index, half_width)
    h_all, g_all = (
        lax.all_gather(h_block, "seq", axis=0, tiled=True),
        lax.all_gather(g_block, "seq", axis=0, tiled=True),
    )
    present = jnp.any(route_table == exp_index, axis=1)
    slot_of = jnp.cumsum(present.astype(jnp.int32)) - 1
    select = ((slot_of[None, :] == jnp.arange(slot_total)[:, None]) & present[None, :]).astype(
        jnp.bfloat16
    )
    x_rows = compact(select, h_all, half_width)
    g_rows = compact(select, g_all, half_width)
    up_local = expert_up_weight[0]
    down_local = expert_down_weight[0]
    pre_act = lax.psum(
        rounded(jnp.dot(x_rows, up_local, preferred_element_type=jnp.float32)).astype(jnp.bfloat16),
        "mp",
    ).astype(jnp.float32)
    activation = jax.nn.silu(pre_act).astype(jnp.bfloat16)
    down_grad = jnp.einsum("tf,td->fd", activation, g_rows, preferred_element_type=jnp.float32)
    act_grad = lax.psum(
        rounded(
            jnp.einsum("td,fd->tf", g_rows, down_local, preferred_element_type=jnp.float32)
        ).astype(jnp.bfloat16),
        "mp",
    ).astype(jnp.float32)
    sigmoid_pre = jax.nn.sigmoid(pre_act)
    pre_grad = (act_grad * sigmoid_pre * (1.0 + pre_act * (1.0 - sigmoid_pre))).astype(jnp.bfloat16)
    up_grad = jnp.einsum("td,tf->df", x_rows, pre_grad, preferred_element_type=jnp.float32)
    row_grad = jnp.einsum("tf,df->td", pre_grad, up_local, preferred_element_type=jnp.float32)
    row_grad = row_grad.astype(jnp.bfloat16).reshape(slot_total, BLOCK, half_width)
    spread_rows = jnp.einsum("js,jrf->srf", select, row_grad, preferred_element_type=jnp.float32)
    back_rows = lax.psum_scatter(
        spread_rows.reshape(BLOCK * lax.axis_size("seq"), half_width).astype(jnp.bfloat16),
        "seq",
        scatter_dimension=0,
        tiled=True,
    )
    arrived = lax.all_gather(back_rows[None], ("expert", "mp"), axis=0, tiled=True)
    halves = lax.dynamic_index_in_dim(
        arrived.reshape(exp_count, mp_count, BLOCK, half_width), slice_half, 1, keepdims=False
    )
    returned = lax.dynamic_slice_in_dim(halves, my_slice % exp_count * slice_width, slice_width, 2)
    token_grad = jnp.einsum("eb,erf->brf", chosen, returned, preferred_element_type=jnp.float32)
    total_grad = output_gradient.astype(jnp.float32) + token_grad.reshape(tokens, slice_width)
    grad_view = total_grad.reshape(tokens, heads_dev, HEAD)
    adjoint = jnp.zeros((heads_dev, HEAD, STATE), jnp.float32)
    back_pieces = [None] * span_count
    for position in reversed(range(span_count)):
        first_row = position * span_rows
        last_row = first_row + span_rows
        cum_block = cum_level[first_row:last_row]
        start_level = cum_level[first_row - 1] if position > 0 else zero_level
        scores = jnp.dot(
            output_state_map[first_row:last_row],
            input_state_map[first_row:last_row].T,
            preferred_element_type=jnp.float32,
        )
        weights = mixing(cum_block, scores, causal)
        weight_high, weight_low = split_parts(weights)
        grad_high, grad_low = split_parts(grad_view[first_row:last_row])
        inner_part = jnp.einsum(
            "hts,thp->shp", weight_high, grad_high, preferred_element_type=jnp.float32
        )
        inner_part = inner_part + jnp.einsum(
            "hts,thp->shp", weight_high, grad_low, preferred_element_type=jnp.float32
        )
        inner_part = inner_part + jnp.einsum(
            "hts,thp->shp", weight_low, grad_high, preferred_element_type=jnp.float32
        )
        end_level = cum_block[-1]
        tail_decay = jnp.exp(end_level[None, :] - cum_block)
        carried = tail_decay[:, :, None] * jnp.einsum(
            "sn,hpn->shp", b_float[first_row:last_row], adjoint, precision=highest
        )
        back_pieces[position] = inner_part + carried
        lead_decay = jnp.exp(cum_block - start_level[None, :])
        adjoint = jnp.exp(end_level - start_level)[:, None, None] * adjoint + jnp.einsum(
            "rhp,rn->hpn",
            grad_view[first_row:last_row] * lead_decay[:, :, None],
            c_float[first_row:last_row],
            precision=highest,
        )
    flat_adjoint = adjoint.reshape(heads_dev, HEAD * STATE)

    def relay_adjoint(rounds, carried_in):
        return from_behind(
            (device_decay[:, None] * carried_in + flat_adjoint).astype(jnp.bfloat16), "seq", -1
        ).astype(jnp.float32)

    later_adjoint = lax.fori_loop(0, seq_count - 1, relay_adjoint, jnp.zeros_like(flat_adjoint))
    later_adjoint = later_adjoint.reshape(heads_dev, HEAD, STATE)
    scan_grad = jnp.concatenate(back_pieces, axis=0) + jnp.exp(cum_level[-1][None, :] - cum_level)[
        :, :, None
    ] * jnp.einsum("sn,hpn->shp", b_float, later_adjoint, precision=highest)
    grad_x = total_grad + (input_scale[None, :, None] * scan_grad).reshape(tokens, slice_width)
    return (grad_x, up_grad[None], down_grad[None])


def solution(mesh):
    in_specs = (
        P("seq", ("expert", "mp")),
        P("seq", ("expert", "mp")),
        P("seq", None),
        P("seq", None),
        P(("expert", "mp")),
        P("seq"),
        P(),
        P("expert", "mp", "seq"),
        P("expert", "seq", "mp"),
    )
    out_specs = (P("seq", ("expert", "mp")), P("expert", "mp", "seq"), P("expert", "seq", "mp"))
    return jax.shard_map(
        per_device, mesh=mesh, in_specs=in_specs, out_specs=out_specs, check_vma=False
    )
```

profile of v0, /device:TPU:6, one launch (start us, length us, event | category | flops | bytes accessed | tf_op | source)
XLA Modules:
  0.0 771.0 jit_solution(8821121066339142544)
XLA Ops:
  47.4 123.4 %while.22 = (s32[]{:T(128)}, f32[8,1024]{1,0:T(8,128)S(1)}, f32[8]{0:T(128)}, f32[8,1024]{1,0:T(8,128)S(1)}, s32[]{:T(128)}, /*index=5*/s32[]{:T(128)}) while((s32[]{:T(128)}, f32[8,1024]{1,0:T(8,128)S(1)}, f32[8]{0:T(128)}, f32[8,1024]{1,0:T(8,128)S(1)}, s32[]{:T(128)}, /*index=5*/s32[]{:T(128)}) %tuple.59), condition=%wide.region_6.7_spmd.clone, body=%wide.region_5.6_spmd.clone.sunk | while | flops 40963 | bytes 196759 | solution.py:127
  62.1 6.3 collective-permute-start
  70.5 6.3 collective-permute-start
  78.9 6.3 collective-permute-start
  87.3 6.3 collective-permute-start
  95.7 6.3 collective-permute-start
  104.2 6.3 collective-permute-start
  112.6 6.3 collective-permute-start
  121.0 6.3 collective-permute-start
  129.4 6.3 collective-permute-start
  137.8 6.3 collective-permute-start
  146.2 6.3 collective-permute-start
  154.7 6.3 collective-permute-start
  163.1 6.3 collective-permute-start
  189.0 35.8 %all-gather.11.cloned.1.call-done = bf16[4,128,4096]{2,0,1:T(4,128)(2,1)} async-done(((bf16[4,128,512]{2,0,1:T(4,128)(2,1)}), bf16[4,128,4096]{2,0,1:T(4,128)(2,1)}) %all-gather.11.cloned.1.call-update) | async-done | bytes 4194320 | tf_op jit(solution)/shard_map/all_gather | solution.py:152
  229.3 34.2 %all-gather.9.cloned.1.call-done = bf16[4,128,4096]{2,0,1:T(4,128)(2,1)} async-done(((bf16[4,128,512]{2,0,1:T(4,128)(2,1)}), bf16[4,128,4096]{2,0,1:T(4,128)(2,1)}) %all-gather.9.cloned.1.call-update) | async-done | bytes 4194320 | tf_op jit(solution)/shard_map/all_gather | solution.py:153
  268.7 69.0 %all-gather.15.cloned.1.call-done = bf16[1,2048,2048]{2,1,0:T(8,128)(2,1)} async-done(((bf16[1,128,2048]{2,1,0:T(8,128)(2,1)}), bf16[1,2048,2048]{2,1,0:T(8,128)(2,1)}) %all-gather.15.cloned.1.call-update) | async-done | bytes 8388624 | tf_op jit(solution)/shard_map/all_gather | solution.py:158
  337.7 12.5 %fusion.56 = bf16[8,128,2048]{2,0,1:T(8,128)(2,1)S(1)} fusion(bf16[16,128,2048]{2,1,0:T(8,128)(2,1)} %bitcast.153, s32[16]{0:T(128)S(1)} %add_reduce_fusion, pred[16]{0:T(512)(128)(4,1)S(1)} %compare_reduce_fusion), kind=kOutput, calls=%fused_computation.58 | convolution fusion | flops 69206272 | bytes 12582992 | tf_op jit(solution)/shard_map/js,srf->jrf/dot_general | solution.py:44
  359.5 51.2 %all-gather.13.cloned.1.call-done = bf16[1,2048,2048]{2,1,0:T(8,128)(2,1)} async-done(((bf16[1,128,2048]{2,1,0:T(8,128)(2,1)}), bf16[1,2048,2048]{2,1,0:T(8,128)(2,1)}) %all-gather.13.cloned.1.call-update) | async-done | bytes 8388624 | tf_op jit(solution)/shard_map/all_gather | solution.py:159
  410.7 12.5 %fusion.53 = bf16[8,128,2048]{2,0,1:T(8,128)(2,1)S(1)} fusion(bf16[16,128,2048]{2,1,0:T(8,128)(2,1)} %bitcast.154, s32[16]{0:T(128)S(1)} %add_reduce_fusion, pred[16]{0:T(512)(128)(4,1)S(1)} %compare_reduce_fusion), kind=kOutput, calls=%fused_computation.57 | convolution fusion | flops 69206272 | bytes 12582992 | tf_op jit(solution)/shard_map/js,srf->jrf/dot_general | solution.py:44
  432.3 28.9 %all-reduce.3.cloned.1.call-done = (bf16[1024,768]{1,0:T(8,128)(2,1)}, bf16[1024,768]{1,0:T(8,128)(2,1)}) async-done(((bf16[1024,768]{1,0:T(8,128)(2,1)}, bf16[1024,768]{1,0:T(8,128)(2,1)}), (bf16[1024,768]{1,0:T(8,128)(2,1)}, bf16[1024,768]{1,0:T(8,128)(2,1)})) %all-reduce.3.cloned.1.call-update) | async-done | bytes 3145744 | tf_op jit(solution)/shard_map/psum | solution.py:170
  461.1 6.9 convolution_convert_fusion.1
  468.0 6.9 convolution_convert_fusion
  474.9 11.3 %copy.146 = bf16[16,128,2048]{2,1,0:T(8,128)(2,1)} copy(bf16[16,128,2048]{2,0,1:T(8,128)(2,1)} %convolution_convert_fusion) | data formatting | bytes 16777216 | tf_op jit(solution)/shard_map/convert_element_type | solution.py:189
  486.3 87.0 %reduce-scatter.2.cloned.1.call-done = bf16[128,2048]{1,0:T(8,128)(2,1)} async-done(((bf16[2048,2048]{1,0:T(8,128)(2,1)}), bf16[128,2048]{1,0:T(8,128)(2,1)}) %reduce-scatter.2.cloned.1.call-update) | async-done | bytes 524304 | tf_op jit(solution)/shard_map/reduce_scatter | solution.py:188
  573.4 7.8 %convolution_bitcast_fusion = f32[1,768,2048]{2,1,0:T(8,128)} fusion(bf16[1024,2048]{1,0:T(8,128)(2,1)} %bitcast.163, bf16[1024,768]{1,0:T(8,128)(2,1)S(1)} %copy-done.44), kind=kOutput, calls=%fused_computation.59 | convolution fusion | flops 3225944064 | bytes 12058624 | tf_op jit(solution)/shard_map/tf,td->fd/dot_general | solution.py:175
  581.3 6.1 convolution_bitcast_fusion.1
  587.4 19.6 %all-gather.17.cloned.1.call-done = bf16[1024,2048]{1,0:T(8,128)(2,1)} async-done(((bf16[128,2048]{1,0:T(8,128)(2,1)}), bf16[1024,2048]{1,0:T(8,128)(2,1)}) %all-gather.17.cloned.1.call-update) | async-done | bytes 4194320 | tf_op jit(solution)/shard_map/all_gather | solution.py:194
  636.8 117.3 %while.23 = (s32[]{:T(128)}, f32[8,1024]{1,0:T(8,128)S(1)}, f32[8]{0:T(128)S(1)}, f32[8,1024]{1,0:T(8,128)S(1)}, s32[]{:T(128)}, /*index=5*/s32[]{:T(128)}) while((s32[]{:T(128)}, f32[8,1024]{1,0:T(8,128)S(1)}, f32[8]{0:T(128)S(1)}, f32[8,1024]{1,0:T(8,128)S(1)}, s32[]{:T(128)}, /*index=5*/s32[]{:T(128)}) %tuple.80), condition=%wide.region_10.11_spmd.clone, body=%wide.region_9.10_spmd.clone.sunk | while | flops 40963 | bytes 196759 | solution.py:246
  646.6 5.8 collective-permute-done.1
  654.4 5.8 collective-permute-done.1
  724.7 5.9 collective-permute-done.1
  (288 shorter events, 266.0 us)
Async XLA Ops:
  7.2 217.5 %all-gather.11.cloned.1.call-start = ((), (), s32[]{:S(2)}) async-start(), calls=%async_computation.2 | async-start | bytes 4718592 | tf_op jit(solution)/shard_map/all_gather | solution.py:152
  62.1 7.7 %collective-permute-start = (bf16[8,1024]{1,0:T(8,128)(2,1)S(1)}, bf16[8,1024]{1,0:T(8,128)(2,1)S(1)}, u32[]{:S(2)}, u32[]{:S(2)}) collective-permute-start(bf16[8,1024]{1,0:T(8,128)(2,1)S(1)} %fusion.212), channel_id=1, source_target_pairs={{0,8},{8,16},{16,24},{24,32},{32,40},{40,48},{48,56},{56,64},{64,7... | collective-permute-start | bytes 49160 | tf_op jit(solution)/shard_map/while/body/eval_jaxpr/ppermute | solution.py:18
  70.5 7.7 %collective-permute-start = (bf16[8,1024]{1,0:T(8,128)(2,1)S(1)}, bf16[8,1024]{1,0:T(8,128)(2,1)S(1)}, u32[]{:S(2)}, u32[]{:S(2)}) collective-permute-start(bf16[8,1024]{1,0:T(8,128)(2,1)S(1)} %fusion.212), channel_id=1, source_target_pairs={{0,8},{8,16},{16,24},{24,32},{32,40},{40,48},{48,56},{56,64},{64,7... | collective-permute-start | bytes 49160 | tf_op jit(solution)/shard_map/while/body/eval_jaxpr/ppermute | solution.py:18
  78.9 7.7 %collective-permute-start = (bf16[8,1024]{1,0:T(8,128)(2,1)S(1)}, bf16[8,1024]{1,0:T(8,128)(2,1)S(1)}, u32[]{:S(2)}, u32[]{:S(2)}) collective-permute-start(bf16[8,1024]{1,0:T(8,128)(2,1)S(1)} %fusion.212), channel_id=1, source_target_pairs={{0,8},{8,16},{16,24},{24,32},{32,40},{40,48},{48,56},{56,64},{64,7... | collective-permute-start | bytes 49160 | tf_op jit(solution)/shard_map/while/body/eval_jaxpr/ppermute | solution.py:18
  87.3 7.7 %collective-permute-start = (bf16[8,1024]{1,0:T(8,128)(2,1)S(1)}, bf16[8,1024]{1,0:T(8,128)(2,1)S(1)}, u32[]{:S(2)}, u32[]{:S(2)}) collective-permute-start(bf16[8,1024]{1,0:T(8,128)(2,1)S(1)} %fusion.212), channel_id=1, source_target_pairs={{0,8},{8,16},{16,24},{24,32},{32,40},{40,48},{48,56},{56,64},{64,7... | collective-permute-start | bytes 49160 | tf_op jit(solution)/shard_map/while/body/eval_jaxpr/ppermute | solution.py:18
  95.7 7.7 %collective-permute-start = (bf16[8,1024]{1,0:T(8,128)(2,1)S(1)}, bf16[8,1024]{1,0:T(8,128)(2,1)S(1)}, u32[]{:S(2)}, u32[]{:S(2)}) collective-permute-start(bf16[8,1024]{1,0:T(8,128)(2,1)S(1)} %fusion.212), channel_id=1, source_target_pairs={{0,8},{8,16},{16,24},{24,32},{32,40},{40,48},{48,56},{56,64},{64,7... | collective-permute-start | bytes 49160 | tf_op jit(solution)/shard_map/while/body/eval_jaxpr/ppermute | solution.py:18
  104.2 7.7 %collective-permute-start = (bf16[8,1024]{1,0:T(8,128)(2,1)S(1)}, bf16[8,1024]{1,0:T(8,128)(2,1)S(1)}, u32[]{:S(2)}, u32[]{:S(2)}) collective-permute-start(bf16[8,1024]{1,0:T(8,128)(2,1)S(1)} %fusion.212), channel_id=1, source_target_pairs={{0,8},{8,16},{16,24},{24,32},{32,40},{40,48},{48,56},{56,64},{64,7... | collective-permute-start | bytes 49160 | tf_op jit(solution)/shard_map/while/body/eval_jaxpr/ppermute | solution.py:18
  112.6 7.7 %collective-permute-start = (bf16[8,1024]{1,0:T(8,128)(2,1)S(1)}, bf16[8,1024]{1,0:T(8,128)(2,1)S(1)}, u32[]{:S(2)}, u32[]{:S(2)}) collective-permute-start(bf16[8,1024]{1,0:T(8,128)(2,1)S(1)} %fusion.212), channel_id=1, source_target_pairs={{0,8},{8,16},{16,24},{24,32},{32,40},{40,48},{48,56},{56,64},{64,7... | collective-permute-start | bytes 49160 | tf_op jit(solution)/shard_map/while/body/eval_jaxpr/ppermute | solution.py:18
  121.0 7.7 %collective-permute-start = (bf16[8,1024]{1,0:T(8,128)(2,1)S(1)}, bf16[8,1024]{1,0:T(8,128)(2,1)S(1)}, u32[]{:S(2)}, u32[]{:S(2)}) collective-permute-start(bf16[8,1024]{1,0:T(8,128)(2,1)S(1)} %fusion.212), channel_id=1, source_target_pairs={{0,8},{8,16},{16,24},{24,32},{32,40},{40,48},{48,56},{56,64},{64,7... | collective-permute-start | bytes 49160 | tf_op jit(solution)/shard_map/while/body/eval_jaxpr/ppermute | solution.py:18
  129.4 7.7 %collective-permute-start = (bf16[8,1024]{1,0:T(8,128)(2,1)S(1)}, bf16[8,1024]{1,0:T(8,128)(2,1)S(1)}, u32[]{:S(2)}, u32[]{:S(2)}) collective-permute-start(bf16[8,1024]{1,0:T(8,128)(2,1)S(1)} %fusion.212), channel_id=1, source_target_pairs={{0,8},{8,16},{16,24},{24,32},{32,40},{40,48},{48,56},{56,64},{64,7... | collective-permute-start | bytes 49160 | tf_op jit(solution)/shard_map/while/body/eval_jaxpr/ppermute | solution.py:18
  137.8 7.7 %collective-permute-start = (bf16[8,1024]{1,0:T(8,128)(2,1)S(1)}, bf16[8,1024]{1,0:T(8,128)(2,1)S(1)}, u32[]{:S(2)}, u32[]{:S(2)}) collective-permute-start(bf16[8,1024]{1,0:T(8,128)(2,1)S(1)} %fusion.212), channel_id=1, source_target_pairs={{0,8},{8,16},{16,24},{24,32},{32,40},{40,48},{48,56},{56,64},{64,7... | collective-permute-start | bytes 49160 | tf_op jit(solution)/shard_map/while/body/eval_jaxpr/ppermute | solution.py:18
  146.2 7.7 %collective-permute-start = (bf16[8,1024]{1,0:T(8,128)(2,1)S(1)}, bf16[8,1024]{1,0:T(8,128)(2,1)S(1)}, u32[]{:S(2)}, u32[]{:S(2)}) collective-permute-start(bf16[8,1024]{1,0:T(8,128)(2,1)S(1)} %fusion.212), channel_id=1, source_target_pairs={{0,8},{8,16},{16,24},{24,32},{32,40},{40,48},{48,56},{56,64},{64,7... | collective-permute-start | bytes 49160 | tf_op jit(solution)/shard_map/while/body/eval_jaxpr/ppermute | solution.py:18
  154.7 7.7 %collective-permute-start = (bf16[8,1024]{1,0:T(8,128)(2,1)S(1)}, bf16[8,1024]{1,0:T(8,128)(2,1)S(1)}, u32[]{:S(2)}, u32[]{:S(2)}) collective-permute-start(bf16[8,1024]{1,0:T(8,128)(2,1)S(1)} %fusion.212), channel_id=1, source_target_pairs={{0,8},{8,16},{16,24},{24,32},{32,40},{40,48},{48,56},{56,64},{64,7... | collective-permute-start | bytes 49160 | tf_op jit(solution)/shard_map/while/body/eval_jaxpr/ppermute | solution.py:18
  163.1 7.7 %collective-permute-start = (bf16[8,1024]{1,0:T(8,128)(2,1)S(1)}, bf16[8,1024]{1,0:T(8,128)(2,1)S(1)}, u32[]{:S(2)}, u32[]{:S(2)}) collective-permute-start(bf16[8,1024]{1,0:T(8,128)(2,1)S(1)} %fusion.212), channel_id=1, source_target_pairs={{0,8},{8,16},{16,24},{24,32},{32,40},{40,48},{48,56},{56,64},{64,7... | collective-permute-start | bytes 49160 | tf_op jit(solution)/shard_map/while/body/eval_jaxpr/ppermute | solution.py:18
  186.1 77.5 %all-gather.9.cloned.1.call-start = ((), (), s32[]{:S(2)}) async-start(), calls=%async_computation.1 | async-start | bytes 4718592 | tf_op jit(solution)/shard_map/all_gather | solution.py:153
  188.9 148.8 %all-gather.15.cloned.1.call-start = ((), (), s32[]{:S(2)}) async-start(), calls=%async_computation.5 | async-start | bytes 8912896 | tf_op jit(solution)/shard_map/all_gather | solution.py:158
  229.3 181.4 %all-gather.13.cloned.1.call-start = ((), (), s32[]{:S(2)}) async-start(), calls=%async_computation.4 | async-start | bytes 8912896 | tf_op jit(solution)/shard_map/all_gather | solution.py:159
  268.1 193.0 %all-reduce.3.cloned.1.call-start = ((), (), s32[]{:S(2)}) async-start(), calls=%async_computation.7 | async-start | bytes 6291456 | tf_op jit(solution)/shard_map/psum | solution.py:170
  432.2 141.1 %reduce-scatter.2.cloned.1.call-start = ((), (), s32[]{:S(2)}) async-start(), calls=%async_computation.3 | async-start | bytes 8912896 | tf_op jit(solution)/shard_map/reduce_scatter | solution.py:188
  486.3 120.8 %all-gather.17.cloned.1.call-start = ((), (), s32[]{:S(2)}) async-start(), calls=%async_computation.6 | async-start | bytes 4718592 | tf_op jit(solution)/shard_map/all_gather | solution.py:194
  636.9 7.7 %collective-permute-start.1 = (bf16[8,1024]{1,0:T(8,128)(2,1)S(1)}, bf16[8,1024]{1,0:T(8,128)(2,1)S(1)}, u32[]{:S(2)}, u32[]{:S(2)}) collective-permute-start(bf16[8,1024]{1,0:T(8,128)(2,1)S(1)} %fusion.213), channel_id=1, source_target_pairs={{8,0},{16,8},{24,16},{32,24},{40,32},{48,40},{56,48},{64,56},{72,6... | collective-permute-start | bytes 49160 | tf_op jit(solution)/shard_map/while/body/eval_jaxpr/ppermute | solution.py:18
  644.7 7.7 %collective-permute-start.1 = (bf16[8,1024]{1,0:T(8,128)(2,1)S(1)}, bf16[8,1024]{1,0:T(8,128)(2,1)S(1)}, u32[]{:S(2)}, u32[]{:S(2)}) collective-permute-start(bf16[8,1024]{1,0:T(8,128)(2,1)S(1)} %fusion.213), channel_id=1, source_target_pairs={{8,0},{16,8},{24,16},{32,24},{40,32},{48,40},{56,48},{64,56},{72,6... | collective-permute-start | bytes 49160 | tf_op jit(solution)/shard_map/while/body/eval_jaxpr/ppermute | solution.py:18
  652.5 7.7 %collective-permute-start.1 = (bf16[8,1024]{1,0:T(8,128)(2,1)S(1)}, bf16[8,1024]{1,0:T(8,128)(2,1)S(1)}, u32[]{:S(2)}, u32[]{:S(2)}) collective-permute-start(bf16[8,1024]{1,0:T(8,128)(2,1)S(1)} %fusion.213), channel_id=1, source_target_pairs={{8,0},{16,8},{24,16},{32,24},{40,32},{48,40},{56,48},{64,56},{72,6... | collective-permute-start | bytes 49160 | tf_op jit(solution)/shard_map/while/body/eval_jaxpr/ppermute | solution.py:18
  660.3 7.7 %collective-permute-start.1 = (bf16[8,1024]{1,0:T(8,128)(2,1)S(1)}, bf16[8,1024]{1,0:T(8,128)(2,1)S(1)}, u32[]{:S(2)}, u32[]{:S(2)}) collective-permute-start(bf16[8,1024]{1,0:T(8,128)(2,1)S(1)} %fusion.213), channel_id=1, source_target_pairs={{8,0},{16,8},{24,16},{32,24},{40,32},{48,40},{56,48},{64,56},{72,6... | collective-permute-start | bytes 49160 | tf_op jit(solution)/shard_map/while/body/eval_jaxpr/ppermute | solution.py:18
  668.1 7.7 %collective-permute-start.1 = (bf16[8,1024]{1,0:T(8,128)(2,1)S(1)}, bf16[8,1024]{1,0:T(8,128)(2,1)S(1)}, u32[]{:S(2)}, u32[]{:S(2)}) collective-permute-start(bf16[8,1024]{1,0:T(8,128)(2,1)S(1)} %fusion.213), channel_id=1, source_target_pairs={{8,0},{16,8},{24,16},{32,24},{40,32},{48,40},{56,48},{64,56},{72,6... | collective-permute-start | bytes 49160 | tf_op jit(solution)/shard_map/while/body/eval_jaxpr/ppermute | solution.py:18
  675.9 7.7 %collective-permute-start.1 = (bf16[8,1024]{1,0:T(8,128)(2,1)S(1)}, bf16[8,1024]{1,0:T(8,128)(2,1)S(1)}, u32[]{:S(2)}, u32[]{:S(2)}) collective-permute-start(bf16[8,1024]{1,0:T(8,128)(2,1)S(1)} %fusion.213), channel_id=1, source_target_pairs={{8,0},{16,8},{24,16},{32,24},{40,32},{48,40},{56,48},{64,56},{72,6... | collective-permute-start | bytes 49160 | tf_op jit(solution)/shard_map/while/body/eval_jaxpr/ppermute | solution.py:18
  683.7 7.7 %collective-permute-start.1 = (bf16[8,1024]{1,0:T(8,128)(2,1)S(1)}, bf16[8,1024]{1,0:T(8,128)(2,1)S(1)}, u32[]{:S(2)}, u32[]{:S(2)}) collective-permute-start(bf16[8,1024]{1,0:T(8,128)(2,1)S(1)} %fusion.213), channel_id=1, source_target_pairs={{8,0},{16,8},{24,16},{32,24},{40,32},{48,40},{56,48},{64,56},{72,6... | collective-permute-start | bytes 49160 | tf_op jit(solution)/shard_map/while/body/eval_jaxpr/ppermute | solution.py:18
  691.6 7.7 %collective-permute-start.1 = (bf16[8,1024]{1,0:T(8,128)(2,1)S(1)}, bf16[8,1024]{1,0:T(8,128)(2,1)S(1)}, u32[]{:S(2)}, u32[]{:S(2)}) collective-permute-start(bf16[8,1024]{1,0:T(8,128)(2,1)S(1)} %fusion.213), channel_id=1, source_target_pairs={{8,0},{16,8},{24,16},{32,24},{40,32},{48,40},{56,48},{64,56},{72,6... | collective-permute-start | bytes 49160 | tf_op jit(solution)/shard_map/while/body/eval_jaxpr/ppermute | solution.py:18
  699.4 7.7 %collective-permute-start.1 = (bf16[8,1024]{1,0:T(8,128)(2,1)S(1)}, bf16[8,1024]{1,0:T(8,128)(2,1)S(1)}, u32[]{:S(2)}, u32[]{:S(2)}) collective-permute-start(bf16[8,1024]{1,0:T(8,128)(2,1)S(1)} %fusion.213), channel_id=1, source_target_pairs={{8,0},{16,8},{24,16},{32,24},{40,32},{48,40},{56,48},{64,56},{72,6... | collective-permute-start | bytes 49160 | tf_op jit(solution)/shard_map/while/body/eval_jaxpr/ppermute | solution.py:18
  707.2 7.7 %collective-permute-start.1 = (bf16[8,1024]{1,0:T(8,128)(2,1)S(1)}, bf16[8,1024]{1,0:T(8,128)(2,1)S(1)}, u32[]{:S(2)}, u32[]{:S(2)}) collective-permute-start(bf16[8,1024]{1,0:T(8,128)(2,1)S(1)} %fusion.213), channel_id=1, source_target_pairs={{8,0},{16,8},{24,16},{32,24},{40,32},{48,40},{56,48},{64,56},{72,6... | collective-permute-start | bytes 49160 | tf_op jit(solution)/shard_map/while/body/eval_jaxpr/ppermute | solution.py:18
  715.0 7.7 %collective-permute-start.1 = (bf16[8,1024]{1,0:T(8,128)(2,1)S(1)}, bf16[8,1024]{1,0:T(8,128)(2,1)S(1)}, u32[]{:S(2)}, u32[]{:S(2)}) collective-permute-start(bf16[8,1024]{1,0:T(8,128)(2,1)S(1)} %fusion.213), channel_id=1, source_target_pairs={{8,0},{16,8},{24,16},{32,24},{40,32},{48,40},{56,48},{64,56},{72,6... | collective-permute-start | bytes 49160 | tf_op jit(solution)/shard_map/while/body/eval_jaxpr/ppermute | solution.py:18
  722.8 7.8 %collective-permute-start.1 = (bf16[8,1024]{1,0:T(8,128)(2,1)S(1)}, bf16[8,1024]{1,0:T(8,128)(2,1)S(1)}, u32[]{:S(2)}, u32[]{:S(2)}) collective-permute-start(bf16[8,1024]{1,0:T(8,128)(2,1)S(1)} %fusion.213), channel_id=1, source_target_pairs={{8,0},{16,8},{24,16},{32,24},{40,32},{48,40},{56,48},{64,56},{72,6... | collective-permute-start | bytes 49160 | tf_op jit(solution)/shard_map/while/body/eval_jaxpr/ppermute | solution.py:18
  (52 other events, 946.2 us)
Sparse Core Ops, SparseCore 0:
  186.2 38.4 all-gather.10
  227.0 36.5 all-gather.8
  266.2 71.4 all-gather.14
  340.3 70.3 all-gather.12
  432.3 28.7 all-reduce.2
  486.4 86.8 reduce-scatter.1
  575.0 31.9 all-gather.16
where the time goes:
time: 781 us; the launch traced here: 771 us
  waiting for transfers between devices  434 us (56%)
  starting transfers between devices  121 us (15%)
  matrix products  119 us (15%)
  local copies, waits for them, and re-layouts  54.2 us (7%)
  other arithmetic  26.6 us (3%)
  between operations  15.5 us (2%)
    ppermute x30, starting transfers between devices, from_behind(): lax.ppermute(value, axis, [(source, source + steps) for source in range(f...  120 us
    ppermute x30, waiting for transfers between devices, from_behind(): lax.ppermute(value, axis, [(source, source + steps) for source in range(f...  109 us
    reduce_scatter x1, waiting for transfers between devices, per_device(): lax.psum_scatter(spread_rows.reshape(BLOCK * lax.axis_size('seq'), half_w...  87 us
    all_gather x1, waiting for transfers between devices, per_device(): lax.all_gather(h_block, 'seq', axis=0, tiled=True)  69 us
    all_gather x1, waiting for transfers between devices, per_device(): lax.all_gather(g_block, 'seq', axis=0, tiled=True)  51.2 us
    all_gather x1, waiting for transfers between devices, per_device(): lax.all_gather(h_pick, ('expert', 'mp'), axis=2, tiled=True)  35.8 us
    all_gather x1, waiting for transfers between devices, per_device(): lax.all_gather(g_pick, ('expert', 'mp'), axis=2, tiled=True)  34.2 us
    psum x1, waiting for transfers between devices, per_device(): lax.psum(rounded(jnp.dot(x_rows, up_local, preferred_element_type=jnp.flo...  28.9 us
  transfers between devices with their start and end apart: 37, of which 37 were waited for; matrix products, arithmetic and copies ran while one was open for 6% of the time, Pallas kernels for 0%

commit v1 on v0

--- a/solution.py
+++ b/solution.py
@@ -12,10 +12,62 @@
 highest = lax.Precision.HIGHEST
 
 
-def from_behind(value, axis, steps):
-    count = lax.axis_size(axis)
-    first, last = (max(0, -steps), min(count, count - steps))
-    return lax.ppermute(value, axis, [(source, source + steps) for source in range(first, last)])
+def carried_sum(values_all, level_all, own, earlier):
+    count = level_all.shape[0]
+    ids = jnp.arange(count)
+    j, k = ids[:, None], ids[None, :]
+    if earlier:
+        between = (j < k) & (k < own)
+        valid = ids < own
+    else:
+        between = (own < k) & (k < j)
+        valid = ids > own
+    exponent = jnp.sum(jnp.where(between[:, :, None], level_all[None], 0.0), axis=1)
+    weight = jnp.where(valid[:, None], jnp.exp(exponent), 0.0)
+    return jnp.sum(weight[:, :, None] * values_all.astype(jnp.float32), axis=0)
+
+
+def mp_sum(part):
+    part = part.astype(jnp.bfloat16)
+    count = lax.axis_size("mp")
+    total = part.astype(jnp.float32)
+    for shift in range(1, count):
+        pairs = [(src, (src + shift) % count) for src in range(count)]
+        total = total + lax.ppermute(part, "mp", pairs).astype(jnp.float32)
+    return total
+
+
+def dispatch_pairs(exp_count, mp_count, shift):
+    return [
+        (src, ((src % exp_count + shift) % exp_count) * mp_count + src // exp_count)
+        for src in range(exp_count * mp_count)
+    ]
+
+
+def dispatch(picks, exp_index, exp_count, mp_count, my_slice):
+    position = my_slice % exp_count
+    received = []
+    for shift in range(exp_count):
+        send = lax.dynamic_index_in_dim(picks, (position + shift) % exp_count, 0, keepdims=False)
+        pairs = dispatch_pairs(exp_count, mp_count, shift)
+        received.append(lax.ppermute(send, ("expert", "mp"), pairs))
+    received = jnp.stack(received)
+    order = (exp_index - jnp.arange(exp_count)) % exp_count
+    placed = jnp.take(received, order, axis=0)
+    rows, width = placed.shape[1], placed.shape[2]
+    return placed.transpose(1, 0, 2).reshape(rows, exp_count * width)
+
+
+def give_back(rows_half, exp_index, exp_count, mp_count):
+    width = rows_half.shape[1] // exp_count
+    pieces = rows_half.reshape(rows_half.shape[0], exp_count, width)
+    received = []
+    for shift in range(exp_count):
+        column = (exp_index - shift) % exp_count
+        send = lax.dynamic_index_in_dim(pieces, column, 1, keepdims=False)
+        pairs = [(dst, src) for src, dst in dispatch_pairs(exp_count, mp_count, shift)]
+        received.append(lax.ppermute(send, ("expert", "mp"), pairs))
+    return jnp.stack(received)
 
 
 def rounded(rounded_in):
@@ -32,11 +84,6 @@
     spread = cum_block.T[:, :, None] - cum_block.T[:, None, :]
     spread = jnp.where(causal[None], spread, -jnp.inf)
     return jnp.exp(spread) * scores[None]
-
-
-def narrow(gathered, exp_index, mp_index, half_width):
-    row_set = lax.dynamic_index_in_dim(gathered, exp_index, 0, keepdims=False)
-    return lax.dynamic_slice_in_dim(row_set, mp_index * half_width, half_width, 1)
 
 
 def compact(select, gathered, half_width):
@@ -65,7 +112,6 @@
     exp_index = lax.axis_index("expert")
     mp_index = lax.axis_index("mp")
     my_slice = exp_index * mp_count + mp_index
-    slice_half = my_slice // exp_count
     half_width = slice_width * exp_count
     slot_total = seq_count // 2
     input_scale = jnp.sqrt(1.0 - jnp.exp(-2.0 * head_decay_speed))
@@ -116,15 +162,10 @@
             b_float[first_row:last_row],
             precision=highest,
         )
-    device_decay = jnp.exp(cum_level[-1])
     flat_state = carry_state.reshape(heads_dev, HEAD * STATE)
-
-    def relay_state(rounds, carried_in):
-        return from_behind(
-            (device_decay[:, None] * carried_in + flat_state).astype(jnp.bfloat16), "seq", 1
-        ).astype(jnp.float32)
-
-    incoming = lax.fori_loop(0, seq_count - 1, relay_state, jnp.zeros_like(flat_state))
+    level_all = lax.all_gather(cum_level[-1], "seq")
+    state_all = lax.all_gather(flat_state.astype(jnp.bfloat16), "seq")
+    incoming = carried_sum(state_all, level_all, seq_index, True)
     incoming = incoming.reshape(heads_dev, HEAD, STATE)
     outputs = jnp.concatenate(pieces, axis=0) + jnp.exp(cum_level)[:, :, None] * jnp.einsum(
         "tn,hpn->thp", c_float, incoming, precision=highest
@@ -148,12 +189,8 @@
         output_gradient.reshape(blocks_dev, BLOCK, slice_width),
         preferred_element_type=jnp.float32,
     ).astype(jnp.bfloat16)
-    h_full, g_full = (
-        lax.all_gather(h_pick, ("expert", "mp"), axis=2, tiled=True),
-        lax.all_gather(g_pick, ("expert", "mp"), axis=2, tiled=True),
-    )
-    h_block = narrow(h_full, exp_index, mp_index, half_width)
-    g_block = narrow(g_full, exp_index, mp_index, half_width)
+    h_block = dispatch(h_pick, exp_index, exp_count, mp_count, my_slice)
+    g_block = dispatch(g_pick, exp_index, exp_count, mp_count, my_slice)
     h_all, g_all = (
         lax.all_gather(h_block, "seq", axis=0, tiled=True),
         lax.all_gather(g_block, "seq", axis=0, tiled=True),
@@ -167,18 +204,12 @@
     g_rows = compact(select, g_all, half_width)
     up_local = expert_up_weight[0]
     down_local = expert_down_weight[0]
-    pre_act = lax.psum(
-        rounded(jnp.dot(x_rows, up_local, preferred_element_type=jnp.float32)).astype(jnp.bfloat16),
-        "mp",
-    ).astype(jnp.float32)
+    pre_act = mp_sum(jnp.dot(x_rows, up_local, preferred_element_type=jnp.float32))
     activation = jax.nn.silu(pre_act).astype(jnp.bfloat16)
     down_grad = jnp.einsum("tf,td->fd", activation, g_rows, preferred_element_type=jnp.float32)
-    act_grad = lax.psum(
-        rounded(
-            jnp.einsum("td,fd->tf", g_rows, down_local, preferred_element_type=jnp.float32)
-        ).astype(jnp.bfloat16),
-        "mp",
-    ).astype(jnp.float32)
+    act_grad = mp_sum(
+        jnp.einsum("td,fd->tf", g_rows, down_local, preferred_element_type=jnp.float32)
+    )
     sigmoid_pre = jax.nn.sigmoid(pre_act)
     pre_grad = (act_grad * sigmoid_pre * (1.0 + pre_act * (1.0 - sigmoid_pre))).astype(jnp.bfloat16)
     up_grad = jnp.einsum("td,tf->df", x_rows, pre_grad, preferred_element_type=jnp.float32)
@@ -191,12 +222,12 @@
         scatter_dimension=0,
         tiled=True,
     )
-    arrived = lax.all_gather(back_rows[None], ("expert", "mp"), axis=0, tiled=True)
-    halves = lax.dynamic_index_in_dim(
-        arrived.reshape(exp_count, mp_count, BLOCK, half_width), slice_half, 1, keepdims=False
-    )
-    returned = lax.dynamic_slice_in_dim(halves, my_slice % exp_count * slice_width, slice_width, 2)
-    token_grad = jnp.einsum("eb,erf->brf", chosen, returned, preferred_element_type=jnp.float32)
+    returned = give_back(back_rows, exp_index, exp_count, mp_count)
+    position = my_slice % exp_count
+    chosen_by_shift = jnp.take(chosen, (position + jnp.arange(exp_count)) % exp_count, axis=0)
+    token_grad = jnp.einsum(
+        "kb,krf->brf", chosen_by_shift, returned, preferred_element_type=jnp.float32
+    )
     total_grad = output_gradient.astype(jnp.float32) + token_grad.reshape(tokens, slice_width)
     grad_view = total_grad.reshape(tokens, heads_dev, HEAD)
     adjoint = jnp.zeros((heads_dev, HEAD, STATE), jnp.float32)
@@ -237,13 +268,8 @@
             precision=highest,
         )
     flat_adjoint = adjoint.reshape(heads_dev, HEAD * STATE)
-
-    def relay_adjoint(rounds, carried_in):
-        return from_behind(
-            (device_decay[:, None] * carried_in + flat_adjoint).astype(jnp.bfloat16), "seq", -1
-        ).astype(jnp.float32)
-
-    later_adjoint = lax.fori_loop(0, seq_count - 1, relay_adjoint, jnp.zeros_like(flat_adjoint))
+    adjoint_all = lax.all_gather(flat_adjoint.astype(jnp.bfloat16), "seq")
+    later_adjoint = carried_sum(adjoint_all, level_all, seq_index, False)
     later_adjoint = later_adjoint.reshape(heads_dev, HEAD, STATE)
     scan_grad = jnp.concatenate(back_pieces, axis=0) + jnp.exp(cum_level[-1][None, :] - cum_level)[
         :, :, None

time: 781 us -> 553 us (0.71)
  the two profiles are of different devices: /device:TPU:6 before, /device:TPU:0 now
where the time goes in v1:
time: 553 us; the launch traced here: 543 us
  waiting for transfers between devices  199 us (36%)
  matrix products  113 us (20%)
  local copies, waits for them, and re-layouts  87 us (16%)
  blocking collectives  68.5 us (12%)
  starting transfers between devices  32.7 us (6%)
  other arithmetic  28.4 us (5%)
  between operations  15.4 us (3%)
    reduce_scatter x1, waiting for transfers between devices, per_device(): lax.psum_scatter(spread_rows.reshape(BLOCK * lax.axis_size('seq'), half_w...  74.4 us
    all_gather x1, waiting for transfers between devices, per_device(): lax.all_gather(h_block, 'seq', axis=0, tiled=True)  74 us
    all_gather x1, waiting for transfers between devices, per_device(): lax.all_gather(g_block, 'seq', axis=0, tiled=True)  46.9 us
    dot_general x2, matrix products, compact(): jnp.einsum('js,srf->jrf', select, shaped, preferred_element_type=jnp.floa...  25.1 us
    all_gather x1, blocking collectives, per_device(): state_all = lax.all_gather(flat_state.astype(jnp.bfloat16), 'seq')  24 us
    all_gather x1, blocking collectives, per_device(): adjoint_all = lax.all_gather(flat_adjoint.astype(jnp.bfloat16), 'seq')  23.3 us
    ppermute x8, starting transfers between devices, dispatch(): received.append(lax.ppermute(send, ('expert', 'mp'), pairs))  22.2 us
    all_gather x1, blocking collectives, per_device(): level_all = lax.all_gather(cum_level[-1], 'seq')  21.2 us
  transfers between devices with their start and end apart: 17, of which 4 were waited for; matrix products, arithmetic and copies ran while one was open for 27% of the time, Pallas kernels for 0%

profile of v1, /device:TPU:0, one launch (start us, length us, event | category | flops | bytes accessed | tf_op | source)
XLA Modules:
  0.0 543.4 jit_solution(18300160911425266512)
XLA Ops:
  12.6 6.0 %collective-permute-start.3 = (bf16[128,512]{1,0:T(8,128)(2,1)}, bf16[128,512]{1,0:T(8,128)(2,1)}, u32[]{:S(2)}, u32[]{:S(2)}) collective-permute-start(bf16[128,512]{1,0:T(8,128)(2,1)} %bitcast.196), channel_id=1, source_target_pairs={{0,6},{1,0},{2,2},{3,4},{4,7},{5,1},{6,3},{7,5},{8,14},{9,8},{10,1... | collective-permute-start | bytes 393224 | tf_op jit(solution)/shard_map/ppermute | solution.py:53
  43.4 4.0 fusion.58
  47.5 3.4 fusion.90
  54.1 24.0 %all_gather.19 = bf16[16,8,1024]{2,1,0:T(8,128)(2,1)S(1)} all-gather(bf16[1,8,1024]{2,1,0:T(8,128)(2,1)} %convert_element_type.178), channel_id=1, replica_groups=mesh['seq'=16,'expert'=4,'mp'=2] {'seq'}, dimensions={0}, use_global_device_ids=true | all-gather | bytes 278528 | tf_op jit(solution)/shard_map/all_gather | solution.py:167
  78.1 21.2 %all-gather = f32[16,1,8]{2,1,0:T(1,128)} all-gather(f32[1,1,8]{2,1,0:T(1,128)} %bitcast.244), channel_id=1, replica_groups=mesh['seq'=16,'expert'=4,'mp'=2] {'seq'}, dimensions={0}, use_global_device_ids=true | all-gather | bytes 544 | tf_op jit(solution)/shard_map/all_gather | solution.py:166
  107.2 4.1 fusion.56
  117.7 2.9 copy.266
  130.2 3.7 collective-permute-start.7
  151.5 74.0 %all-gather.6.cloned.1.call-done = bf16[2048,2048]{0,1:T(8,128)(2,1)} async-done(((bf16[128,2048]{0,1:T(8,128)(2,1)}), bf16[2048,2048]{0,1:T(8,128)(2,1)}) %all-gather.6.cloned.1.call-update) | async-done | bytes 8388624 | tf_op jit(solution)/shard_map/all_gather | solution.py:195
  225.5 12.8 %copy.269 = bf16[2048,2048]{1,0:T(8,128)(2,1)} copy(bf16[2048,2048]{0,1:T(8,128)(2,1)} %all-gather.6.cloned.1.call-done) | data formatting | bytes 16777216 | tf_op jit(solution)/shard_map/all_gather | solution.py:195
  238.3 12.6 %fusion.52 = bf16[8,128,2048]{2,0,1:T(8,128)(2,1)S(1)} fusion(bf16[16,128,2048]{2,1,0:T(8,128)(2,1)} %bitcast.204, s32[16]{0:T(128)S(1)} %add_reduce_fusion, pred[16]{0:T(512)(128)(4,1)S(1)} %compare_reduce_fusion), kind=kOutput, calls=%fused_computation.52 | convolution fusion | flops 69206272 | bytes 12582992 | tf_op jit(solution)/shard_map/js,srf->jrf/dot_general | solution.py:91
  253.3 4.5 fusion.68
  257.8 46.9 %all-gather.4.cloned.1.call-done = bf16[2048,2048]{0,1:T(8,128)(2,1)} async-done(((bf16[128,2048]{0,1:T(8,128)(2,1)}), bf16[2048,2048]{0,1:T(8,128)(2,1)}) %all-gather.4.cloned.1.call-update) | async-done | bytes 8388624 | tf_op jit(solution)/shard_map/all_gather | solution.py:196
  304.7 12.4 %copy.257 = bf16[2048,2048]{1,0:T(8,128)(2,1)} copy(bf16[2048,2048]{0,1:T(8,128)(2,1)} %all-gather.4.cloned.1.call-done) | data formatting | bytes 16777216 | tf_op jit(solution)/shard_map/all_gather | solution.py:196
  317.2 12.5 %fusion.49 = bf16[8,128,2048]{2,0,1:T(8,128)(2,1)S(1)} fusion(bf16[16,128,2048]{2,1,0:T(8,128)(2,1)} %bitcast.205, s32[16]{0:T(128)S(1)} %add_reduce_fusion, pred[16]{0:T(512)(128)(4,1)S(1)} %compare_reduce_fusion), kind=kOutput, calls=%fused_computation.51 | convolution fusion | flops 69206272 | bytes 12582992 | tf_op jit(solution)/shard_map/js,srf->jrf/dot_general | solution.py:91
  332.0 3.8 fusion.65
  335.9 3.4 collective-permute-done.4
  339.3 3.5 multiply_convert_fusion.1
  342.8 3.7 convolution_convert_fusion.1
  346.5 6.9 %convolution_convert_fusion = bf16[16,128,2048]{2,0,1:T(8,128)(2,1)} fusion(bf16[8,128,2048]{2,1,0:T(8,128)(2,1)S(1)} %bitcast.209, s32[16]{0:T(128)S(1)} %add_reduce_fusion, pred[16]{0:T(512)(128)(4,1)S(1)} %compare_reduce_fusion), kind=kOutput, calls=%fused_computation.13 | convolution fusion | flops 71303424 | bytes 12582992 | tf_op jit(solution)/shard_map/js,jrf->srf/dot_general | solution.py:218
  353.4 11.3 %copy.273 = bf16[16,128,2048]{2,1,0:T(8,128)(2,1)} copy(bf16[16,128,2048]{2,0,1:T(8,128)(2,1)} %convolution_convert_fusion) | data formatting | bytes 16777216 | tf_op jit(solution)/shard_map/convert_element_type | solution.py:220
  366.1 9.5 %convolution_bitcast_fusion = f32[1,768,2048]{2,1,0:T(8,128)} fusion(bf16[1024,2048]{1,0:T(8,128)(2,1)} %bitcast.214, bf16[1024,768]{1,0:T(8,128)(2,1)} %collective-permute-done.9, bf16[1024,768]{1,0:T(8,128)(2,1)} %fusion.68), kind=kOutput, calls=%fused_computation.53 | convolution fusion | flops 3227516928 | bytes 13631488 | tf_op jit(solution)/shard_map/tf,td->fd/dot_general | solution.py:209
  375.7 74.4 %reduce-scatter.2.cloned.1.call-done = bf16[128,2048]{1,0:T(8,128)(2,1)} async-done(((bf16[2048,2048]{1,0:T(8,128)(2,1)}), bf16[128,2048]{1,0:T(8,128)(2,1)}) %reduce-scatter.2.cloned.1.call-update) | async-done | bytes 524304 | tf_op jit(solution)/shard_map/reduce_scatter | solution.py:219
  452.3 3.9 collective-permute-start.11
  458.0 4.8 collective-permute-start.13
  462.9 8.4 %convolution_bitcast_fusion.1 = f32[1,2048,768]{2,1,0:T(8,128)} fusion(bf16[1024,2048]{1,0:T(8,128)(2,1)} %bitcast.212, bf16[1024,768]{1,0:T(8,128)(2,1)S(1)} %copy-done.8), kind=kOutput, calls=%fused_computation.54 | convolution fusion | flops 3221225472 | bytes 12058624 | tf_op jit(solution)/shard_map/td,tf->df/dot_general | solution.py:215
  478.4 4.3 fusion.12
  485.1 4.4 fusion.6
  490.6 23.3 %all_gather.21 = bf16[16,8,1024]{2,1,0:T(8,128)(2,1)S(1)} all-gather(bf16[1,8,1024]{2,1,0:T(8,128)(2,1)S(1)} %convert_element_type.197), channel_id=1, replica_groups=mesh['seq'=16,'expert'=4,'mp'=2] {'seq'}, dimensions={0}, use_global_device_ids=true | all-gather | bytes 278528 | tf_op jit(solution)/shard_map/all_gather | solution.py:271
  514.9 3.6 fusion.105
  529.4 3.0 copy.288
  532.5 4.0 add.290
  (236 shorter events, 106.5 us)
Async XLA Ops:
  7.2 246.1 %copy-start = (bf16[1,2048,768]{2,1,0:T(8,128)(2,1)S(1)}, bf16[1,2048,768]{2,1,0:T(8,128)(2,1)}, u32[]{:S(2)}) copy-start(bf16[1,2048,768]{2,1,0:T(8,128)(2,1)} %param.18) | copy-start | bytes 9437188
  7.2 20.0 %copy-start.50 = (f32[8]{0:T(128)S(1)}, f32[8]{0:T(128)}, u32[]{:S(2)}) copy-start(f32[8]{0:T(128)} %param.15) | copy-start | bytes 100
  7.2 20.7 %copy-start.41 = (s32[1024]{0:T(1024)S(1)}, s32[1024]{0:T(1024)}, u32[]{:S(2)}) copy-start(s32[1024]{0:T(1024)} %param.16) | copy-start | bytes 12292
  7.2 218.3 %all-gather.6.cloned.1.call-start = ((), (), s32[]{:S(2)}) async-start(), calls=%async_computation.2 | async-start | bytes 8912896 | tf_op jit(solution)/shard_map/all_gather | solution.py:195
  8.2 19.7 %copy-start.32 = (s32[16,8]{1,0:T(8,128)}, s32[16,8]{1,0:T(8,128)S(1)}, u32[]{:S(2)}) copy-start(s32[16,8]{1,0:T(8,128)S(1)} %reshape.347) | copy-start | bytes 1540
  11.9 26.2 %copy-start.15 = (bf16[1024,16]{0,1:T(8,128)(2,1)S(1)}, bf16[1024,16]{0,1:T(8,128)(2,1)}, u32[]{:S(2)}) copy-start(bf16[1024,16]{0,1:T(8,128)(2,1)} %param.14) | copy-start | bytes 98308
  11.9 26.2 %copy-start.16 = (bf16[1024,16]{0,1:T(8,128)(2,1)S(1)}, bf16[1024,16]{0,1:T(8,128)(2,1)}, u32[]{:S(2)}) copy-start(bf16[1024,16]{0,1:T(8,128)(2,1)} %param.13) | copy-start | bytes 98308
  12.6 114.8 %collective-permute-start.3 = (bf16[128,512]{1,0:T(8,128)(2,1)}, bf16[128,512]{1,0:T(8,128)(2,1)}, u32[]{:S(2)}, u32[]{:S(2)}) collective-permute-start(bf16[128,512]{1,0:T(8,128)(2,1)} %bitcast.196), channel_id=1, source_target_pairs={{0,6},{1,0},{2,2},{3,4},{4,7},{5,1},{6,3},{7,5},{8,14},{9,8},{10,1... | collective-permute-start | bytes 393224 | tf_op jit(solution)/shard_map/ppermute | solution.py:53
  19.3 110.8 %collective-permute-start = (bf16[128,512]{1,0:T(8,128)(2,1)}, bf16[128,512]{1,0:T(8,128)(2,1)}, u32[]{:S(2)}, u32[]{:S(2)}) collective-permute-start(bf16[128,512]{1,0:T(8,128)(2,1)} %bitcast.199), channel_id=1, source_target_pairs={{0,0},{1,2},{2,4},{3,6},{4,1},{5,3},{6,5},{7,7},{8,8},{9,10},{10,1... | collective-permute-start | bytes 393224 | tf_op jit(solution)/shard_map/ppermute | solution.py:53
  22.2 111.7 %collective-permute-start.1 = (bf16[128,512]{1,0:T(8,128)(2,1)}, bf16[128,512]{1,0:T(8,128)(2,1)}, u32[]{:S(2)}, u32[]{:S(2)}) collective-permute-start(bf16[128,512]{1,0:T(8,128)(2,1)} %bitcast.198), channel_id=1, source_target_pairs={{0,2},{1,4},{2,6},{3,0},{4,3},{5,5},{6,7},{7,1},{8,10},{9,12},{10,... | collective-permute-start | bytes 393224 | tf_op jit(solution)/shard_map/ppermute | solution.py:53
  25.3 110.5 %collective-permute-start.2 = (bf16[128,512]{1,0:T(8,128)(2,1)}, bf16[128,512]{1,0:T(8,128)(2,1)}, u32[]{:S(2)}, u32[]{:S(2)}) collective-permute-start(bf16[128,512]{1,0:T(8,128)(2,1)} %bitcast.197), channel_id=1, source_target_pairs={{0,4},{1,6},{2,0},{3,2},{4,5},{5,7},{6,1},{7,3},{8,12},{9,14},{10,... | collective-permute-start | bytes 393224 | tf_op jit(solution)/shard_map/ppermute | solution.py:53
  27.2 20.2 %copy-start.19 = (pred[512,512]{1,0:T(8,128)(4,1)}, pred[512,512]{1,0:T(8,128)(4,1)S(1)}, u32[]{:S(2)}) copy-start(pred[512,512]{1,0:T(8,128)(4,1)S(1)} %iota_compare_fusion) | copy-start | bytes 786436
  32.1 8.5 %copy-start.40 = (f32[8]{0:T(128)S(1)}, f32[8]{0:T(128)}, u32[]{:S(2)}) copy-start(f32[8]{0:T(128)} %copy-done.39) | copy-start | bytes 100
  32.1 11.3 %copy-start.34 = (f32[8,512]{1,0:T(8,128)S(1)}, f32[8,512]{1,0:T(8,128)}, u32[]{:S(2)}) copy-start(f32[8,512]{1,0:T(8,128)} %get-tuple-element.34) | copy-start | bytes 49156
  117.7 5.1 copy-start.46
  124.7 15.5 %collective-permute-start.5 = (bf16[128,512]{1,0:T(8,128)(2,1)S(1)}, bf16[128,512]{1,0:T(8,128)(2,1)}, u32[]{:S(2)}, u32[]{:S(2)}) collective-permute-start(bf16[128,512]{1,0:T(8,128)(2,1)S(1)} %bitcast.233), channel_id=1, source_target_pairs={{0,0},{1,2},{2,4},{3,6},{4,1},{5,3},{6,5},{7,7},{8,8},{9,10},{10,1... | collective-permute-start | bytes 393224 | tf_op jit(solution)/shard_map/ppermute | solution.py:53
  127.4 12.8 %collective-permute-start.6 = (bf16[128,512]{1,0:T(8,128)(2,1)}, bf16[128,512]{1,0:T(8,128)(2,1)}, u32[]{:S(2)}, u32[]{:S(2)}) collective-permute-start(bf16[128,512]{1,0:T(8,128)(2,1)} %bitcast.194), channel_id=1, source_target_pairs={{0,2},{1,4},{2,6},{3,0},{4,3},{5,5},{6,7},{7,1},{8,10},{9,12},{10,... | collective-permute-start | bytes 393224 | tf_op jit(solution)/shard_map/ppermute | solution.py:53
  130.2 10.0 %collective-permute-start.7 = (bf16[128,512]{1,0:T(8,128)(2,1)}, bf16[128,512]{1,0:T(8,128)(2,1)}, u32[]{:S(2)}, u32[]{:S(2)}) collective-permute-start(bf16[128,512]{1,0:T(8,128)(2,1)} %bitcast.193), channel_id=1, source_target_pairs={{0,4},{1,6},{2,0},{3,2},{4,5},{5,7},{6,1},{7,3},{8,12},{9,14},{10,... | collective-permute-start | bytes 393224 | tf_op jit(solution)/shard_map/ppermute | solution.py:53
  133.9 6.3 %collective-permute-start.8 = (bf16[128,512]{1,0:T(8,128)(2,1)S(1)}, bf16[128,512]{1,0:T(8,128)(2,1)}, u32[]{:S(2)}, u32[]{:S(2)}) collective-permute-start(bf16[128,512]{1,0:T(8,128)(2,1)S(1)} %bitcast.234), channel_id=1, source_target_pairs={{0,6},{1,0},{2,2},{3,4},{4,7},{5,1},{6,3},{7,5},{8,14},{9,8},{10,1... | collective-permute-start | bytes 393224 | tf_op jit(solution)/shard_map/ppermute | solution.py:53
  137.8 13.4 %copy-start.33 = (s32[16,8]{1,0:T(8,128)S(1)}, s32[16,8]{1,0:T(8,128)}, u32[]{:S(2)}) copy-start(s32[16,8]{1,0:T(8,128)} %copy-done.32) | copy-start | bytes 1540
  149.0 155.7 %all-gather.4.cloned.1.call-start = ((), (), s32[]{:S(2)}) async-start(), calls=%async_computation.1 | async-start | bytes 8912896 | tf_op jit(solution)/shard_map/all_gather | solution.py:196
  151.1 299.0 %reduce-scatter.2.cloned.1.call-start = ((), (), s32[]{:S(2)}) async-start(), calls=%async_computation.3 | async-start | bytes 8912896 | tf_op jit(solution)/shard_map/reduce_scatter | solution.py:219
  257.8 78.1 %collective-permute-start.9 = (bf16[1024,768]{1,0:T(8,128)(2,1)}, bf16[1024,768]{1,0:T(8,128)(2,1)}, u32[]{:S(2)}, u32[]{:S(2)}) collective-permute-start(bf16[1024,768]{1,0:T(8,128)(2,1)} %fusion.68), channel_id=1, source_target_pairs={{0,1},{1,0},{2,3},{3,2},{4,5},{5,4},{6,7},{7,6},{8,9},{9,8},{10,11... | collective-permute-start | bytes 4718600 | tf_op jit(solution)/shard_map/ppermute | solution.py:36
  335.8 3.5 collective-permute-start.4
  366.1 96.8 %copy-start.8 = (bf16[1024,768]{1,0:T(8,128)(2,1)S(1)}, bf16[1024,768]{1,0:T(8,128)(2,1)}, u32[]{:S(2)}) copy-start(bf16[1024,768]{1,0:T(8,128)(2,1)} %copy-done.7) | copy-start | bytes 4718596
  451.5 19.8 %collective-permute-start.10 = (bf16[128,512]{1,0:T(8,128)(2,1)S(1)}, bf16[128,512]{1,0:T(8,128)(2,1)S(1)}, u32[]{:S(2)}, u32[]{:S(2)}) collective-permute-start(bf16[128,512]{1,0:T(8,128)(2,1)S(1)} %bitcast.239), channel_id=1, source_target_pairs={{0,0},{2,1},{4,2},{6,3},{1,4},{3,5},{5,6},{7,7},{8,8},{10,9},{12,1... | collective-permute-start | bytes 393224 | tf_op jit(solution)/shard_map/ppermute | solution.py:69
  452.3 19.2 %collective-permute-start.11 = (bf16[128,512]{1,0:T(8,128)(2,1)S(1)}, bf16[128,512]{1,0:T(8,128)(2,1)S(1)}, u32[]{:S(2)}, u32[]{:S(2)}) collective-permute-start(bf16[128,512]{1,0:T(8,128)(2,1)S(1)} %bitcast.240), channel_id=1, source_target_pairs={{2,0},{4,1},{6,2},{0,3},{3,4},{5,5},{7,6},{1,7},{10,8},{12,9},{14,... | collective-permute-start | bytes 393224 | tf_op jit(solution)/shard_map/ppermute | solution.py:69
  456.4 15.3 %collective-permute-start.12 = (bf16[128,512]{1,0:T(8,128)(2,1)S(1)}, bf16[128,512]{1,0:T(8,128)(2,1)S(1)}, u32[]{:S(2)}, u32[]{:S(2)}) collective-permute-start(bf16[128,512]{1,0:T(8,128)(2,1)S(1)} %bitcast.241), channel_id=1, source_target_pairs={{4,0},{6,1},{0,2},{2,3},{5,4},{7,5},{1,6},{3,7},{12,8},{14,9},{8,1... | collective-permute-start | bytes 393224 | tf_op jit(solution)/shard_map/ppermute | solution.py:69
  458.0 13.9 %collective-permute-start.13 = (bf16[128,512]{1,0:T(8,128)(2,1)}, bf16[128,512]{1,0:T(8,128)(2,1)S(1)}, u32[]{:S(2)}, u32[]{:S(2)}) collective-permute-start(bf16[128,512]{1,0:T(8,128)(2,1)} %bitcast.54), channel_id=1, source_target_pairs={{6,0},{0,1},{2,2},{4,3},{7,4},{1,5},{3,6},{5,7},{14,8},{8,9},{10,1... | collective-permute-start | bytes 393224 | tf_op jit(solution)/shard_map/ppermute | solution.py:69
  475.2 7.5 %copy-start.2 = (f32[1024,512]{1,0:T(8,128)}, f32[1024,512]{1,0:T(8,128)S(1)}, u32[]{:S(2)}) copy-start(f32[1024,512]{1,0:T(8,128)S(1)} %bitcast_add_fusion) | copy-start | bytes 6291460
  485.1 29.8 %copy-start.12 = (f32[512,512]{1,0:T(8,128)S(1)}, f32[512,512]{1,0:T(8,128)}, u32[]{:S(2)}) copy-start(f32[512,512]{1,0:T(8,128)} %fusion.147) | copy-start | bytes 3145732
  529.4 7.1 %copy-start.1 = (bf16[1,2048,768]{2,1,0:T(8,128)(2,1)S(1)}, bf16[1,2048,768]{2,1,0:T(8,128)(2,1)}, u32[]{:S(2)}) copy-start(bf16[1,2048,768]{2,1,0:T(8,128)(2,1)} %param.18) | copy-start | bytes 9437188
  (37 other events, 119.9 us)
Sparse Core Ops, SparseCore 0:
  149.1 76.3 all-gather.5
  228.2 76.4 all-gather.3
  364.8 85.1 reduce-scatter.1

commit v2 on v1

--- a/solution.py
+++ b/solution.py
@@ -114,6 +114,18 @@
     my_slice = exp_index * mp_count + mp_index
     half_width = slice_width * exp_count
     slot_total = seq_count // 2
+    blocks_dev = tokens // BLOCK
+    route_table = assign.reshape(seq_count, blocks_dev)
+    own_row = lax.dynamic_index_in_dim(route_table, seq_index, 0, keepdims=False)
+    chosen = (own_row[None, :] == jnp.arange(exp_count)[:, None]).astype(jnp.bfloat16)
+    g_pick = jnp.einsum(
+        "eb,brf->erf",
+        chosen,
+        output_gradient.reshape(blocks_dev, BLOCK, slice_width),
+        preferred_element_type=jnp.float32,
+    ).astype(jnp.bfloat16)
+    g_block = dispatch(g_pick, exp_index, exp_count, mp_count, my_slice)
+    g_all = lax.all_gather(g_block, "seq", axis=0, tiled=True)
     input_scale = jnp.sqrt(1.0 - jnp.exp(-2.0 * head_decay_speed))
     cum_level = jnp.cumsum(
         -head_decay_speed[None, :]
@@ -163,8 +175,10 @@
             precision=highest,
         )
     flat_state = carry_state.reshape(heads_dev, HEAD * STATE)
-    level_all = lax.all_gather(cum_level[-1], "seq")
-    state_all = lax.all_gather(flat_state.astype(jnp.bfloat16), "seq")
+    level_lanes = jnp.broadcast_to(cum_level[-1][:, None], (heads_dev, 128))
+    joined_all = lax.all_gather(jnp.concatenate([flat_state, level_lanes], axis=1), "seq")
+    state_all = joined_all[:, :, : HEAD * STATE]
+    level_all = joined_all[:, :, HEAD * STATE]
     incoming = carried_sum(state_all, level_all, seq_index, True)
     incoming = incoming.reshape(heads_dev, HEAD, STATE)
     outputs = jnp.concatenate(pieces, axis=0) + jnp.exp(cum_level)[:, :, None] * jnp.einsum(
@@ -173,28 +187,15 @@
     mixed_out = (activations.astype(jnp.float32) + outputs.reshape(tokens, slice_width)).astype(
         jnp.bfloat16
     )
-    blocks_dev = tokens // BLOCK
-    route_table = assign.reshape(seq_count, blocks_dev)
-    own_row = lax.dynamic_index_in_dim(route_table, seq_index, 0, keepdims=False)
-    chosen = (own_row[None, :] == jnp.arange(exp_count)[:, None]).astype(jnp.bfloat16)
+    g_all, mixed_out = lax.optimization_barrier((g_all, mixed_out))
     h_pick = jnp.einsum(
         "eb,brf->erf",
         chosen,
         mixed_out.reshape(blocks_dev, BLOCK, slice_width),
         preferred_element_type=jnp.float32,
     ).astype(jnp.bfloat16)
-    g_pick = jnp.einsum(
-        "eb,brf->erf",
-        chosen,
-        output_gradient.reshape(blocks_dev, BLOCK, slice_width),
-        preferred_element_type=jnp.float32,
-    ).astype(jnp.bfloat16)
     h_block = dispatch(h_pick, exp_index, exp_count, mp_count, my_slice)
-    g_block = dispatch(g_pick, exp_index, exp_count, mp_count, my_slice)
-    h_all, g_all = (
-        lax.all_gather(h_block, "seq", axis=0, tiled=True),
-        lax.all_gather(g_block, "seq", axis=0, tiled=True),
-    )
+    h_all = lax.all_gather(h_block, "seq", axis=0, tiled=True)
     present = jnp.any(route_table == exp_index, axis=1)
     slot_of = jnp.cumsum(present.astype(jnp.int32)) - 1
     select = ((slot_of[None, :] == jnp.arange(slot_total)[:, None]) & present[None, :]).astype(

time: 553 us -> 473 us (0.86)
  waiting for transfers between devices: 199 us -> 127 us
  blocking collectives: 68.5 us -> 48.4 us
  matrix products: 113 us -> 124 us
    all_gather x2, waiting for transfers between devices: 121 us -> 44 us  [the longest x1 44 us: per_device(): h_all = lax.all_gather(h_block, 'seq', axis=0, tiled=True)]
    all_gather x2 -> x1, blocking collectives: 45.2 us -> 25.1 us  [per_device(): lax.all_gather(jnp.concatenate([flat_state, level_lanes], axis=1), 'seq')]
    all_gather x3 -> x1, local copies, waits for them, and re-layouts: 26.6 us -> 12.7 us  [per_device(): h_all = lax.all_gather(h_block, 'seq', axis=0, tiled=True)]
    dot_general x1, matrix products: 2.34 us -> 15.6 us  [per_device(): jnp.einsum('tn,hpn->thp', c_float, incoming, precision=highest)]
    optimization_barrier x0 -> x1, local copies, waits for them, and re-layouts: none -> 12.3 us  [per_device(): g_all, mixed_out = lax.optimization_barrier((g_all, mixed_out))]
    ppermute x8, waiting for transfers between devices: 0.02 us -> 5.67 us  [dispatch(): received.append(lax.ppermute(send, ('expert', 'mp'), pairs))]
  transfers between devices with their start and end apart: 17 -> 17, of which waited for: 4 -> 6; matrix products, arithmetic and copies ran while one was open for 27% -> 31% of each run, Pallas kernels for 0% -> 0%
where the time goes in v2:
time: 473 us; the launch traced here: 466 us
  waiting for transfers between devices  127 us (27%)
  matrix products  124 us (26%)
  local copies, waits for them, and re-layouts  85.5 us (18%)
  blocking collectives  48.4 us (10%)
  starting transfers between devices  36.5 us (8%)
  other arithmetic  29.1 us (6%)
  between operations  15.3 us (3%)
    reduce_scatter x1, waiting for transfers between devices, per_device(): lax.psum_scatter(spread_rows.reshape(BLOCK * lax.axis_size('seq'), half_w...  74.4 us
    all_gather x1, waiting for transfers between devices, per_device(): h_all = lax.all_gather(h_block, 'seq', axis=0, tiled=True)  44 us
    all_gather x1, blocking collectives, per_device(): lax.all_gather(jnp.concatenate([flat_state, level_lanes], axis=1), 'seq')  25.1 us
    dot_general x2, matrix products, compact(): jnp.einsum('js,srf->jrf', select, shaped, preferred_element_type=jnp.floa...  25 us
    ppermute x8, starting transfers between devices, dispatch(): received.append(lax.ppermute(send, ('expert', 'mp'), pairs))  24.6 us
    all_gather x1, blocking collectives, per_device(): adjoint_all = lax.all_gather(flat_adjoint.astype(jnp.bfloat16), 'seq')  23.3 us
    dot_general x1, matrix products, per_device(): jnp.einsum('tn,hpn->thp', c_float, incoming, precision=highest)  15.6 us
    all_gather x1, local copies, waits for them, and re-layouts, per_device(): h_all = lax.all_gather(h_block, 'seq', axis=0, tiled=True)  12.7 us
  transfers between devices with their start and end apart: 17, of which 6 were waited for; matrix products, arithmetic and copies ran while one was open for 31% of the time, Pallas kernels for 0%

profile of v2, /device:TPU:0, one launch (start us, length us, event | category | flops | bytes accessed | tf_op | source)
XLA Modules:
  0.0 465.8 jit_solution(2502755287572609092)
XLA Ops:
  11.9 6.1 %collective-permute-start.3 = (bf16[128,512]{1,0:T(8,128)(2,1)S(1)}, bf16[128,512]{1,0:T(8,128)(2,1)S(1)}, u32[]{:S(2)}, u32[]{:S(2)}) collective-permute-start(bf16[128,512]{1,0:T(8,128)(2,1)S(1)} %bitcast.235), channel_id=1, source_target_pairs={{0,6},{1,0},{2,2},{3,4},{4,7},{5,1},{6,3},{7,5},{8,14},{9,8},{10,1... | collective-permute-start | bytes 393224 | tf_op jit(solution)/shard_map/ppermute | solution.py:53
  18.7 4.0 collective-permute-start.1
  50.0 25.1 %all-gather = f32[128,1152]{1,0:T(8,128)S(1)} all-gather(f32[8,1152]{1,0:T(8,128)S(1)} %pad_maximum_fusion.2), channel_id=2, replica_groups=mesh['seq'=16,'expert'=4,'mp'=2] {'seq'}, dimensions={0}, use_global_device_ids=true | all-gather | bytes 626688 | tf_op jit(solution)/shard_map/all_gather | solution.py:179
  88.2 4.2 fusion.56
  101.9 15.6 %maximum_add_fusion = f32[1024,8,64]{0,2,1:T(8,128)} fusion(f32[512,8,64]{0,2,1:T(8,128)S(1)} %fusion.77, f32[512,8,64]{0,2,1:T(8,128)S(1)} %fusion.79, f32[8,64,16]{2,1,0:T(8,128)S(1)} %reshape.344, f32[1024,8]{0,1:T(8,128)S(1)} %get-tuple-element.33, bf16[1024,16]{0,1:T(8,128)(2,1)S(1)} %copy-done.16), kind=kOutput, calls=%fused_computation.69 | convolution fusion | flops 102236160 | bytes 4292608 | tf_op jit(solution)/shard_map/tn,hpn->thp/dot_general | solution.py:184
  117.5 2.9 copy.263
  120.4 3.2 add_convert_fusion
  127.4 6.4 %collective-permute-start.6 = (bf16[128,512]{1,0:T(8,128)(2,1)S(1)}, bf16[128,512]{1,0:T(8,128)(2,1)S(1)}, u32[]{:S(2)}, u32[]{:S(2)}) collective-permute-start(bf16[128,512]{1,0:T(8,128)(2,1)S(1)} %bitcast.243), channel_id=1, source_target_pairs={{0,2},{1,4},{2,6},{3,0},{4,3},{5,5},{6,7},{7,1},{8,10},{9,12},{10,... | collective-permute-start | bytes 393224 | tf_op jit(solution)/shard_map/ppermute | solution.py:53
  135.3 3.5 collective-permute-start.8
  149.1 12.3 %copy.264 = bf16[2048,2048]{1,0:T(8,128)(2,1)} copy(bf16[2048,2048]{0,1:T(8,128)(2,1)} %all-gather.4.cloned.1.call-done) | data formatting | bytes 16777216 | tf_op jit(solution)/shard_map/optimization_barrier | solution.py:190
  161.5 12.5 %fusion.49 = bf16[8,128,2048]{2,0,1:T(8,128)(2,1)S(1)} fusion(bf16[16,128,2048]{2,1,0:T(8,128)(2,1)} %bitcast.204, s32[16]{0:T(128)S(1)} %add_reduce_fusion, pred[16]{0:T(512)(128)(4,1)S(1)} %compare_reduce_fusion), kind=kOutput, calls=%fused_computation.51 | convolution fusion | flops 69206272 | bytes 12582992 | tf_op jit(solution)/shard_map/js,srf->jrf/dot_general | solution.py:91
  176.3 4.6 fusion.65
  181.8 44.0 %all-gather.6.cloned.1.call-done = bf16[2048,2048]{0,1:T(8,128)(2,1)} async-done(((bf16[128,2048]{0,1:T(8,128)(2,1)}), bf16[2048,2048]{0,1:T(8,128)(2,1)}) %all-gather.6.cloned.1.call-update) | async-done | bytes 8388624 | tf_op jit(solution)/shard_map/all_gather | solution.py:198
  225.8 12.7 %copy.269 = bf16[2048,2048]{1,0:T(8,128)(2,1)} copy(bf16[2048,2048]{0,1:T(8,128)(2,1)} %all-gather.6.cloned.1.call-done) | data formatting | bytes 16777216 | tf_op jit(solution)/shard_map/all_gather | solution.py:198
  238.5 12.5 %fusion.52 = bf16[8,128,2048]{2,0,1:T(8,128)(2,1)S(1)} fusion(bf16[16,128,2048]{2,1,0:T(8,128)(2,1)} %bitcast.205, s32[16]{0:T(128)S(1)} %add_reduce_fusion, pred[16]{0:T(512)(128)(4,1)S(1)} %compare_reduce_fusion), kind=kOutput, calls=%fused_computation.52 | convolution fusion | flops 69206272 | bytes 12582992 | tf_op jit(solution)/shard_map/js,srf->jrf/dot_general | solution.py:91
  253.3 3.6 fusion.68
  257.0 3.4 collective-permute-done.9
  261.6 3.5 multiply_convert_fusion.1
  265.1 3.7 convolution_convert_fusion.1
  268.8 6.9 %convolution_convert_fusion = bf16[16,128,2048]{2,0,1:T(8,128)(2,1)} fusion(bf16[8,128,2048]{2,1,0:T(8,128)(2,1)S(1)} %bitcast.209, s32[16]{0:T(128)S(1)} %add_reduce_fusion, pred[16]{0:T(512)(128)(4,1)S(1)} %compare_reduce_fusion), kind=kOutput, calls=%fused_computation.13 | convolution fusion | flops 71303424 | bytes 12582992 | tf_op jit(solution)/shard_map/js,jrf->srf/dot_general | solution.py:219
  275.7 11.3 %copy.273 = bf16[16,128,2048]{2,1,0:T(8,128)(2,1)} copy(bf16[16,128,2048]{2,0,1:T(8,128)(2,1)} %convolution_convert_fusion) | data formatting | bytes 16777216 | tf_op jit(solution)/shard_map/convert_element_type | solution.py:221
  288.4 9.5 %convolution_bitcast_fusion = f32[1,768,2048]{2,1,0:T(8,128)} fusion(bf16[1024,2048]{1,0:T(8,128)(2,1)} %bitcast.214, bf16[1024,768]{1,0:T(8,128)(2,1)} %copy-done.10, bf16[1024,768]{1,0:T(8,128)(2,1)} %copy-done.9), kind=kOutput, calls=%fused_computation.53 | convolution fusion | flops 3227516928 | bytes 13631488 | tf_op jit(solution)/shard_map/tf,td->fd/dot_general | solution.py:210
  297.9 74.4 %reduce-scatter.2.cloned.1.call-done = bf16[128,2048]{1,0:T(8,128)(2,1)} async-done(((bf16[2048,2048]{1,0:T(8,128)(2,1)}), bf16[128,2048]{1,0:T(8,128)(2,1)}) %reduce-scatter.2.cloned.1.call-update) | async-done | bytes 524304 | tf_op jit(solution)/shard_map/reduce_scatter | solution.py:220
  374.6 4.0 collective-permute-start.11
  380.4 5.1 %collective-permute-start.13 = (bf16[128,512]{1,0:T(8,128)(2,1)}, bf16[128,512]{1,0:T(8,128)(2,1)S(1)}, u32[]{:S(2)}, u32[]{:S(2)}) collective-permute-start(bf16[128,512]{1,0:T(8,128)(2,1)} %bitcast.55), channel_id=1, source_target_pairs={{6,0},{0,1},{2,2},{4,3},{7,4},{1,5},{3,6},{5,7},{14,8},{8,9},{10,1... | collective-permute-start | bytes 393224 | tf_op jit(solution)/shard_map/ppermute | solution.py:69
  385.5 8.4 %convolution_bitcast_fusion.1 = f32[1,2048,768]{2,1,0:T(8,128)} fusion(bf16[1024,2048]{1,0:T(8,128)(2,1)} %bitcast.212, bf16[1024,768]{1,0:T(8,128)(2,1)S(1)} %copy-done.8), kind=kOutput, calls=%fused_computation.54 | convolution fusion | flops 3221225472 | bytes 12058624 | tf_op jit(solution)/shard_map/td,tf->df/dot_general | solution.py:216
  401.0 4.3 fusion.12
  407.7 4.4 fusion.6
  413.2 23.3 %all_gather.20 = bf16[16,8,1024]{2,1,0:T(8,128)(2,1)S(1)} all-gather(bf16[1,8,1024]{2,1,0:T(8,128)(2,1)S(1)} %convert_element_type.178), channel_id=1, replica_groups=mesh['seq'=16,'expert'=4,'mp'=2] {'seq'}, dimensions={0}, use_global_device_ids=true | all-gather | bytes 278528 | tf_op jit(solution)/shard_map/all_gather | solution.py:272
  437.5 3.6 fusion.105
  452.0 3.0 copy.288
  455.0 4.0 add.290
  (243 shorter events, 104.5 us)
Async XLA Ops:
  7.2 246.1 %copy-start = (bf16[1,2048,768]{2,1,0:T(8,128)(2,1)S(1)}, bf16[1,2048,768]{2,1,0:T(8,128)(2,1)}, u32[]{:S(2)}) copy-start(bf16[1,2048,768]{2,1,0:T(8,128)(2,1)} %param.18) | copy-start | bytes 9437188
  7.2 116.4 %all-gather.4.cloned.1.call-start = ((), (), s32[]{:S(2)}) async-start(), calls=%async_computation.1 | async-start | bytes 8912896 | tf_op jit(solution)/shard_map/all_gather | solution.py:128
  8.2 24.9 %copy-start.32 = (s32[16,8]{1,0:T(8,128)}, s32[16,8]{1,0:T(8,128)S(1)}, u32[]{:S(2)}) copy-start(s32[16,8]{1,0:T(8,128)S(1)} %reshape.339) | copy-start | bytes 1540
  10.8 24.5 %copy-start.52 = (f32[8]{0:T(128)S(1)}, f32[8]{0:T(128)}, u32[]{:S(2)}) copy-start(f32[8]{0:T(128)} %param.15) | copy-start | bytes 100
  10.8 24.5 %copy-start.41 = (s32[1024]{0:T(1024)S(1)}, s32[1024]{0:T(1024)}, u32[]{:S(2)}) copy-start(s32[1024]{0:T(1024)} %param.16) | copy-start | bytes 12292
  11.9 12.8 %collective-permute-start.3 = (bf16[128,512]{1,0:T(8,128)(2,1)S(1)}, bf16[128,512]{1,0:T(8,128)(2,1)S(1)}, u32[]{:S(2)}, u32[]{:S(2)}) collective-permute-start(bf16[128,512]{1,0:T(8,128)(2,1)S(1)} %bitcast.235), channel_id=1, source_target_pairs={{0,6},{1,0},{2,2},{3,4},{4,7},{5,1},{6,3},{7,5},{8,14},{9,8},{10,1... | collective-permute-start | bytes 393224 | tf_op jit(solution)/shard_map/ppermute | solution.py:53
  18.0 6.7 %collective-permute-start = (bf16[128,512]{1,0:T(8,128)(2,1)S(1)}, bf16[128,512]{1,0:T(8,128)(2,1)S(1)}, u32[]{:S(2)}, u32[]{:S(2)}) collective-permute-start(bf16[128,512]{1,0:T(8,128)(2,1)S(1)} %bitcast.239), channel_id=1, source_target_pairs={{0,0},{1,2},{2,4},{3,6},{4,1},{5,3},{6,5},{7,7},{8,8},{9,10},{10,1... | collective-permute-start | bytes 393224 | tf_op jit(solution)/shard_map/ppermute | solution.py:53
  18.7 7.4 %collective-permute-start.1 = (bf16[128,512]{1,0:T(8,128)(2,1)S(1)}, bf16[128,512]{1,0:T(8,128)(2,1)S(1)}, u32[]{:S(2)}, u32[]{:S(2)}) collective-permute-start(bf16[128,512]{1,0:T(8,128)(2,1)S(1)} %bitcast.241), channel_id=1, source_target_pairs={{0,2},{1,4},{2,6},{3,0},{4,3},{5,5},{6,7},{7,1},{8,10},{9,12},{10,... | collective-permute-start | bytes 393224 | tf_op jit(solution)/shard_map/ppermute | solution.py:53
  22.7 5.1 %collective-permute-start.2 = (bf16[128,512]{1,0:T(8,128)(2,1)S(1)}, bf16[128,512]{1,0:T(8,128)(2,1)S(1)}, u32[]{:S(2)}, u32[]{:S(2)}) collective-permute-start(bf16[128,512]{1,0:T(8,128)(2,1)S(1)} %bitcast.244), channel_id=1, source_target_pairs={{0,4},{1,6},{2,0},{3,2},{4,5},{5,7},{6,1},{7,3},{8,12},{9,14},{10,... | collective-permute-start | bytes 393224 | tf_op jit(solution)/shard_map/ppermute | solution.py:53
  24.7 10.6 %copy-start.47 = (pred[4]{0:T(512)(128)(4,1)}, pred[4]{0:T(512)(128)(4,1)S(1)}, u32[]{:S(2)}) copy-start(pred[4]{0:T(512)(128)(4,1)S(1)} %compare_and_fusion) | copy-start | bytes 16
  24.7 10.6 %copy-start.40 = (s32[1024]{0:T(1024)}, s32[1024]{0:T(1024)S(1)}, u32[]{:S(2)}) copy-start(s32[1024]{0:T(1024)S(1)} %pad_clamp_fusion) | copy-start | bytes 12292
  35.2 9.5 %copy-start.17 = (bf16[1024,16]{0,1:T(8,128)(2,1)S(1)}, bf16[1024,16]{0,1:T(8,128)(2,1)}, u32[]{:S(2)}) copy-start(bf16[1024,16]{0,1:T(8,128)(2,1)} %param.13) | copy-start | bytes 98308
  35.2 190.6 %all-gather.6.cloned.1.call-start = ((), (), s32[]{:S(2)}) async-start(), calls=%async_computation.2 | async-start | bytes 8912896 | tf_op jit(solution)/shard_map/all_gather | solution.py:198
  35.3 9.3 %copy-start.42 = (f32[8]{0:T(128)}, f32[8]{0:T(128)S(1)}, u32[]{:S(2)}) copy-start(f32[8]{0:T(128)S(1)} %get-tuple-element.44) | copy-start | bytes 100
  45.4 42.1 %copy-start.16 = (bf16[1024,16]{0,1:T(8,128)(2,1)S(1)}, bf16[1024,16]{0,1:T(8,128)(2,1)}, u32[]{:S(2)}) copy-start(bf16[1024,16]{0,1:T(8,128)(2,1)} %param.14) | copy-start | bytes 98308
  86.0 12.5 %copy-start.21 = (pred[512,512]{1,0:T(8,128)(4,1)}, pred[512,512]{1,0:T(8,128)(4,1)S(1)}, u32[]{:S(2)}) copy-start(pred[512,512]{1,0:T(8,128)(4,1)S(1)} %iota_compare_fusion) | copy-start | bytes 786436
  87.8 10.7 %copy-start.11 = (f32[512,512]{1,0:T(8,128)}, f32[512,512]{1,0:T(8,128)S(1)}, u32[]{:S(2)}) copy-start(f32[512,512]{1,0:T(8,128)S(1)} %fusion.140) | copy-start | bytes 3145732
  123.5 21.1 %copy-start.48 = (pred[4]{0:T(512)(128)(4,1)S(1)}, pred[4]{0:T(512)(128)(4,1)}, u32[]{:S(2)}) copy-start(pred[4]{0:T(512)(128)(4,1)} %copy-done.47) | copy-start | bytes 16
  125.5 23.2 %copy-start.33 = (s32[16,8]{1,0:T(8,128)S(1)}, s32[16,8]{1,0:T(8,128)}, u32[]{:S(2)}) copy-start(s32[16,8]{1,0:T(8,128)} %copy-done.32) | copy-start | bytes 1540
  126.7 12.1 %collective-permute-start.5 = (bf16[128,512]{1,0:T(8,128)(2,1)S(1)}, bf16[128,512]{1,0:T(8,128)(2,1)S(1)}, u32[]{:S(2)}, u32[]{:S(2)}) collective-permute-start(bf16[128,512]{1,0:T(8,128)(2,1)S(1)} %bitcast.242), channel_id=1, source_target_pairs={{0,0},{1,2},{2,4},{3,6},{4,1},{5,3},{6,5},{7,7},{8,8},{9,10},{10,1... | collective-permute-start | bytes 393224 | tf_op jit(solution)/shard_map/ppermute | solution.py:53
  127.4 11.4 %collective-permute-start.6 = (bf16[128,512]{1,0:T(8,128)(2,1)S(1)}, bf16[128,512]{1,0:T(8,128)(2,1)S(1)}, u32[]{:S(2)}, u32[]{:S(2)}) collective-permute-start(bf16[128,512]{1,0:T(8,128)(2,1)S(1)} %bitcast.243), channel_id=1, source_target_pairs={{0,2},{1,4},{2,6},{3,0},{4,3},{5,5},{6,7},{7,1},{8,10},{9,12},{10,... | collective-permute-start | bytes 393224 | tf_op jit(solution)/shard_map/ppermute | solution.py:53
  133.8 5.0 %collective-permute-start.7 = (bf16[128,512]{1,0:T(8,128)(2,1)S(1)}, bf16[128,512]{1,0:T(8,128)(2,1)S(1)}, u32[]{:S(2)}, u32[]{:S(2)}) collective-permute-start(bf16[128,512]{1,0:T(8,128)(2,1)S(1)} %bitcast.245), channel_id=1, source_target_pairs={{0,4},{1,6},{2,0},{3,2},{4,5},{5,7},{6,1},{7,3},{8,12},{9,14},{10,... | collective-permute-start | bytes 393224 | tf_op jit(solution)/shard_map/ppermute | solution.py:53
  135.3 6.0 %collective-permute-start.8 = (bf16[128,512]{1,0:T(8,128)(2,1)S(1)}, bf16[128,512]{1,0:T(8,128)(2,1)S(1)}, u32[]{:S(2)}, u32[]{:S(2)}) collective-permute-start(bf16[128,512]{1,0:T(8,128)(2,1)S(1)} %bitcast.246), channel_id=1, source_target_pairs={{0,6},{1,0},{2,2},{3,4},{4,7},{5,1},{6,3},{7,5},{8,14},{9,8},{10,1... | collective-permute-start | bytes 393224 | tf_op jit(solution)/shard_map/ppermute | solution.py:53
  148.7 223.6 %reduce-scatter.2.cloned.1.call-start = ((), (), s32[]{:S(2)}) async-start(), calls=%async_computation.3 | async-start | bytes 8912896 | tf_op jit(solution)/shard_map/reduce_scatter | solution.py:220
  180.9 76.1 %collective-permute-start.4 = (bf16[1024,768]{1,0:T(8,128)(2,1)}, bf16[1024,768]{1,0:T(8,128)(2,1)}, u32[]{:S(2)}, u32[]{:S(2)}) collective-permute-start(bf16[1024,768]{1,0:T(8,128)(2,1)} %fusion.65), channel_id=1, source_target_pairs={{0,1},{1,0},{2,3},{3,2},{4,5},{5,4},{6,7},{7,6},{8,9},{9,8},{10,11... | collective-permute-start | bytes 4718600 | tf_op jit(solution)/shard_map/ppermute | solution.py:36
  256.9 3.5 collective-permute-start.9
  288.4 97.1 %copy-start.8 = (bf16[1024,768]{1,0:T(8,128)(2,1)S(1)}, bf16[1024,768]{1,0:T(8,128)(2,1)}, u32[]{:S(2)}) copy-start(bf16[1024,768]{1,0:T(8,128)(2,1)} %copy-done.7) | copy-start | bytes 4718596
  373.8 20.1 %collective-permute-start.10 = (bf16[128,512]{1,0:T(8,128)(2,1)S(1)}, bf16[128,512]{1,0:T(8,128)(2,1)S(1)}, u32[]{:S(2)}, u32[]{:S(2)}) collective-permute-start(bf16[128,512]{1,0:T(8,128)(2,1)S(1)} %bitcast.247), channel_id=1, source_target_pairs={{0,0},{2,1},{4,2},{6,3},{1,4},{3,5},{5,6},{7,7},{8,8},{10,9},{12,1... | collective-permute-start | bytes 393224 | tf_op jit(solution)/shard_map/ppermute | solution.py:69
  374.6 19.5 %collective-permute-start.11 = (bf16[128,512]{1,0:T(8,128)(2,1)S(1)}, bf16[128,512]{1,0:T(8,128)(2,1)S(1)}, u32[]{:S(2)}, u32[]{:S(2)}) collective-permute-start(bf16[128,512]{1,0:T(8,128)(2,1)S(1)} %bitcast.248), channel_id=1, source_target_pairs={{2,0},{4,1},{6,2},{0,3},{3,4},{5,5},{7,6},{1,7},{10,8},{12,9},{14,... | collective-permute-start | bytes 393224 | tf_op jit(solution)/shard_map/ppermute | solution.py:69
  378.8 15.6 %collective-permute-start.12 = (bf16[128,512]{1,0:T(8,128)(2,1)S(1)}, bf16[128,512]{1,0:T(8,128)(2,1)S(1)}, u32[]{:S(2)}, u32[]{:S(2)}) collective-permute-start(bf16[128,512]{1,0:T(8,128)(2,1)S(1)} %bitcast.249), channel_id=1, source_target_pairs={{4,0},{6,1},{0,2},{2,3},{5,4},{7,5},{1,6},{3,7},{12,8},{14,9},{8,1... | collective-permute-start | bytes 393224 | tf_op jit(solution)/shard_map/ppermute | solution.py:69
  380.4 14.2 %collective-permute-start.13 = (bf16[128,512]{1,0:T(8,128)(2,1)}, bf16[128,512]{1,0:T(8,128)(2,1)S(1)}, u32[]{:S(2)}, u32[]{:S(2)}) collective-permute-start(bf16[128,512]{1,0:T(8,128)(2,1)} %bitcast.55), channel_id=1, source_target_pairs={{6,0},{0,1},{2,2},{4,3},{7,4},{1,5},{3,6},{5,7},{14,8},{8,9},{10,1... | collective-permute-start | bytes 393224 | tf_op jit(solution)/shard_map/ppermute | solution.py:69
  407.7 29.8 %copy-start.14 = (f32[512,512]{1,0:T(8,128)S(1)}, f32[512,512]{1,0:T(8,128)}, u32[]{:S(2)}) copy-start(f32[512,512]{1,0:T(8,128)} %copy-done.13) | copy-start | bytes 3145732
  (39 other events, 132.6 us)
Sparse Core Ops, SparseCore 0:
  35.3 80.2 all-gather.3
  148.8 76.9 all-gather.5
  287.1 85.1 reduce-scatter.1

commit v3 on v2

--- a/solution.py
+++ b/solution.py
@@ -87,9 +87,27 @@
 
 
 def compact(select, gathered, half_width):
-    shaped = gathered.reshape(select.shape[1], -1, half_width)
-    rows_out = jnp.einsum("js,srf->jrf", select, shaped, preferred_element_type=jnp.float32)
-    return rows_out.astype(jnp.bfloat16).reshape(-1, half_width)
+    blocks = gathered.reshape(select.shape[1], -1, half_width)
+    used = jnp.any(select > 0, axis=1)
+    source = jnp.argmax(select, axis=1)
+    rows_out = [
+        jnp.where(used[slot], lax.dynamic_index_in_dim(blocks, source[slot], 0, keepdims=False), 0)
+        for slot in range(select.shape[0])
+    ]
+    return jnp.concatenate(rows_out, axis=0).astype(jnp.bfloat16)
+
+
+def spread(present, slot_of, rows, half_width):
+    blocks = rows.reshape(-1, BLOCK, half_width)
+    placed = [
+        jnp.where(
+            present[shard],
+            lax.dynamic_index_in_dim(blocks, jnp.maximum(slot_of[shard], 0), 0, keepdims=False),
+            0,
+        )
+        for shard in range(present.shape[0])
+    ]
+    return jnp.concatenate(placed, axis=0).astype(jnp.bfloat16)
 
 
 def per_device(
@@ -125,7 +143,7 @@
         preferred_element_type=jnp.float32,
     ).astype(jnp.bfloat16)
     g_block = dispatch(g_pick, exp_index, exp_count, mp_count, my_slice)
-    g_all = lax.all_gather(g_block, "seq", axis=0, tiled=True)
+    g_all = lax.all_gather(g_block, "seq", axis=0)
     input_scale = jnp.sqrt(1.0 - jnp.exp(-2.0 * head_decay_speed))
     cum_level = jnp.cumsum(
         -head_decay_speed[None, :]
@@ -195,7 +213,7 @@
         preferred_element_type=jnp.float32,
     ).astype(jnp.bfloat16)
     h_block = dispatch(h_pick, exp_index, exp_count, mp_count, my_slice)
-    h_all = lax.all_gather(h_block, "seq", axis=0, tiled=True)
+    h_all = lax.all_gather(h_block, "seq", axis=0)
     present = jnp.any(route_table == exp_index, axis=1)
     slot_of = jnp.cumsum(present.astype(jnp.int32)) - 1
     select = ((slot_of[None, :] == jnp.arange(slot_total)[:, None]) & present[None, :]).astype(
@@ -215,10 +233,9 @@
     pre_grad = (act_grad * sigmoid_pre * (1.0 + pre_act * (1.0 - sigmoid_pre))).astype(jnp.bfloat16)
     up_grad = jnp.einsum("td,tf->df", x_rows, pre_grad, preferred_element_type=jnp.float32)
     row_grad = jnp.einsum("tf,df->td", pre_grad, up_local, preferred_element_type=jnp.float32)
-    row_grad = row_grad.astype(jnp.bfloat16).reshape(slot_total, BLOCK, half_width)
-    spread_rows = jnp.einsum("js,jrf->srf", select, row_grad, preferred_element_type=jnp.float32)
+    spread_rows = spread(present, slot_of, row_grad.astype(jnp.bfloat16), half_width)
     back_rows = lax.psum_scatter(
-        spread_rows.reshape(BLOCK * lax.axis_size("seq"), half_width).astype(jnp.bfloat16),
+        spread_rows,
         "seq",
         scatter_dimension=0,
         tiled=True,

time: 473 us -> 463 us (0.979)
  other arithmetic: 29.1 us -> 82.7 us
  matrix products: 124 us -> 78.8 us
  local copies, waits for them, and re-layouts: 85.5 us -> 52.4 us
  between operations: 15.3 us -> 40.5 us
  waiting for transfers between devices: 127 us -> 116 us
    unnamed x3 -> x4, waiting for transfers between devices: 0.05 us -> 75.9 us
    reduce_scatter x1 -> x0, waiting for transfers between devices: 74.4 us -> none  [per_device(): lax.psum_scatter(spread_rows.reshape(BLOCK * lax.axis_size('seq'), half_w...]
    unnamed x1 -> x30, other arithmetic: 0.08 us -> 48.1 us
    dot_general x3 -> x0, matrix products: 31.8 us -> none  [the longest x2 25 us: compact(): jnp.einsum('js,srf->jrf', select, shaped, preferred_element_type=jnp.floa...]
    convert_element_type x3 -> x0, local copies, waits for them, and re-layouts: 15.9 us -> none  [the longest x1 11.3 us: per_device(): spread_rows.reshape(BLOCK * lax.axis_size('seq'), half_width)]
    dot_general x1, matrix products: 15.6 us -> 2.81 us  [per_device(): jnp.einsum('tn,hpn->thp', c_float, incoming, precision=highest)]
    all_gather x1 -> x0, local copies, waits for them, and re-layouts: 12.7 us -> none  [per_device(): h_all = lax.all_gather(h_block, 'seq', axis=0, tiled=True)]
    optimization_barrier x1 -> x0, local copies, waits for them, and re-layouts: 12.3 us -> none  [per_device(): g_all, mixed_out = lax.optimization_barrier((g_all, mixed_out))]
  transfers between devices with their start and end apart: 17 -> 17, of which waited for: 6 -> 6; matrix products, arithmetic and copies ran while one was open for 31% -> 24% of each run, Pallas kernels for 0% -> 0%
where the time goes in v3:
time: 463 us; the launch traced here: 455 us
  waiting for transfers between devices  116 us (25%)
  other arithmetic  82.7 us (18%)
  matrix products  78.8 us (17%)
  local copies, waits for them, and re-layouts  52.4 us (11%)
  blocking collectives  48.3 us (10%)
  between operations  40.5 us (9%)
  starting transfers between devices  36.9 us (8%)
    unnamed x4, waiting for transfers between devices  75.9 us
    unnamed x30, other arithmetic  48.1 us
    all_gather x1, waiting for transfers between devices, per_device(): h_all = lax.all_gather(h_block, 'seq', axis=0)  34.3 us
    ppermute x8, starting transfers between devices, dispatch(): received.append(lax.ppermute(send, ('expert', 'mp'), pairs))  26 us
    all_gather x1, blocking collectives, per_device(): lax.all_gather(jnp.concatenate([flat_state, level_lanes], axis=1), 'seq')  24.9 us
    all_gather x1, blocking collectives, per_device(): adjoint_all = lax.all_gather(flat_adjoint.astype(jnp.bfloat16), 'seq')  23.3 us
    ppermute x4, starting transfers between devices, give_back(): received.append(lax.ppermute(send, ('expert', 'mp'), pairs))  10.4 us
    dot_general x2, matrix products, per_device(): jnp.einsum('hts,thp->shp', weight_high, grad_low, preferred_element_type=...  9.4 us
  transfers between devices with their start and end apart: 17, of which 6 were waited for; matrix products, arithmetic and copies ran while one was open for 24% of the time, Pallas kernels for 0%

profile of v3, /device:TPU:0, one launch (start us, length us, event | category | flops | bytes accessed | tf_op | source)
XLA Modules:
  0.0 455.3 jit_solution(1705713660174789465)
XLA Ops:
  11.9 4.1 collective-permute-start.2
  18.8 4.3 collective-permute-start.1
  23.2 2.6 collective-permute-done.1
  38.7 2.6 copy.209
  50.0 24.9 %all-gather = f32[128,1152]{1,0:T(8,128)S(1)} all-gather(f32[8,1152]{1,0:T(8,128)S(1)} %pad_maximum_fusion.2), channel_id=2, replica_groups=mesh['seq'=16,'expert'=4,'mp'=2] {'seq'}, dimensions={0}, use_global_device_ids=true | all-gather | bytes 626688 | tf_op jit(solution)/shard_map/all_gather | solution.py:197
  88.0 4.2 fusion.45
  92.3 2.7 fusion.91
  95.6 2.7 fusion.47
  98.4 2.7 fusion.79
  101.7 2.8 maximum_add_fusion
  104.5 2.9 copy.213
  107.4 3.2 add_convert_fusion
  114.7 8.9 %collective-permute-start.6 = (bf16[128,512]{1,0:T(8,128)(2,1)S(1)}, bf16[128,512]{1,0:T(8,128)(2,1)S(1)}, u32[]{:S(2)}, u32[]{:S(2)}) collective-permute-start(bf16[128,512]{1,0:T(8,128)(2,1)S(1)} %bitcast.354), channel_id=1, source_target_pairs={{0,2},{1,4},{2,6},{3,0},{4,3},{5,5},{6,7},{7,1},{8,10},{9,12},{10,... | collective-permute-start | bytes 393224 | tf_op jit(solution)/shard_map/ppermute | solution.py:53
  123.6 3.4 collective-permute-start.7
  172.5 4.6 %fusion.54 = bf16[1024,768]{1,0:T(8,128)(2,1)} fusion(bf16[1024,2048]{1,0:T(8,128)(2,1)S(1)} %bitcast_dynamic-update-slice_fusion.24, bf16[1,768,2048]{2,1,0:T(8,128)(2,1)S(1)} %copy-done.53), kind=kOutput, calls=%fused_computation.68 | convolution fusion | flops 3222011904 | bytes 8912896 | tf_op jit(solution)/shard_map/td,fd->tf/dot_general | solution.py:230
  177.3 34.3 %all-gather.6.cloned.1.call-done = bf16[16,128,2048]{2,1,0:T(8,128)(2,1)} async-done(((bf16[1,128,2048]{2,1,0:T(8,128)(2,1)}), bf16[16,128,2048]{2,1,0:T(8,128)(2,1)}) %all-gather.6.cloned.1.call-update) | async-done | bytes 8388624 | tf_op jit(solution)/shard_map/all_gather | solution.py:216
  225.7 3.4 fusion.57
  242.3 3.5 multiply_convert_fusion.1
  245.8 3.7 convolution_convert_fusion
  276.0 7.7 %convolution_bitcast_fusion = f32[1,768,2048]{2,1,0:T(8,128)} fusion(bf16[1024,2048]{1,0:T(8,128)(2,1)} %copy-done.32, bf16[1024,768]{1,0:T(8,128)(2,1)S(1)} %copy-done.10, bf16[1024,768]{1,0:T(8,128)(2,1)S(1)} %copy-done.8), kind=kOutput, calls=%fused_computation.45 | convolution fusion | flops 3227516928 | bytes 13631488 | tf_op jit(solution)/shard_map/tf,td->fd/dot_general | solution.py:228
  283.7 75.9 %reduce-scatter.4.cloned.1.call-done = bf16[128,2048]{1,0:T(8,128)(2,1)} async-done(((bf16[2048,2048]{1,0:T(8,128)(2,1)}), bf16[128,2048]{1,0:T(8,128)(2,1)}) %reduce-scatter.4.cloned.1.call-update) | async-done | bytes 524304
  361.9 4.0 collective-permute-start.11
  367.0 4.9 %collective-permute-start.13 = (bf16[128,512]{1,0:T(8,128)(2,1)S(1)}, bf16[128,512]{1,0:T(8,128)(2,1)S(1)}, u32[]{:S(2)}, u32[]{:S(2)}) collective-permute-start(bf16[128,512]{1,0:T(8,128)(2,1)S(1)} %bitcast.361), channel_id=1, source_target_pairs={{6,0},{0,1},{2,2},{4,3},{7,4},{1,5},{3,6},{5,7},{14,8},{8,9},{10,1... | collective-permute-start | bytes 393224 | tf_op jit(solution)/shard_map/ppermute | solution.py:69
  371.9 8.9 %convolution_bitcast_fusion.1 = f32[1,2048,768]{2,1,0:T(8,128)} fusion(bf16[1024,2048]{1,0:T(8,128)(2,1)} %copy-done.31, bf16[1024,768]{1,0:T(8,128)(2,1)} %copy-done.11), kind=kOutput, calls=%fused_computation.46 | convolution fusion | flops 3221225472 | bytes 12058624 | tf_op jit(solution)/shard_map/td,tf->df/dot_general | solution.py:234
  387.9 4.3 fusion.8
  393.0 2.5 copy.227
  395.5 5.1 %fusion.2 = f32[8,64,512]{2,1,0:T(8,128)} fusion(f32[512,512]{1,0:T(8,128)} %copy-done.14, f32[8,512]{1,0:T(8,128)} %get-tuple-element.41, pred[512,512]{1,0:T(8,128)(4,1)S(1)} %copy-done.22, f32[512,8,64]{0,2,1:T(8,128)} %bitcast.330), kind=kOutput, calls=%fused_computation.9 | convolution fusion | flops 277872640 | bytes 3424256 | tf_op jit(solution)/shard_map/hts,thp->shp/dot_general | solution.py:269
  401.7 23.3 %all_gather.20 = bf16[16,8,1024]{2,1,0:T(8,128)(2,1)S(1)} all-gather(bf16[1,8,1024]{2,1,0:T(8,128)(2,1)S(1)} %convert_element_type.196), channel_id=1, replica_groups=mesh['seq'=16,'expert'=4,'mp'=2] {'seq'}, dimensions={0}, use_global_device_ids=true | all-gather | bytes 278528 | tf_op jit(solution)/shard_map/all_gather | solution.py:289
  426.0 4.2 fusion.94
  430.3 2.5 fusion.72
  441.2 3.1 copy.231
  444.3 4.0 add.348
  (279 shorter events, 142.9 us)
Async XLA Ops:
  7.2 218.5 %copy-start = (bf16[1,2048,768]{2,1,0:T(8,128)(2,1)S(1)}, bf16[1,2048,768]{2,1,0:T(8,128)(2,1)}, u32[]{:S(2)}) copy-start(bf16[1,2048,768]{2,1,0:T(8,128)(2,1)} %param.18) | copy-start | bytes 9437188
  7.2 103.7 %all-gather.4.cloned.1.call-start = ((), (), s32[]{:S(2)}) async-start(), calls=%async_computation.1 | async-start | bytes 8912896 | tf_op jit(solution)/shard_map/all_gather | solution.py:146
  8.2 22.9 %copy-start.34 = (s32[16,8]{1,0:T(8,128)}, s32[16,8]{1,0:T(8,128)S(1)}, u32[]{:S(2)}) copy-start(s32[16,8]{1,0:T(8,128)S(1)} %reshape.505) | copy-start | bytes 1540
  11.9 23.4 %copy-start.54 = (f32[8]{0:T(128)S(1)}, f32[8]{0:T(128)}, u32[]{:S(2)}) copy-start(f32[8]{0:T(128)} %param.15) | copy-start | bytes 100
  11.9 23.4 %copy-start.43 = (s32[1024]{0:T(1024)S(1)}, s32[1024]{0:T(1024)}, u32[]{:S(2)}) copy-start(s32[1024]{0:T(1024)} %param.16) | copy-start | bytes 12292
  11.9 11.3 %collective-permute-start.2 = (bf16[128,512]{1,0:T(8,128)(2,1)S(1)}, bf16[128,512]{1,0:T(8,128)(2,1)S(1)}, u32[]{:S(2)}, u32[]{:S(2)}) collective-permute-start(bf16[128,512]{1,0:T(8,128)(2,1)S(1)} %bitcast.346), channel_id=1, source_target_pairs={{0,4},{1,6},{2,0},{3,2},{4,5},{5,7},{6,1},{7,3},{8,12},{9,14},{10,... | collective-permute-start | bytes 393224 | tf_op jit(solution)/shard_map/ppermute | solution.py:53
  16.0 7.2 %collective-permute-start.3 = (bf16[128,512]{1,0:T(8,128)(2,1)S(1)}, bf16[128,512]{1,0:T(8,128)(2,1)S(1)}, u32[]{:S(2)}, u32[]{:S(2)}) collective-permute-start(bf16[128,512]{1,0:T(8,128)(2,1)S(1)} %bitcast.350), channel_id=1, source_target_pairs={{0,6},{1,0},{2,2},{3,4},{4,7},{5,1},{6,3},{7,5},{8,14},{9,8},{10,1... | collective-permute-start | bytes 393224 | tf_op jit(solution)/shard_map/ppermute | solution.py:53
  18.1 5.1 %collective-permute-start = (bf16[128,512]{1,0:T(8,128)(2,1)S(1)}, bf16[128,512]{1,0:T(8,128)(2,1)S(1)}, u32[]{:S(2)}, u32[]{:S(2)}) collective-permute-start(bf16[128,512]{1,0:T(8,128)(2,1)S(1)} %bitcast.352), channel_id=1, source_target_pairs={{0,0},{1,2},{2,4},{3,6},{4,1},{5,3},{6,5},{7,7},{8,8},{9,10},{10,1... | collective-permute-start | bytes 393224 | tf_op jit(solution)/shard_map/ppermute | solution.py:53
  18.8 7.0 %collective-permute-start.1 = (bf16[128,512]{1,0:T(8,128)(2,1)S(1)}, bf16[128,512]{1,0:T(8,128)(2,1)S(1)}, u32[]{:S(2)}, u32[]{:S(2)}) collective-permute-start(bf16[128,512]{1,0:T(8,128)(2,1)S(1)} %bitcast.355), channel_id=1, source_target_pairs={{0,2},{1,4},{2,6},{3,0},{4,3},{5,5},{6,7},{7,1},{8,10},{9,12},{10,... | collective-permute-start | bytes 393224 | tf_op jit(solution)/shard_map/ppermute | solution.py:53
  23.2 12.2 %copy-start.49 = (pred[4]{0:T(512)(128)(4,1)}, pred[4]{0:T(512)(128)(4,1)S(1)}, u32[]{:S(2)}) copy-start(pred[4]{0:T(512)(128)(4,1)S(1)} %compare_and_fusion) | copy-start | bytes 16
  23.2 12.1 %copy-start.42 = (s32[1024]{0:T(1024)}, s32[1024]{0:T(1024)S(1)}, u32[]{:S(2)}) copy-start(s32[1024]{0:T(1024)S(1)} %pad_clamp_fusion) | copy-start | bytes 12292
  35.2 9.4 %copy-start.17 = (bf16[1024,16]{0,1:T(8,128)(2,1)S(1)}, bf16[1024,16]{0,1:T(8,128)(2,1)}, u32[]{:S(2)}) copy-start(bf16[1024,16]{0,1:T(8,128)(2,1)} %param.13) | copy-start | bytes 98308
  35.2 176.5 %all-gather.6.cloned.1.call-start = ((), (), s32[]{:S(2)}) async-start(), calls=%async_computation.2 | async-start | bytes 8912896 | tf_op jit(solution)/shard_map/all_gather | solution.py:216
  45.4 41.9 %copy-start.16 = (bf16[1024,16]{0,1:T(8,128)(2,1)S(1)}, bf16[1024,16]{0,1:T(8,128)(2,1)}, u32[]{:S(2)}) copy-start(bf16[1024,16]{0,1:T(8,128)(2,1)} %param.14) | copy-start | bytes 98308
  85.8 12.5 %copy-start.21 = (pred[512,512]{1,0:T(8,128)(4,1)}, pred[512,512]{1,0:T(8,128)(4,1)S(1)}, u32[]{:S(2)}) copy-start(pred[512,512]{1,0:T(8,128)(4,1)S(1)} %iota_compare_fusion) | copy-start | bytes 786436
  87.7 10.7 %copy-start.12 = (f32[512,512]{1,0:T(8,128)}, f32[512,512]{1,0:T(8,128)S(1)}, u32[]{:S(2)}) copy-start(f32[512,512]{1,0:T(8,128)S(1)} %fusion.129) | copy-start | bytes 3145732
  110.6 24.3 %copy-start.50 = (pred[4]{0:T(512)(128)(4,1)S(1)}, pred[4]{0:T(512)(128)(4,1)}, u32[]{:S(2)}) copy-start(pred[4]{0:T(512)(128)(4,1)} %copy-done.49) | copy-start | bytes 16
  113.9 27.0 %copy-start.35 = (s32[16,8]{1,0:T(8,128)S(1)}, s32[16,8]{1,0:T(8,128)}, u32[]{:S(2)}) copy-start(s32[16,8]{1,0:T(8,128)} %copy-done.34) | copy-start | bytes 1540
  114.0 15.0 %collective-permute-start.5 = (bf16[128,512]{1,0:T(8,128)(2,1)S(1)}, bf16[128,512]{1,0:T(8,128)(2,1)S(1)}, u32[]{:S(2)}, u32[]{:S(2)}) collective-permute-start(bf16[128,512]{1,0:T(8,128)(2,1)S(1)} %bitcast.353), channel_id=1, source_target_pairs={{0,0},{1,2},{2,4},{3,6},{4,1},{5,3},{6,5},{7,7},{8,8},{9,10},{10,1... | collective-permute-start | bytes 393224 | tf_op jit(solution)/shard_map/ppermute | solution.py:53
  114.7 14.3 %collective-permute-start.6 = (bf16[128,512]{1,0:T(8,128)(2,1)S(1)}, bf16[128,512]{1,0:T(8,128)(2,1)S(1)}, u32[]{:S(2)}, u32[]{:S(2)}) collective-permute-start(bf16[128,512]{1,0:T(8,128)(2,1)S(1)} %bitcast.354), channel_id=1, source_target_pairs={{0,2},{1,4},{2,6},{3,0},{4,3},{5,5},{6,7},{7,1},{8,10},{9,12},{10,... | collective-permute-start | bytes 393224 | tf_op jit(solution)/shard_map/ppermute | solution.py:53
  123.6 6.7 %collective-permute-start.7 = (bf16[128,512]{1,0:T(8,128)(2,1)S(1)}, bf16[128,512]{1,0:T(8,128)(2,1)S(1)}, u32[]{:S(2)}, u32[]{:S(2)}) collective-permute-start(bf16[128,512]{1,0:T(8,128)(2,1)S(1)} %bitcast.356), channel_id=1, source_target_pairs={{0,4},{1,6},{2,0},{3,2},{4,5},{5,7},{6,1},{7,3},{8,12},{9,14},{10,... | collective-permute-start | bytes 393224 | tf_op jit(solution)/shard_map/ppermute | solution.py:53
  127.0 4.4 collective-permute-start.8
  140.9 218.7 %reduce-scatter.4.cloned.1.call-start = ((), (), s32[]{:S(2)}) async-start(), calls=%async_computation.3 | async-start | bytes 8912896
  158.1 14.4 %copy-start.53 = (bf16[1,768,2048]{2,1,0:T(8,128)(2,1)S(1)}, bf16[1,768,2048]{2,1,0:T(8,128)(2,1)}, u32[]{:S(2)}) copy-start(bf16[1,768,2048]{2,1,0:T(8,128)(2,1)} %param.19) | copy-start | bytes 9437188
  177.1 64.0 %collective-permute-start.4 = (bf16[1024,768]{1,0:T(8,128)(2,1)}, bf16[1024,768]{1,0:T(8,128)(2,1)}, u32[]{:S(2)}, u32[]{:S(2)}) collective-permute-start(bf16[1024,768]{1,0:T(8,128)(2,1)} %fusion.54), channel_id=1, source_target_pairs={{0,1},{1,0},{2,3},{3,2},{4,5},{5,4},{6,7},{7,6},{8,9},{9,8},{10,11... | collective-permute-start | bytes 4718600 | tf_op jit(solution)/shard_map/ppermute | solution.py:36
  229.1 12.0 %copy-start.7 = (bf16[1024,768]{1,0:T(8,128)(2,1)}, bf16[1024,768]{1,0:T(8,128)(2,1)S(1)}, u32[]{:S(2)}) copy-start(bf16[1024,768]{1,0:T(8,128)(2,1)S(1)} %fusion.57) | copy-start | bytes 4718596
  229.1 12.0 %collective-permute-start.9 = (bf16[1024,768]{1,0:T(8,128)(2,1)S(1)}, bf16[1024,768]{1,0:T(8,128)(2,1)S(1)}, u32[]{:S(2)}, u32[]{:S(2)}) collective-permute-start(bf16[1024,768]{1,0:T(8,128)(2,1)S(1)} %fusion.57), channel_id=1, source_target_pairs={{0,1},{1,0},{2,3},{3,2},{4,5},{5,4},{6,7},{7,6},{8,9},{9,8},{10,11... | collective-permute-start | bytes 4718600 | tf_op jit(solution)/shard_map/ppermute | solution.py:36
  361.1 19.7 %collective-permute-start.10 = (bf16[128,512]{1,0:T(8,128)(2,1)S(1)}, bf16[128,512]{1,0:T(8,128)(2,1)S(1)}, u32[]{:S(2)}, u32[]{:S(2)}) collective-permute-start(bf16[128,512]{1,0:T(8,128)(2,1)S(1)} %bitcast.358), channel_id=1, source_target_pairs={{0,0},{2,1},{4,2},{6,3},{1,4},{3,5},{5,6},{7,7},{8,8},{10,9},{12,1... | collective-permute-start | bytes 393224 | tf_op jit(solution)/shard_map/ppermute | solution.py:69
  361.9 19.1 %collective-permute-start.11 = (bf16[128,512]{1,0:T(8,128)(2,1)S(1)}, bf16[128,512]{1,0:T(8,128)(2,1)S(1)}, u32[]{:S(2)}, u32[]{:S(2)}) collective-permute-start(bf16[128,512]{1,0:T(8,128)(2,1)S(1)} %bitcast.359), channel_id=1, source_target_pairs={{2,0},{4,1},{6,2},{0,3},{3,4},{5,5},{7,6},{1,7},{10,8},{12,9},{14,... | collective-permute-start | bytes 393224 | tf_op jit(solution)/shard_map/ppermute | solution.py:69
  366.0 15.2 %collective-permute-start.12 = (bf16[128,512]{1,0:T(8,128)(2,1)S(1)}, bf16[128,512]{1,0:T(8,128)(2,1)S(1)}, u32[]{:S(2)}, u32[]{:S(2)}) collective-permute-start(bf16[128,512]{1,0:T(8,128)(2,1)S(1)} %bitcast.360), channel_id=1, source_target_pairs={{4,0},{6,1},{0,2},{2,3},{5,4},{7,5},{1,6},{3,7},{12,8},{14,9},{8,1... | collective-permute-start | bytes 393224 | tf_op jit(solution)/shard_map/ppermute | solution.py:69
  367.0 14.5 %collective-permute-start.13 = (bf16[128,512]{1,0:T(8,128)(2,1)S(1)}, bf16[128,512]{1,0:T(8,128)(2,1)S(1)}, u32[]{:S(2)}, u32[]{:S(2)}) collective-permute-start(bf16[128,512]{1,0:T(8,128)(2,1)S(1)} %bitcast.361), channel_id=1, source_target_pairs={{6,0},{0,1},{2,2},{4,3},{7,4},{1,5},{3,6},{5,7},{14,8},{8,9},{10,1... | collective-permute-start | bytes 393224 | tf_op jit(solution)/shard_map/ppermute | solution.py:69
  384.7 15.9 %copy-start.2 = (f32[1024,512]{1,0:T(8,128)}, f32[1024,512]{1,0:T(8,128)S(1)}, u32[]{:S(2)}) copy-start(f32[1024,512]{1,0:T(8,128)S(1)} %bitcast_add_fusion) | copy-start | bytes 6291460
  (41 other events, 144.6 us)
Sparse Core Ops, SparseCore 0:
  35.3 75.5 all-gather.3
  141.0 70.5 all-gather.5
  274.3 85.3 reduce-scatter.3

commit v4 on v3

--- a/solution.py
+++ b/solution.py
@@ -97,8 +97,8 @@
     return jnp.concatenate(rows_out, axis=0).astype(jnp.bfloat16)
 
 
-def spread(present, slot_of, rows, half_width):
-    blocks = rows.reshape(-1, BLOCK, half_width)
+def spread(present, slot_of, rows, half_width, block_rows):
+    blocks = rows.reshape(-1, block_rows, half_width)
     placed = [
         jnp.where(
             present[shard],
@@ -213,33 +213,40 @@
         preferred_element_type=jnp.float32,
     ).astype(jnp.bfloat16)
     h_block = dispatch(h_pick, exp_index, exp_count, mp_count, my_slice)
-    h_all = lax.all_gather(h_block, "seq", axis=0)
+    chunks = 2
+    chunk_rows = BLOCK // chunks
+    h_parts = [
+        lax.all_gather(h_block[c * chunk_rows : (c + 1) * chunk_rows], "seq", axis=0)
+        for c in range(chunks)
+    ]
     present = jnp.any(route_table == exp_index, axis=1)
     slot_of = jnp.cumsum(present.astype(jnp.int32)) - 1
     select = ((slot_of[None, :] == jnp.arange(slot_total)[:, None]) & present[None, :]).astype(
         jnp.bfloat16
     )
-    x_rows = compact(select, h_all, half_width)
-    g_rows = compact(select, g_all, half_width)
     up_local = expert_up_weight[0]
     down_local = expert_down_weight[0]
-    pre_act = mp_sum(jnp.dot(x_rows, up_local, preferred_element_type=jnp.float32))
-    activation = jax.nn.silu(pre_act).astype(jnp.bfloat16)
-    down_grad = jnp.einsum("tf,td->fd", activation, g_rows, preferred_element_type=jnp.float32)
-    act_grad = mp_sum(
-        jnp.einsum("td,fd->tf", g_rows, down_local, preferred_element_type=jnp.float32)
-    )
-    sigmoid_pre = jax.nn.sigmoid(pre_act)
-    pre_grad = (act_grad * sigmoid_pre * (1.0 + pre_act * (1.0 - sigmoid_pre))).astype(jnp.bfloat16)
-    up_grad = jnp.einsum("td,tf->df", x_rows, pre_grad, preferred_element_type=jnp.float32)
-    row_grad = jnp.einsum("tf,df->td", pre_grad, up_local, preferred_element_type=jnp.float32)
-    spread_rows = spread(present, slot_of, row_grad.astype(jnp.bfloat16), half_width)
-    back_rows = lax.psum_scatter(
-        spread_rows,
-        "seq",
-        scatter_dimension=0,
-        tiled=True,
-    )
+    back_parts = []
+    for c in range(chunks):
+        x_rows = compact(select, h_parts[c], half_width)
+        g_rows = compact(select, g_all[:, c * chunk_rows : (c + 1) * chunk_rows], half_width)
+        pre_act = mp_sum(jnp.dot(x_rows, up_local, preferred_element_type=jnp.float32))
+        activation = jax.nn.silu(pre_act).astype(jnp.bfloat16)
+        down_part = jnp.einsum("tf,td->fd", activation, g_rows, preferred_element_type=jnp.float32)
+        act_grad = mp_sum(
+            jnp.einsum("td,fd->tf", g_rows, down_local, preferred_element_type=jnp.float32)
+        )
+        sigmoid_pre = jax.nn.sigmoid(pre_act)
+        pre_grad = (act_grad * sigmoid_pre * (1.0 + pre_act * (1.0 - sigmoid_pre))).astype(
+            jnp.bfloat16
+        )
+        up_part = jnp.einsum("td,tf->df", x_rows, pre_grad, preferred_element_type=jnp.float32)
+        down_grad = down_part if c == 0 else down_grad + down_part
+        up_grad = up_part if c == 0 else up_grad + up_part
+        row_grad = jnp.einsum("tf,df->td", pre_grad, up_local, preferred_element_type=jnp.float32)
+        spread_rows = spread(present, slot_of, row_grad.astype(jnp.bfloat16), half_width, chunk_rows)
+        back_parts.append(lax.psum_scatter(spread_rows, "seq", scatter_dimension=0, tiled=True))
+    back_rows = jnp.concatenate(back_parts, axis=0)
     returned = give_back(back_rows, exp_index, exp_count, mp_count)
     position = my_slice % exp_count
     chosen_by_shift = jnp.take(chosen, (position + jnp.arange(exp_count)) % exp_count, axis=0)

time: 463 us -> 506 us (1.093)
  other arithmetic: 82.7 us -> 121 us
  local copies, waits for them, and re-layouts: 52.4 us -> 62.9 us
  waiting for transfers between devices: 116 us -> 108 us
    unnamed x30 -> x59, other arithmetic: 48.1 us -> 81.6 us
    all_gather x1 -> x2, waiting for transfers between devices: 34.3 us -> 2.69 us  [per_device(): lax.all_gather(h_block[c * chunk_rows:(c + 1) * chunk_rows], 'seq', axis=0)]
    unnamed x4 -> x7, waiting for transfers between devices: 75.9 us -> 97 us
    unnamed x126 -> x153, local copies, waits for them, and re-layouts: 5.75 us -> 12.5 us
    slice x1 -> x5, local copies, waits for them, and re-layouts: 0.16 us -> 5.33 us  [the longest x1 4.01 us: per_device(): g_all[:, c * chunk_rows:(c + 1) * chunk_rows]]
    dot_general x1 -> x2, matrix products: 8.9 us -> 11.9 us  [per_device(): jnp.einsum('td,tf->df', x_rows, pre_grad, preferred_element_type=jnp.floa...]
  transfers between devices with their start and end apart: 17 -> 21, of which waited for: 6 -> 8; matrix products, arithmetic and copies ran while one was open for 24% -> 38% of each run, Pallas kernels for 0% -> 0%
where the time goes in v4:
time: 506 us; the launch traced here: 497 us
  other arithmetic  121 us (24%)
  waiting for transfers between devices  108 us (21%)
  matrix products  80.7 us (16%)
  local copies, waits for them, and re-layouts  62.9 us (12%)
  blocking collectives  49 us (10%)
  between operations  40.2 us (8%)
  starting transfers between devices  35.5 us (7%)
    unnamed x7, waiting for transfers between devices  97 us
    unnamed x59, other arithmetic  81.6 us
    all_gather x1, blocking collectives, per_device(): lax.all_gather(jnp.concatenate([flat_state, level_lanes], axis=1), 'seq')  25.9 us
    all_gather x1, blocking collectives, per_device(): adjoint_all = lax.all_gather(flat_adjoint.astype(jnp.bfloat16), 'seq')  23 us
    ppermute x8, starting transfers between devices, dispatch(): received.append(lax.ppermute(send, ('expert', 'mp'), pairs))  21.5 us
    unnamed x153, local copies, waits for them, and re-layouts  12.5 us
    dot_general x2, matrix products, per_device(): jnp.einsum('td,tf->df', x_rows, pre_grad, preferred_element_type=jnp.floa...  11.9 us
  transfers between devices with their start and end apart: 21, of which 8 were waited for; matrix products, arithmetic and copies ran while one was open for 38% of the time, Pallas kernels for 0%

profile of v4, /device:TPU:0, one launch (start us, length us, event | category | flops | bytes accessed | tf_op | source)
XLA Modules:
  0.0 497.4 jit_solution(1383945368686858481)
XLA Ops:
  8.7 2.8 convolution_convert_fusion.1
  11.5 3.3 constant_dynamic-slice_fusion.11
  14.8 6.1 %collective-permute-start.3 = (bf16[128,512]{1,0:T(8,128)(2,1)S(1)}, bf16[128,512]{1,0:T(8,128)(2,1)S(1)}, u32[]{:S(2)}, u32[]{:S(2)}) collective-permute-start(bf16[128,512]{1,0:T(8,128)(2,1)S(1)} %bitcast.446), channel_id=1, source_target_pairs={{0,6},{1,0},{2,2},{3,4},{4,7},{5,1},{6,3},{7,5},{8,14},{9,8},{10,1... | collective-permute-start | bytes 393224 | tf_op jit(solution)/shard_map/ppermute | solution.py:53
  21.9 3.0 collective-permute-start.1
  26.0 3.3 collective-permute-done.1
  59.8 25.9 %all-gather = f32[128,1152]{1,0:T(8,128)S(1)} all-gather(f32[8,1152]{1,0:T(8,128)S(1)} %pad_maximum_fusion.3), channel_id=2, replica_groups=mesh['seq'=16,'expert'=4,'mp'=2] {'seq'}, dimensions={0}, use_global_device_ids=true | all-gather | bytes 626688 | tf_op jit(solution)/shard_map/all_gather | solution.py:197
  92.4 4.3 fusion.45
  96.8 2.7 fusion.109
  100.0 2.7 fusion.47
  102.8 2.7 fusion.97
  106.1 2.6 maximum_add_fusion
  108.7 2.9 copy.235
  111.6 3.2 add_convert_fusion
  117.9 6.1 %collective-permute-start.8 = (bf16[128,512]{1,0:T(8,128)(2,1)S(1)}, bf16[128,512]{1,0:T(8,128)(2,1)S(1)}, u32[]{:S(2)}, u32[]{:S(2)}) collective-permute-start(bf16[128,512]{1,0:T(8,128)(2,1)S(1)} %bitcast.453), channel_id=1, source_target_pairs={{0,6},{1,0},{2,2},{3,4},{4,7},{5,1},{6,3},{7,5},{8,14},{9,8},{10,1... | collective-permute-start | bytes 393224 | tf_op jit(solution)/shard_map/ppermute | solution.py:53
  124.1 3.9 collective-permute-start.6
  165.9 4.0 fusion.205
  177.1 2.7 fusion.70
  179.8 3.0 collective-permute-start.10
  187.4 2.7 all-gather.9.cloned.1.call-done
  243.8 5.2 %fusion.67 = bf16[512,768]{1,0:T(8,128)(2,1)} fusion(bf16[512,2048]{1,0:T(8,128)(2,1)} %bitcast_dynamic-update-slice_fusion.56, bf16[1,768,2048]{2,1,0:T(8,128)(2,1)} %param.19), kind=kOutput, calls=%fused_computation.80 | convolution fusion | flops 1611005952 | bytes 6029312 | tf_op jit(solution)/shard_map/td,fd->tf/dot_general | solution.py:237
  295.3 4.5 fusion.214
  301.9 4.6 add_bitcast_fusion
  306.5 18.0 %reduce-scatter.9.cloned.1.call-done = bf16[64,2048]{1,0:T(8,128)(2,1)} async-done(((bf16[1024,2048]{1,0:T(8,128)(2,1)}), bf16[64,2048]{1,0:T(8,128)(2,1)}) %reduce-scatter.9.cloned.1.call-update) | async-done | bytes 262160
  326.5 78.9 %reduce-scatter.7.cloned.1.call-done = bf16[64,2048]{1,0:T(8,128)(2,1)} async-done(((bf16[1024,2048]{1,0:T(8,128)(2,1)}), bf16[64,2048]{1,0:T(8,128)(2,1)}) %reduce-scatter.7.cloned.1.call-update) | async-done | bytes 262160
  414.3 4.7 collective-permute-start.13
  421.6 7.3 %add_bitcast_fusion.1 = f32[1,2048,768]{2,1,0:T(8,128)} fusion(f32[2048,768]{1,0:T(8,128)} %fusion.214, bf16[512,2048]{1,0:T(8,128)(2,1)S(1)} %copy-done.5, bf16[512,768]{1,0:T(8,128)(2,1)S(1)} %copy-done.12), kind=kOutput, calls=%fused_computation.10 | convolution fusion | flops 1612185600 | bytes 15466496 | tf_op jit(solution)/shard_map/td,tf->df/dot_general | solution.py:243
  436.0 3.4 fusion.8
  441.5 2.7 fusion.88
  446.4 3.7 fusion.2
  457.6 23.0 %all_gather.32 = bf16[16,8,1024]{2,1,0:T(8,128)(2,1)S(1)} all-gather(bf16[1,8,1024]{2,1,0:T(8,128)(2,1)S(1)} %convert_element_type.263), channel_id=1, replica_groups=mesh['seq'=16,'expert'=4,'mp'=2] {'seq'}, dimensions={0}, use_global_device_ids=true | all-gather | bytes 278528 | tf_op jit(solution)/shard_map/all_gather | solution.py:296
  483.4 3.1 copy.254
  486.4 4.0 add.405
  (359 shorter events, 206.1 us)
Async XLA Ops:
  7.2 195.8 %copy-start = (bf16[1,2048,768]{2,1,0:T(8,128)(2,1)S(1)}, bf16[1,2048,768]{2,1,0:T(8,128)(2,1)}, u32[]{:S(2)}) copy-start(bf16[1,2048,768]{2,1,0:T(8,128)(2,1)} %param.18) | copy-start | bytes 9437188
  7.2 107.6 %all-gather.5.cloned.1.call-start = ((), (), s32[]{:S(2)}) async-start(), calls=%async_computation.2 | async-start | bytes 8912896 | tf_op jit(solution)/shard_map/all_gather | solution.py:146
  8.2 22.0 %copy-start.49 = (s32[16,8]{1,0:T(8,128)}, s32[16,8]{1,0:T(8,128)S(1)}, u32[]{:S(2)}) copy-start(s32[16,8]{1,0:T(8,128)S(1)} %reshape.609) | copy-start | bytes 1540
  14.8 10.9 %collective-permute-start.3 = (bf16[128,512]{1,0:T(8,128)(2,1)S(1)}, bf16[128,512]{1,0:T(8,128)(2,1)S(1)}, u32[]{:S(2)}, u32[]{:S(2)}) collective-permute-start(bf16[128,512]{1,0:T(8,128)(2,1)S(1)} %bitcast.446), channel_id=1, source_target_pairs={{0,6},{1,0},{2,2},{3,4},{4,7},{5,1},{6,3},{7,5},{8,14},{9,8},{10,1... | collective-permute-start | bytes 393224 | tf_op jit(solution)/shard_map/ppermute | solution.py:53
  20.9 5.0 %collective-permute-start.2 = (bf16[128,512]{1,0:T(8,128)(2,1)S(1)}, bf16[128,512]{1,0:T(8,128)(2,1)S(1)}, u32[]{:S(2)}, u32[]{:S(2)}) collective-permute-start(bf16[128,512]{1,0:T(8,128)(2,1)S(1)} %bitcast.451), channel_id=1, source_target_pairs={{0,4},{1,6},{2,0},{3,2},{4,5},{5,7},{6,1},{7,3},{8,12},{9,14},{10,... | collective-permute-start | bytes 393224 | tf_op jit(solution)/shard_map/ppermute | solution.py:53
  21.9 7.4 %collective-permute-start.1 = (bf16[128,512]{1,0:T(8,128)(2,1)S(1)}, bf16[128,512]{1,0:T(8,128)(2,1)S(1)}, u32[]{:S(2)}, u32[]{:S(2)}) collective-permute-start(bf16[128,512]{1,0:T(8,128)(2,1)S(1)} %bitcast.452), channel_id=1, source_target_pairs={{0,2},{1,4},{2,6},{3,0},{4,3},{5,5},{6,7},{7,1},{8,10},{9,12},{10,... | collective-permute-start | bytes 393224 | tf_op jit(solution)/shard_map/ppermute | solution.py:53
  25.0 4.3 collective-permute-start
  25.7 15.6 %copy-start.63 = (pred[4]{0:T(512)(128)(4,1)}, pred[4]{0:T(512)(128)(4,1)S(1)}, u32[]{:S(2)}) copy-start(pred[4]{0:T(512)(128)(4,1)S(1)} %compare_and_fusion) | copy-start | bytes 16
  25.7 15.6 %copy-start.56 = (s32[1024]{0:T(1024)}, s32[1024]{0:T(1024)S(1)}, u32[]{:S(2)}) copy-start(s32[1024]{0:T(1024)S(1)} %pad_clamp_fusion) | copy-start | bytes 12292
  38.6 151.4 %all-gather.9.cloned.1.call-start = ((), (), s32[]{:S(2)}) async-start(), calls=%async_computation.4 | async-start | bytes 4456448 | tf_op jit(solution)/shard_map/all_gather | solution.py:219
  54.3 37.4 %copy-start.29 = (bf16[1024,16]{0,1:T(8,128)(2,1)S(1)}, bf16[1024,16]{0,1:T(8,128)(2,1)}, u32[]{:S(2)}) copy-start(bf16[1024,16]{0,1:T(8,128)(2,1)} %param.14) | copy-start | bytes 98308
  116.8 18.0 %copy-start.64 = (pred[4]{0:T(512)(128)(4,1)S(1)}, pred[4]{0:T(512)(128)(4,1)}, u32[]{:S(2)}) copy-start(pred[4]{0:T(512)(128)(4,1)} %copy-done.63) | copy-start | bytes 16
  117.9 10.9 %collective-permute-start.8 = (bf16[128,512]{1,0:T(8,128)(2,1)S(1)}, bf16[128,512]{1,0:T(8,128)(2,1)S(1)}, u32[]{:S(2)}, u32[]{:S(2)}) collective-permute-start(bf16[128,512]{1,0:T(8,128)(2,1)S(1)} %bitcast.453), channel_id=1, source_target_pairs={{0,6},{1,0},{2,2},{3,4},{4,7},{5,1},{6,3},{7,5},{8,14},{9,8},{10,1... | collective-permute-start | bytes 393224 | tf_op jit(solution)/shard_map/ppermute | solution.py:53
  124.0 5.1 %collective-permute-start.7 = (bf16[128,512]{1,0:T(8,128)(2,1)S(1)}, bf16[128,512]{1,0:T(8,128)(2,1)S(1)}, u32[]{:S(2)}, u32[]{:S(2)}) collective-permute-start(bf16[128,512]{1,0:T(8,128)(2,1)S(1)} %bitcast.454), channel_id=1, source_target_pairs={{0,4},{1,6},{2,0},{3,2},{4,5},{5,7},{6,1},{7,3},{8,12},{9,14},{10,... | collective-permute-start | bytes 393224 | tf_op jit(solution)/shard_map/ppermute | solution.py:53
  124.1 7.2 %collective-permute-start.6 = (bf16[128,512]{1,0:T(8,128)(2,1)S(1)}, bf16[128,512]{1,0:T(8,128)(2,1)S(1)}, u32[]{:S(2)}, u32[]{:S(2)}) collective-permute-start(bf16[128,512]{1,0:T(8,128)(2,1)S(1)} %bitcast.456), channel_id=1, source_target_pairs={{0,2},{1,4},{2,6},{3,0},{4,3},{5,5},{6,7},{7,1},{8,10},{9,12},{10,... | collective-permute-start | bytes 393224 | tf_op jit(solution)/shard_map/ppermute | solution.py:53
  128.1 3.3 collective-permute-start.5
  137.8 111.8 %all-gather.7.cloned.1.call-start = ((), (), s32[]{:S(2)}) async-start(), calls=%async_computation.3 | async-start | bytes 4456448 | tf_op jit(solution)/shard_map/all_gather | solution.py:219
  179.8 34.8 %collective-permute-start.10 = (bf16[512,768]{1,0:T(8,128)(2,1)}, bf16[512,768]{1,0:T(8,128)(2,1)}, u32[]{:S(2)}, u32[]{:S(2)}) collective-permute-start(bf16[512,768]{1,0:T(8,128)(2,1)} %fusion.70), channel_id=1, source_target_pairs={{0,1},{1,0},{2,3},{3,2},{4,5},{5,4},{6,7},{7,6},{8,9},{9,8},{10,11... | collective-permute-start | bytes 2359304 | tf_op jit(solution)/shard_map/ppermute | solution.py:36
  187.3 137.2 %reduce-scatter.9.cloned.1.call-start = ((), (), s32[]{:S(2)}) async-start(), calls=%async_computation.6 | async-start | bytes 4456448
  204.8 9.8 %collective-permute-start.11 = (bf16[512,768]{1,0:T(8,128)(2,1)S(1)}, bf16[512,768]{1,0:T(8,128)(2,1)S(1)}, u32[]{:S(2)}, u32[]{:S(2)}) collective-permute-start(bf16[512,768]{1,0:T(8,128)(2,1)S(1)} %fusion.76), channel_id=1, source_target_pairs={{0,1},{1,0},{2,3},{3,2},{4,5},{5,4},{6,7},{7,6},{8,9},{9,8},{10,11... | collective-permute-start | bytes 2359304 | tf_op jit(solution)/shard_map/ppermute | solution.py:36
  241.5 164.0 %reduce-scatter.7.cloned.1.call-start = ((), (), s32[]{:S(2)}) async-start(), calls=%async_computation.5 | async-start | bytes 4456448
  249.0 15.5 %collective-permute-start.4 = (bf16[512,768]{1,0:T(8,128)(2,1)}, bf16[512,768]{1,0:T(8,128)(2,1)}, u32[]{:S(2)}, u32[]{:S(2)}) collective-permute-start(bf16[512,768]{1,0:T(8,128)(2,1)} %fusion.67), channel_id=1, source_target_pairs={{0,1},{1,0},{2,3},{3,2},{4,5},{5,4},{6,7},{7,6},{8,9},{9,8},{10,11... | collective-permute-start | bytes 2359304 | tf_op jit(solution)/shard_map/ppermute | solution.py:36
  264.3 2.5 collective-permute-start.9
  306.5 115.0 %copy-start.5 = (bf16[512,2048]{1,0:T(8,128)(2,1)S(1)}, bf16[512,2048]{1,0:T(8,128)(2,1)}, u32[]{:S(2)}) copy-start(bf16[512,2048]{1,0:T(8,128)(2,1)} %copy-done.4) | copy-start | bytes 6291460
  306.5 115.0 %copy-start.12 = (bf16[512,768]{1,0:T(8,128)(2,1)S(1)}, bf16[512,768]{1,0:T(8,128)(2,1)}, u32[]{:S(2)}) copy-start(bf16[512,768]{1,0:T(8,128)(2,1)} %copy-done.11) | copy-start | bytes 2359300
  409.7 19.2 %collective-permute-start.15 = (bf16[128,512]{1,0:T(8,128)(2,1)}, bf16[128,512]{1,0:T(8,128)(2,1)S(1)}, u32[]{:S(2)}, u32[]{:S(2)}) collective-permute-start(bf16[128,512]{1,0:T(8,128)(2,1)} %bitcast.458), channel_id=1, source_target_pairs={{6,0},{0,1},{2,2},{4,3},{7,4},{1,5},{3,6},{5,7},{14,8},{8,9},{10,1... | collective-permute-start | bytes 393224 | tf_op jit(solution)/shard_map/ppermute | solution.py:69
  412.4 16.7 %collective-permute-start.14 = (bf16[128,512]{1,0:T(8,128)(2,1)}, bf16[128,512]{1,0:T(8,128)(2,1)S(1)}, u32[]{:S(2)}, u32[]{:S(2)}) collective-permute-start(bf16[128,512]{1,0:T(8,128)(2,1)} %bitcast.459), channel_id=1, source_target_pairs={{4,0},{6,1},{0,2},{2,3},{5,4},{7,5},{1,6},{3,7},{12,8},{14,9},{8,1... | collective-permute-start | bytes 393224 | tf_op jit(solution)/shard_map/ppermute | solution.py:69
  414.3 15.0 %collective-permute-start.13 = (bf16[128,512]{1,0:T(8,128)(2,1)}, bf16[128,512]{1,0:T(8,128)(2,1)S(1)}, u32[]{:S(2)}, u32[]{:S(2)}) collective-permute-start(bf16[128,512]{1,0:T(8,128)(2,1)} %bitcast.460), channel_id=1, source_target_pairs={{2,0},{4,1},{6,2},{0,3},{3,4},{5,5},{7,6},{1,7},{10,8},{12,9},{14,... | collective-permute-start | bytes 393224 | tf_op jit(solution)/shard_map/ppermute | solution.py:69
  419.8 9.8 %collective-permute-start.12 = (bf16[128,512]{1,0:T(8,128)(2,1)}, bf16[128,512]{1,0:T(8,128)(2,1)S(1)}, u32[]{:S(2)}, u32[]{:S(2)}) collective-permute-start(bf16[128,512]{1,0:T(8,128)(2,1)} %bitcast.461), channel_id=1, source_target_pairs={{0,0},{2,1},{4,2},{6,3},{1,4},{3,5},{5,6},{7,7},{8,8},{10,9},{12,1... | collective-permute-start | bytes 393224 | tf_op jit(solution)/shard_map/ppermute | solution.py:69
  455.0 25.7 %copy-start.44 = (f32[16,8]{1,0:T(8,128)S(1)}, f32[16,8]{1,0:T(8,128)}, u32[]{:S(2)}) copy-start(f32[16,8]{1,0:T(8,128)} %exponential_select_fusion) | copy-start | bytes 1540
  455.0 25.9 %copy-start.42 = (f32[1024,8]{0,1:T(8,128)S(1)}, f32[1024,8]{0,1:T(8,128)}, u32[]{:S(2)}) copy-start(f32[1024,8]{0,1:T(8,128)} %get-tuple-element.38) | copy-start | bytes 98308
  455.0 25.9 %copy-start.60 = (f32[8]{0:T(128)S(1)}, f32[8]{0:T(128)}, u32[]{:S(2)}) copy-start(f32[8]{0:T(128)} %copy-done.58) | copy-start | bytes 100
  (58 other events, 257.5 us)
Sparse Core Ops, SparseCore 0:
  38.7 75.0 all-gather.4
  137.9 52.1 all-gather.8
  192.2 50.9 all-gather.6
  246.4 78.0 reduce-scatter.8
  327.7 77.6 reduce-scatter.6

commit v5 on v3

--- a/solution.py
+++ b/solution.py
@@ -90,24 +90,15 @@
     blocks = gathered.reshape(select.shape[1], -1, half_width)
     used = jnp.any(select > 0, axis=1)
     source = jnp.argmax(select, axis=1)
-    rows_out = [
-        jnp.where(used[slot], lax.dynamic_index_in_dim(blocks, source[slot], 0, keepdims=False), 0)
-        for slot in range(select.shape[0])
-    ]
-    return jnp.concatenate(rows_out, axis=0).astype(jnp.bfloat16)
+    rows_out = jnp.where(used[:, None, None], jnp.take(blocks, source, axis=0, mode="clip"), 0)
+    return rows_out.reshape(-1, half_width).astype(jnp.bfloat16)
 
 
 def spread(present, slot_of, rows, half_width):
     blocks = rows.reshape(-1, BLOCK, half_width)
-    placed = [
-        jnp.where(
-            present[shard],
-            lax.dynamic_index_in_dim(blocks, jnp.maximum(slot_of[shard], 0), 0, keepdims=False),
-            0,
-        )
-        for shard in range(present.shape[0])
-    ]
-    return jnp.concatenate(placed, axis=0).astype(jnp.bfloat16)
+    placed = jnp.take(blocks, jnp.maximum(slot_of, 0), axis=0, mode="clip")
+    placed = jnp.where(present[:, None, None], placed, 0)
+    return placed.reshape(-1, half_width).astype(jnp.bfloat16)
 
 
 def per_device(
@@ -144,6 +135,12 @@
     ).astype(jnp.bfloat16)
     g_block = dispatch(g_pick, exp_index, exp_count, mp_count, my_slice)
     g_all = lax.all_gather(g_block, "seq", axis=0)
+    present = jnp.any(route_table == exp_index, axis=1)
+    slot_of = jnp.cumsum(present.astype(jnp.int32)) - 1
+    select = ((slot_of[None, :] == jnp.arange(slot_total)[:, None]) & present[None, :]).astype(
+        jnp.bfloat16
+    )
+    g_rows = compact(select, g_all, half_width)
     input_scale = jnp.sqrt(1.0 - jnp.exp(-2.0 * head_decay_speed))
     cum_level = jnp.cumsum(
         -head_decay_speed[None, :]
@@ -205,7 +202,7 @@
     mixed_out = (activations.astype(jnp.float32) + outputs.reshape(tokens, slice_width)).astype(
         jnp.bfloat16
     )
-    g_all, mixed_out = lax.optimization_barrier((g_all, mixed_out))
+    g_rows, mixed_out = lax.optimization_barrier((g_rows, mixed_out))
     h_pick = jnp.einsum(
         "eb,brf->erf",
         chosen,
@@ -214,13 +211,7 @@
     ).astype(jnp.bfloat16)
     h_block = dispatch(h_pick, exp_index, exp_count, mp_count, my_slice)
     h_all = lax.all_gather(h_block, "seq", axis=0)
-    present = jnp.any(route_table == exp_index, axis=1)
-    slot_of = jnp.cumsum(present.astype(jnp.int32)) - 1
-    select = ((slot_of[None, :] == jnp.arange(slot_total)[:, None]) & present[None, :]).astype(
-        jnp.bfloat16
-    )
     x_rows = compact(select, h_all, half_width)
-    g_rows = compact(select, g_all, half_width)
     up_local = expert_up_weight[0]
     down_local = expert_down_weight[0]
     pre_act = mp_sum(jnp.dot(x_rows, up_local, preferred_element_type=jnp.float32))

time: 463 us -> 473 us (1.022)
  local copies, waits for them, and re-layouts: 52.4 us -> 93.8 us
  other arithmetic: 82.7 us -> 49 us
  waiting for transfers between devices: 116 us -> 144 us
  between operations: 40.5 us -> 15.5 us
    unnamed x30 -> x1, other arithmetic: 48.1 us -> 0.08 us
    gather x0 -> x4, local copies, waits for them, and re-layouts: none -> 31.6 us  [the longest x2 19.1 us: spread(): placed = jnp.take(blocks, jnp.maximum(slot_of, 0), axis=0, mode='clip')]
    all_gather x1, waiting for transfers between devices: 34.3 us -> 62.4 us  [per_device(): h_all = lax.all_gather(h_block, 'seq', axis=0)]
    select_n x0 -> x4, other arithmetic: none -> 19.2 us  [the longest x3 12 us: compact(): jnp.where(used[:, None, None], jnp.take(blocks, source, axis=0, mode='cli...]
    unnamed x126 -> x121, local copies, waits for them, and re-layouts: 5.75 us -> 18.3 us
    concatenate x3 -> x0, other arithmetic: 4.92 us -> none  [the longest x2 3.42 us: compact(): return jnp.concatenate(rows_out, axis=0).astype(jnp.bfloat16)]
  transfers between devices with their start and end apart: 17 -> 17, of which waited for: 6 -> 6; matrix products, arithmetic and copies ran while one was open for 24% -> 20% of each run, Pallas kernels for 0% -> 0%
where the time goes in v5:
time: 473 us; the launch traced here: 466 us
  waiting for transfers between devices  144 us (30%)
  local copies, waits for them, and re-layouts  93.8 us (20%)
  matrix products  78.2 us (17%)
  other arithmetic  49 us (10%)
  blocking collectives  48.2 us (10%)
  starting transfers between devices  37.5 us (8%)
  between operations  15.5 us (3%)
    unnamed x4, waiting for transfers between devices  72.8 us
    all_gather x1, waiting for transfers between devices, per_device(): h_all = lax.all_gather(h_block, 'seq', axis=0)  62.4 us
    ppermute x8, starting transfers between devices, dispatch(): received.append(lax.ppermute(send, ('expert', 'mp'), pairs))  26.4 us
    all_gather x1, blocking collectives, per_device(): lax.all_gather(jnp.concatenate([flat_state, level_lanes], axis=1), 'seq')  24.9 us
    all_gather x1, blocking collectives, per_device(): adjoint_all = lax.all_gather(flat_adjoint.astype(jnp.bfloat16), 'seq')  23.3 us
    gather x2, local copies, waits for them, and re-layouts, spread(): placed = jnp.take(blocks, jnp.maximum(slot_of, 0), axis=0, mode='clip')  19.1 us
    unnamed x121, local copies, waits for them, and re-layouts  18.3 us
    gather x2, local copies, waits for them, and re-layouts, compact(): jnp.take(blocks, source, axis=0, mode='clip')  12.4 us
  transfers between devices with their start and end apart: 17, of which 6 were waited for; matrix products, arithmetic and copies ran while one was open for 20% of the time, Pallas kernels for 0%

profile of v5, /device:TPU:0, one launch (start us, length us, event | category | flops | bytes accessed | tf_op | source)
XLA Modules:
  0.0 465.9 jit_solution(1482515830136544033)
XLA Ops:
  12.0 4.1 collective-permute-start.2
  18.9 4.3 collective-permute-start.1
  50.1 24.9 %all-gather = f32[128,1152]{1,0:T(8,128)S(1)} all-gather(f32[8,1152]{1,0:T(8,128)S(1)} %pad_maximum_fusion.2), channel_id=2, replica_groups=mesh['seq'=16,'expert'=4,'mp'=2] {'seq'}, dimensions={0}, use_global_device_ids=true | all-gather | bytes 626688 | tf_op jit(solution)/shard_map/all_gather | solution.py:194
  88.1 4.2 fusion.45
  108.6 3.2 add_convert_fusion
  111.8 6.2 %gather_fusion.1 = bf16[8,128,2048]{2,1,0:T(8,128)(2,1)} fusion(bf16[16,128,2048]{2,1,0:T(8,128)(2,1)} %all-gather.4.cloned.1.call-done, s32[1024]{0:T(1024)S(1)} %pad_clamp_fusion.1), kind=kCustom, calls=%fused_computation.3 | custom fusion | bytes 8388640 | tf_op jit(solution)/shard_map/jit(_take)/gather | solution.py:93
  118.0 4.6 bitcast_select_fusion.1
  125.3 9.2 %collective-permute-start.6 = (bf16[128,512]{1,0:T(8,128)(2,1)S(1)}, bf16[128,512]{1,0:T(8,128)(2,1)S(1)}, u32[]{:S(2)}, u32[]{:S(2)}) collective-permute-start(bf16[128,512]{1,0:T(8,128)(2,1)S(1)} %bitcast.239), channel_id=1, source_target_pairs={{0,2},{1,4},{2,6},{3,0},{4,3},{5,5},{6,7},{7,1},{8,10},{9,12},{10,... | collective-permute-start | bytes 393224 | tf_op jit(solution)/shard_map/ppermute | solution.py:53
  134.5 3.5 collective-permute-start.7
  152.0 7.8 %fusion.54 = bf16[1024,768]{1,0:T(8,128)(2,1)} fusion(bf16[1024,2048]{1,0:T(8,128)(2,1)} %bitcast_select_fusion.1, bf16[1,768,2048]{2,1,0:T(8,128)(2,1)} %param.19), kind=kOutput, calls=%fused_computation.75 | convolution fusion | flops 3222011904 | bytes 8912896 | tf_op jit(solution)/shard_map/td,fd->tf/dot_general | solution.py:221
  160.0 62.4 %all-gather.6.cloned.1.call-done = bf16[16,128,2048]{2,1,0:T(8,128)(2,1)} async-done(((bf16[1,128,2048]{2,1,0:T(8,128)(2,1)}), bf16[16,128,2048]{2,1,0:T(8,128)(2,1)}) %all-gather.6.cloned.1.call-update) | async-done | bytes 8388624 | tf_op jit(solution)/shard_map/all_gather | solution.py:213
  222.4 6.2 %gather_fusion.2 = bf16[8,128,2048]{2,1,0:T(8,128)(2,1)} fusion(bf16[16,128,2048]{2,1,0:T(8,128)(2,1)} %all-gather.6.cloned.1.call-done, s32[1024]{0:T(1024)S(1)} %pad_clamp_fusion.1), kind=kCustom, calls=%fused_computation.4 | custom fusion | bytes 8388640 | tf_op jit(solution)/shard_map/jit(_take)/gather | solution.py:93
  231.2 3.4 fusion.57
  235.0 3.3 collective-permute-done.9
  239.5 3.5 multiply_convert_fusion.1
  243.0 5.0 %convolution_convert_fusion = bf16[1024,2048]{1,0:T(8,128)(2,1)} fusion(bf16[1024,768]{1,0:T(8,128)(2,1)S(1)} %multiply_convert_fusion.1, bf16[1,2048,768]{2,1,0:T(8,128)(2,1)S(1)} %copy-done), kind=kOutput, calls=%fused_computation.54 | convolution fusion | flops 3223322624 | bytes 8912896 | tf_op jit(solution)/shard_map/tf,df->td/dot_general | solution.py:226
  248.0 6.8 %gather_fusion.3 = bf16[16,128,2048]{2,1,0:T(8,128)(2,1)} fusion(bf16[8,128,2048]{2,1,0:T(8,128)(2,1)} %bitcast.205, s32[1024]{0:T(1024)S(1)} %pad_clamp_fusion), kind=kCustom, calls=%fused_computation.5 | custom fusion | bytes 16777280 | tf_op jit(solution)/shard_map/jit(_take)/gather | solution.py:99
  254.8 12.3 %copy.253 = bf16[2048,2048]{0,1:T(8,128)(2,1)} copy(bf16[2048,2048]{1,0:T(8,128)(2,1)} %bitcast.204) | data formatting | bytes 16777216 | tf_op jit(solution)/shard_map/jit(_take)/gather | solution.py:99
  267.1 7.2 %broadcast_select_fusion = bf16[2048,2048]{0,1:T(8,128)(2,1)} fusion(bf16[2048,2048]{0,1:T(8,128)(2,1)} %copy.253, pred[2048]{0:T(1024)(128)(4,1)S(1)} %broadcast_bitcast_fusion), kind=kLoop, calls=%fused_computation.12 | loop fusion | flops 4194304 | bytes 16779264 | tf_op jit(solution)/shard_map/jit(_where)/select_n | solution.py:100
  274.3 12.3 %copy.254 = bf16[2048,2048]{1,0:T(8,128)(2,1)} copy(bf16[2048,2048]{0,1:T(8,128)(2,1)} %broadcast_select_fusion) | data formatting | bytes 16777216
  288.1 4.8 %bitcast_select_fusion = bf16[1024,2048]{1,0:T(8,128)(2,1)} fusion(bf16[8,128,2048]{2,1,0:T(8,128)(2,1)} %gather_fusion.2, pred[1024]{0:T(1024)(128)(4,1)S(1)} %broadcast_bitcast_fusion.1), kind=kLoop, calls=%fused_computation.19 | loop fusion | flops 2097152 | bytes 8389632 | tf_op jit(solution)/shard_map/jit(_where)/select_n | solution.py:93
  294.0 5.7 %convolution_bitcast_fusion = f32[1,768,2048]{2,1,0:T(8,128)} fusion(bf16[1024,2048]{1,0:T(8,128)(2,1)S(1)} %copy-done.4, bf16[1024,768]{1,0:T(8,128)(2,1)S(1)} %copy-done.12, bf16[1024,768]{1,0:T(8,128)(2,1)S(1)} %copy-done.10), kind=kOutput, calls=%fused_computation.52 | convolution fusion | flops 3227516928 | bytes 13631488 | tf_op jit(solution)/shard_map/tf,td->fd/dot_general | solution.py:219
  299.7 72.7 %reduce-scatter.4.cloned.1.call-done = bf16[128,2048]{1,0:T(8,128)(2,1)} async-done(((bf16[2048,2048]{1,0:T(8,128)(2,1)}), bf16[128,2048]{1,0:T(8,128)(2,1)}) %reduce-scatter.4.cloned.1.call-update) | async-done | bytes 524304
  374.7 4.0 collective-permute-start.11
  380.4 4.9 %collective-permute-start.13 = (bf16[128,512]{1,0:T(8,128)(2,1)}, bf16[128,512]{1,0:T(8,128)(2,1)S(1)}, u32[]{:S(2)}, u32[]{:S(2)}) collective-permute-start(bf16[128,512]{1,0:T(8,128)(2,1)} %bitcast.54), channel_id=1, source_target_pairs={{6,0},{0,1},{2,2},{4,3},{7,4},{1,5},{3,6},{5,7},{14,8},{8,9},{10,1... | collective-permute-start | bytes 393224 | tf_op jit(solution)/shard_map/ppermute | solution.py:69
  385.3 8.4 %convolution_bitcast_fusion.1 = f32[1,2048,768]{2,1,0:T(8,128)} fusion(bf16[1024,2048]{1,0:T(8,128)(2,1)} %bitcast_select_fusion, bf16[1024,768]{1,0:T(8,128)(2,1)S(1)} %copy-done.8), kind=kOutput, calls=%fused_computation.53 | convolution fusion | flops 3221225472 | bytes 12058624 | tf_op jit(solution)/shard_map/td,tf->df/dot_general | solution.py:225
  400.8 4.3 fusion.8
  407.5 4.4 fusion.2
  413.0 23.3 %all_gather.20 = bf16[16,8,1024]{2,1,0:T(8,128)(2,1)S(1)} all-gather(bf16[1,8,1024]{2,1,0:T(8,128)(2,1)S(1)} %convert_element_type.168), channel_id=1, replica_groups=mesh['seq'=16,'expert'=4,'mp'=2] {'seq'}, dimensions={0}, use_global_device_ids=true | all-gather | bytes 278528 | tf_op jit(solution)/shard_map/all_gather | solution.py:280
  437.3 3.6 fusion.94
  451.8 3.0 copy.250
  454.9 4.0 add.297
  (254 shorter events, 112.7 us)
Async XLA Ops:
  7.2 224.0 %copy-start = (bf16[1,2048,768]{2,1,0:T(8,128)(2,1)S(1)}, bf16[1,2048,768]{2,1,0:T(8,128)(2,1)}, u32[]{:S(2)}) copy-start(bf16[1,2048,768]{2,1,0:T(8,128)(2,1)} %param.18) | copy-start | bytes 9437188
  7.2 104.6 %all-gather.4.cloned.1.call-start = ((), (), s32[]{:S(2)}) async-start(), calls=%async_computation.1 | async-start | bytes 8912896 | tf_op jit(solution)/shard_map/all_gather | solution.py:137
  8.2 22.9 %copy-start.34 = (s32[16,8]{1,0:T(8,128)}, s32[16,8]{1,0:T(8,128)S(1)}, u32[]{:S(2)}) copy-start(s32[16,8]{1,0:T(8,128)S(1)} %reshape.355) | copy-start | bytes 1540
  11.9 23.4 %copy-start.53 = (f32[8]{0:T(128)S(1)}, f32[8]{0:T(128)}, u32[]{:S(2)}) copy-start(f32[8]{0:T(128)} %param.15) | copy-start | bytes 100
  11.9 23.4 %copy-start.43 = (s32[1024]{0:T(1024)S(1)}, s32[1024]{0:T(1024)}, u32[]{:S(2)}) copy-start(s32[1024]{0:T(1024)} %param.16) | copy-start | bytes 12292
  12.0 11.3 %collective-permute-start.2 = (bf16[128,512]{1,0:T(8,128)(2,1)S(1)}, bf16[128,512]{1,0:T(8,128)(2,1)S(1)}, u32[]{:S(2)}, u32[]{:S(2)}) collective-permute-start(bf16[128,512]{1,0:T(8,128)(2,1)S(1)} %bitcast.231), channel_id=1, source_target_pairs={{0,4},{1,6},{2,0},{3,2},{4,5},{5,7},{6,1},{7,3},{8,12},{9,14},{10,... | collective-permute-start | bytes 393224 | tf_op jit(solution)/shard_map/ppermute | solution.py:53
  16.0 7.2 %collective-permute-start.3 = (bf16[128,512]{1,0:T(8,128)(2,1)S(1)}, bf16[128,512]{1,0:T(8,128)(2,1)S(1)}, u32[]{:S(2)}, u32[]{:S(2)}) collective-permute-start(bf16[128,512]{1,0:T(8,128)(2,1)S(1)} %bitcast.235), channel_id=1, source_target_pairs={{0,6},{1,0},{2,2},{3,4},{4,7},{5,1},{6,3},{7,5},{8,14},{9,8},{10,1... | collective-permute-start | bytes 393224 | tf_op jit(solution)/shard_map/ppermute | solution.py:53
  18.2 5.1 %collective-permute-start = (bf16[128,512]{1,0:T(8,128)(2,1)S(1)}, bf16[128,512]{1,0:T(8,128)(2,1)S(1)}, u32[]{:S(2)}, u32[]{:S(2)}) collective-permute-start(bf16[128,512]{1,0:T(8,128)(2,1)S(1)} %bitcast.237), channel_id=1, source_target_pairs={{0,0},{1,2},{2,4},{3,6},{4,1},{5,3},{6,5},{7,7},{8,8},{9,10},{10,1... | collective-permute-start | bytes 393224 | tf_op jit(solution)/shard_map/ppermute | solution.py:53
  18.9 7.0 %collective-permute-start.1 = (bf16[128,512]{1,0:T(8,128)(2,1)S(1)}, bf16[128,512]{1,0:T(8,128)(2,1)S(1)}, u32[]{:S(2)}, u32[]{:S(2)}) collective-permute-start(bf16[128,512]{1,0:T(8,128)(2,1)S(1)} %bitcast.240), channel_id=1, source_target_pairs={{0,2},{1,4},{2,6},{3,0},{4,3},{5,5},{6,7},{7,1},{8,10},{9,12},{10,... | collective-permute-start | bytes 393224 | tf_op jit(solution)/shard_map/ppermute | solution.py:53
  23.2 12.2 %copy-start.49 = (pred[4]{0:T(512)(128)(4,1)}, pred[4]{0:T(512)(128)(4,1)S(1)}, u32[]{:S(2)}) copy-start(pred[4]{0:T(512)(128)(4,1)S(1)} %compare_and_fusion) | copy-start | bytes 16
  23.2 12.1 %copy-start.42 = (s32[1024]{0:T(1024)}, s32[1024]{0:T(1024)S(1)}, u32[]{:S(2)}) copy-start(s32[1024]{0:T(1024)S(1)} %pad_clamp_fusion.2) | copy-start | bytes 12292
  35.2 9.5 %copy-start.19 = (bf16[1024,16]{0,1:T(8,128)(2,1)S(1)}, bf16[1024,16]{0,1:T(8,128)(2,1)}, u32[]{:S(2)}) copy-start(bf16[1024,16]{0,1:T(8,128)(2,1)} %param.13) | copy-start | bytes 98308
  35.2 187.2 %all-gather.6.cloned.1.call-start = ((), (), s32[]{:S(2)}) async-start(), calls=%async_computation.2 | async-start | bytes 8912896 | tf_op jit(solution)/shard_map/all_gather | solution.py:213
  35.3 9.3 %copy-start.44 = (f32[8]{0:T(128)}, f32[8]{0:T(128)S(1)}, u32[]{:S(2)}) copy-start(f32[8]{0:T(128)S(1)} %get-tuple-element.48) | copy-start | bytes 100
  45.4 41.9 %copy-start.18 = (bf16[1024,16]{0,1:T(8,128)(2,1)S(1)}, bf16[1024,16]{0,1:T(8,128)(2,1)}, u32[]{:S(2)}) copy-start(bf16[1024,16]{0,1:T(8,128)(2,1)} %param.14) | copy-start | bytes 98308
  85.9 12.5 %copy-start.23 = (pred[512,512]{1,0:T(8,128)(4,1)}, pred[512,512]{1,0:T(8,128)(4,1)S(1)}, u32[]{:S(2)}) copy-start(pred[512,512]{1,0:T(8,128)(4,1)S(1)} %iota_compare_fusion) | copy-start | bytes 786436
  87.7 10.7 %copy-start.13 = (f32[512,512]{1,0:T(8,128)}, f32[512,512]{1,0:T(8,128)S(1)}, u32[]{:S(2)}) copy-start(f32[512,512]{1,0:T(8,128)S(1)} %fusion.129) | copy-start | bytes 3145732
  122.7 23.2 %copy-start.50 = (pred[4]{0:T(512)(128)(4,1)S(1)}, pred[4]{0:T(512)(128)(4,1)}, u32[]{:S(2)}) copy-start(pred[4]{0:T(512)(128)(4,1)} %copy-done.49) | copy-start | bytes 16
  124.6 15.4 %collective-permute-start.5 = (bf16[128,512]{1,0:T(8,128)(2,1)S(1)}, bf16[128,512]{1,0:T(8,128)(2,1)S(1)}, u32[]{:S(2)}, u32[]{:S(2)}) collective-permute-start(bf16[128,512]{1,0:T(8,128)(2,1)S(1)} %bitcast.238), channel_id=1, source_target_pairs={{0,0},{1,2},{2,4},{3,6},{4,1},{5,3},{6,5},{7,7},{8,8},{9,10},{10,1... | collective-permute-start | bytes 393224 | tf_op jit(solution)/shard_map/ppermute | solution.py:53
  125.3 14.7 %collective-permute-start.6 = (bf16[128,512]{1,0:T(8,128)(2,1)S(1)}, bf16[128,512]{1,0:T(8,128)(2,1)S(1)}, u32[]{:S(2)}, u32[]{:S(2)}) collective-permute-start(bf16[128,512]{1,0:T(8,128)(2,1)S(1)} %bitcast.239), channel_id=1, source_target_pairs={{0,2},{1,4},{2,6},{3,0},{4,3},{5,5},{6,7},{7,1},{8,10},{9,12},{10,... | collective-permute-start | bytes 393224 | tf_op jit(solution)/shard_map/ppermute | solution.py:53
  134.5 6.8 %collective-permute-start.7 = (bf16[128,512]{1,0:T(8,128)(2,1)S(1)}, bf16[128,512]{1,0:T(8,128)(2,1)S(1)}, u32[]{:S(2)}, u32[]{:S(2)}) collective-permute-start(bf16[128,512]{1,0:T(8,128)(2,1)S(1)} %bitcast.241), channel_id=1, source_target_pairs={{0,4},{1,6},{2,0},{3,2},{4,5},{5,7},{6,1},{7,3},{8,12},{9,14},{10,... | collective-permute-start | bytes 393224 | tf_op jit(solution)/shard_map/ppermute | solution.py:53
  138.1 4.4 collective-permute-start.8
  151.9 220.5 %reduce-scatter.4.cloned.1.call-start = ((), (), s32[]{:S(2)}) async-start(), calls=%async_computation.3 | async-start | bytes 8912896
  159.7 75.2 %collective-permute-start.4 = (bf16[1024,768]{1,0:T(8,128)(2,1)}, bf16[1024,768]{1,0:T(8,128)(2,1)}, u32[]{:S(2)}, u32[]{:S(2)}) collective-permute-start(bf16[1024,768]{1,0:T(8,128)(2,1)} %fusion.54), channel_id=1, source_target_pairs={{0,1},{1,0},{2,3},{3,2},{4,5},{5,4},{6,7},{7,6},{8,9},{9,8},{10,11... | collective-permute-start | bytes 4718600 | tf_op jit(solution)/shard_map/ppermute | solution.py:36
  234.6 3.7 collective-permute-start.9
  294.0 91.3 %copy-start.8 = (bf16[1024,768]{1,0:T(8,128)(2,1)S(1)}, bf16[1024,768]{1,0:T(8,128)(2,1)}, u32[]{:S(2)}) copy-start(bf16[1024,768]{1,0:T(8,128)(2,1)} %copy-done.7) | copy-start | bytes 4718596
  373.9 19.9 %collective-permute-start.10 = (bf16[128,512]{1,0:T(8,128)(2,1)S(1)}, bf16[128,512]{1,0:T(8,128)(2,1)S(1)}, u32[]{:S(2)}, u32[]{:S(2)}) collective-permute-start(bf16[128,512]{1,0:T(8,128)(2,1)S(1)} %bitcast.243), channel_id=1, source_target_pairs={{0,0},{2,1},{4,2},{6,3},{1,4},{3,5},{5,6},{7,7},{8,8},{10,9},{12,1... | collective-permute-start | bytes 393224 | tf_op jit(solution)/shard_map/ppermute | solution.py:69
  374.7 19.3 %collective-permute-start.11 = (bf16[128,512]{1,0:T(8,128)(2,1)S(1)}, bf16[128,512]{1,0:T(8,128)(2,1)S(1)}, u32[]{:S(2)}, u32[]{:S(2)}) collective-permute-start(bf16[128,512]{1,0:T(8,128)(2,1)S(1)} %bitcast.244), channel_id=1, source_target_pairs={{2,0},{4,1},{6,2},{0,3},{3,4},{5,5},{7,6},{1,7},{10,8},{12,9},{14,... | collective-permute-start | bytes 393224 | tf_op jit(solution)/shard_map/ppermute | solution.py:69
  378.8 15.4 %collective-permute-start.12 = (bf16[128,512]{1,0:T(8,128)(2,1)S(1)}, bf16[128,512]{1,0:T(8,128)(2,1)S(1)}, u32[]{:S(2)}, u32[]{:S(2)}) collective-permute-start(bf16[128,512]{1,0:T(8,128)(2,1)S(1)} %bitcast.245), channel_id=1, source_target_pairs={{4,0},{6,1},{0,2},{2,3},{5,4},{7,5},{1,6},{3,7},{12,8},{14,9},{8,1... | collective-permute-start | bytes 393224 | tf_op jit(solution)/shard_map/ppermute | solution.py:69
  380.4 14.0 %collective-permute-start.13 = (bf16[128,512]{1,0:T(8,128)(2,1)}, bf16[128,512]{1,0:T(8,128)(2,1)S(1)}, u32[]{:S(2)}, u32[]{:S(2)}) collective-permute-start(bf16[128,512]{1,0:T(8,128)(2,1)} %bitcast.54), channel_id=1, source_target_pairs={{6,0},{0,1},{2,2},{4,3},{7,4},{1,5},{3,6},{5,7},{14,8},{8,9},{10,1... | collective-permute-start | bytes 393224 | tf_op jit(solution)/shard_map/ppermute | solution.py:69
  397.7 7.4 %copy-start.2 = (f32[1024,512]{1,0:T(8,128)}, f32[1024,512]{1,0:T(8,128)S(1)}, u32[]{:S(2)}) copy-start(f32[1024,512]{1,0:T(8,128)S(1)} %bitcast_add_fusion) | copy-start | bytes 6291460
  407.5 29.8 %copy-start.16 = (f32[512,512]{1,0:T(8,128)S(1)}, f32[512,512]{1,0:T(8,128)}, u32[]{:S(2)}) copy-start(f32[512,512]{1,0:T(8,128)} %copy-done.15) | copy-start | bytes 3145732
  (40 other events, 140.5 us)
Sparse Core Ops, SparseCore 0:
  35.3 75.5 all-gather.3
  152.1 70.3 all-gather.5
  286.8 85.5 reduce-scatter.3

commit v6 on v5

--- a/solution.py
+++ b/solution.py
@@ -223,8 +223,9 @@
     sigmoid_pre = jax.nn.sigmoid(pre_act)
     pre_grad = (act_grad * sigmoid_pre * (1.0 + pre_act * (1.0 - sigmoid_pre))).astype(jnp.bfloat16)
     up_grad = jnp.einsum("td,tf->df", x_rows, pre_grad, preferred_element_type=jnp.float32)
-    row_grad = jnp.einsum("tf,df->td", pre_grad, up_local, preferred_element_type=jnp.float32)
-    spread_rows = spread(present, slot_of, row_grad.astype(jnp.bfloat16), half_width)
+    shard_grad = spread(present, slot_of, pre_grad, pre_grad.shape[1])
+    row_grad = jnp.einsum("tf,df->td", shard_grad, up_local, preferred_element_type=jnp.float32)
+    spread_rows = row_grad.astype(jnp.bfloat16)
     back_rows = lax.psum_scatter(
         spread_rows,
         "seq",

time: 473 us -> 444 us (0.939)
  local copies, waits for them, and re-layouts: 93.8 us -> 65 us
    reduce_scatter x0 -> x1, waiting for transfers between devices: none -> 72.9 us  [per_device(): lax.psum_scatter(spread_rows, 'seq', scatter_dimension=0, tiled=True)]
    unnamed x4 -> x3, waiting for transfers between devices: 72.8 us -> 0.05 us
    gather x2 -> x1, local copies, waits for them, and re-layouts: 19.1 us -> 3.79 us  [spread(): placed = jnp.take(blocks, jnp.maximum(slot_of, 0), axis=0, mode='clip')]
    unnamed x121, local copies, waits for them, and re-layouts: 18.3 us -> 3.51 us
    select_n x1, other arithmetic: 7.16 us -> 2.16 us  [spread(): placed = jnp.where(present[:, None, None], placed, 0)]
  transfers between devices with their start and end apart: 17 -> 17, of which waited for: 6 -> 6; matrix products, arithmetic and copies ran while one was open for 20% -> 21% of each run, Pallas kernels for 0% -> 0%
where the time goes in v6:
time: 444 us; the launch traced here: 438 us
  waiting for transfers between devices  144 us (32%)
  matrix products  82.2 us (19%)
  local copies, waits for them, and re-layouts  65 us (15%)
  blocking collectives  48.6 us (11%)
  other arithmetic  45.6 us (10%)
  starting transfers between devices  36.7 us (8%)
  between operations  15.6 us (4%)
    reduce_scatter x1, waiting for transfers between devices, per_device(): lax.psum_scatter(spread_rows, 'seq', scatter_dimension=0, tiled=True)  72.9 us
    all_gather x1, waiting for transfers between devices, per_device(): h_all = lax.all_gather(h_block, 'seq', axis=0)  62 us
    all_gather x1, blocking collectives, per_device(): lax.all_gather(jnp.concatenate([flat_state, level_lanes], axis=1), 'seq')  25.3 us
    ppermute x8, starting transfers between devices, dispatch(): received.append(lax.ppermute(send, ('expert', 'mp'), pairs))  25.2 us
    all_gather x1, blocking collectives, per_device(): adjoint_all = lax.all_gather(flat_adjoint.astype(jnp.bfloat16), 'seq')  23.3 us
    gather x2, local copies, waits for them, and re-layouts, compact(): jnp.take(blocks, source, axis=0, mode='clip')  12.4 us
    select_n x3, other arithmetic, compact(): jnp.where(used[:, None, None], jnp.take(blocks, source, axis=0, mode='cli...  12 us
    ppermute x4, starting transfers between devices, give_back(): received.append(lax.ppermute(send, ('expert', 'mp'), pairs))  10.3 us
  transfers between devices with their start and end apart: 17, of which 6 were waited for; matrix products, arithmetic and copies ran while one was open for 21% of the time, Pallas kernels for 0%

profile of v6, /device:TPU:0, one launch (start us, length us, event | category | flops | bytes accessed | tf_op | source)
XLA Modules:
  0.0 437.8 jit_solution(13989864294972557223)
XLA Ops:
  11.9 6.1 %collective-permute-start.3 = (bf16[128,512]{1,0:T(8,128)(2,1)S(1)}, bf16[128,512]{1,0:T(8,128)(2,1)S(1)}, u32[]{:S(2)}, u32[]{:S(2)}) collective-permute-start(bf16[128,512]{1,0:T(8,128)(2,1)S(1)} %bitcast.234), channel_id=1, source_target_pairs={{0,6},{1,0},{2,2},{3,4},{4,7},{5,1},{6,3},{7,5},{8,14},{9,8},{10,1... | collective-permute-start | bytes 393224 | tf_op jit(solution)/shard_map/ppermute | solution.py:53
  18.7 4.0 collective-permute-start.1
  52.1 25.3 %all-gather = f32[128,1152]{1,0:T(8,128)S(1)} all-gather(f32[8,1152]{1,0:T(8,128)S(1)} %pad_maximum_fusion.2), channel_id=2, replica_groups=mesh['seq'=16,'expert'=4,'mp'=2] {'seq'}, dimensions={0}, use_global_device_ids=true | all-gather | bytes 626688 | tf_op jit(solution)/shard_map/all_gather | solution.py:194
  90.5 4.2 fusion.45
  98.1 2.7 fusion.47
  104.2 2.8 maximum_add_fusion
  107.0 2.9 copy.231
  111.1 3.2 add_convert_fusion
  114.3 6.2 %gather_fusion.1 = bf16[8,128,2048]{2,1,0:T(8,128)(2,1)} fusion(bf16[16,128,2048]{2,1,0:T(8,128)(2,1)} %all-gather.4.cloned.1.call-done, s32[1024]{0:T(1024)S(1)} %pad_clamp_fusion.1), kind=kCustom, calls=%fused_computation.3 | custom fusion | bytes 8388640 | tf_op jit(solution)/shard_map/jit(_take)/gather | solution.py:93
  120.5 4.6 %bitcast_select_fusion.1 = bf16[1024,2048]{1,0:T(8,128)(2,1)} fusion(bf16[8,128,2048]{2,1,0:T(8,128)(2,1)} %gather_fusion.1, pred[1024]{0:T(1024)(128)(4,1)S(1)} %broadcast_bitcast_fusion), kind=kLoop, calls=%fused_computation.20 | loop fusion | flops 2097152 | bytes 8389632 | tf_op jit(solution)/shard_map/jit(_where)/select_n | solution.py:93
  127.7 7.0 %collective-permute-start.6 = (bf16[128,512]{1,0:T(8,128)(2,1)S(1)}, bf16[128,512]{1,0:T(8,128)(2,1)S(1)}, u32[]{:S(2)}, u32[]{:S(2)}) collective-permute-start(bf16[128,512]{1,0:T(8,128)(2,1)S(1)} %bitcast.246), channel_id=1, source_target_pairs={{0,2},{1,4},{2,6},{3,0},{4,3},{5,5},{6,7},{7,1},{8,10},{9,12},{10,... | collective-permute-start | bytes 393224 | tf_op jit(solution)/shard_map/ppermute | solution.py:53
  135.2 4.5 %collective-permute-start.8 = (bf16[128,512]{1,0:T(8,128)(2,1)S(1)}, bf16[128,512]{1,0:T(8,128)(2,1)S(1)}, u32[]{:S(2)}, u32[]{:S(2)}) collective-permute-start(bf16[128,512]{1,0:T(8,128)(2,1)S(1)} %bitcast.249), channel_id=1, source_target_pairs={{0,6},{1,0},{2,2},{3,4},{4,7},{5,1},{6,3},{7,5},{8,14},{9,8},{10,1... | collective-permute-start | bytes 393224 | tf_op jit(solution)/shard_map/ppermute | solution.py:53
  151.7 7.8 %fusion.54 = bf16[1024,768]{1,0:T(8,128)(2,1)} fusion(bf16[1024,2048]{1,0:T(8,128)(2,1)} %bitcast_select_fusion.1, bf16[1,768,2048]{2,1,0:T(8,128)(2,1)} %param.19), kind=kOutput, calls=%fused_computation.75 | convolution fusion | flops 3222011904 | bytes 8912896 | tf_op jit(solution)/shard_map/td,fd->tf/dot_general | solution.py:221
  160.3 62.0 %all-gather.6.cloned.1.call-done = bf16[16,128,2048]{2,1,0:T(8,128)(2,1)} async-done(((bf16[1,128,2048]{2,1,0:T(8,128)(2,1)}), bf16[16,128,2048]{2,1,0:T(8,128)(2,1)}) %all-gather.6.cloned.1.call-update) | async-done | bytes 8388624 | tf_op jit(solution)/shard_map/all_gather | solution.py:213
  222.3 6.2 %gather_fusion.2 = bf16[8,128,2048]{2,1,0:T(8,128)(2,1)} fusion(bf16[16,128,2048]{2,1,0:T(8,128)(2,1)} %all-gather.6.cloned.1.call-done, s32[1024]{0:T(1024)S(1)} %pad_clamp_fusion.1), kind=kCustom, calls=%fused_computation.4 | custom fusion | bytes 8388640 | tf_op jit(solution)/shard_map/jit(_take)/gather | solution.py:93
  231.1 3.4 fusion.57
  234.8 3.4 collective-permute-done.9
  238.2 5.2 %multiply_convert_fusion.1 = bf16[1024,768]{1,0:T(8,128)(2,1)} fusion(bf16[1024,768]{1,0:T(8,128)(2,1)} %collective-permute-done.4, bf16[1024,768]{1,0:T(8,128)(2,1)} %fusion.54, bf16[1024,768]{1,0:T(8,128)(2,1)S(1)} %collective-permute-done.9, bf16[1024,768]{1,0:T(8,128)(2,1)S(1)} %fusion.57), kind=kLoop, calls=%fused_computation.64 | loop fusion | flops 11796480 | bytes 7864320 | tf_op jit(solution)/shard_map/convert_element_type | solution.py:224
  243.3 3.8 gather_fusion.3
  249.3 9.1 %convolution_convert_fusion = bf16[2048,2048]{1,0:T(8,128)(2,1)} fusion(bf16[2048,768]{1,0:T(8,128)(2,1)S(1)} %bitcast.223, bf16[1,2048,768]{2,1,0:T(8,128)(2,1)S(1)} %copy-done), kind=kOutput, calls=%fused_computation.12 | convolution fusion | flops 6446645248 | bytes 14680064 | tf_op jit(solution)/shard_map/tf,df->td/dot_general | solution.py:227
  259.8 4.8 %bitcast_select_fusion = bf16[1024,2048]{1,0:T(8,128)(2,1)} fusion(bf16[8,128,2048]{2,1,0:T(8,128)(2,1)} %gather_fusion.2, pred[1024]{0:T(1024)(128)(4,1)S(1)} %broadcast_bitcast_fusion), kind=kLoop, calls=%fused_computation.19 | loop fusion | flops 2097152 | bytes 8389632 | tf_op jit(solution)/shard_map/jit(_where)/select_n | solution.py:93
  265.7 5.6 %convolution_bitcast_fusion = f32[1,768,2048]{2,1,0:T(8,128)} fusion(bf16[1024,2048]{1,0:T(8,128)(2,1)S(1)} %copy-done.5, bf16[1024,768]{1,0:T(8,128)(2,1)S(1)} %copy-done.11, bf16[1024,768]{1,0:T(8,128)(2,1)S(1)} %copy-done.9), kind=kOutput, calls=%fused_computation.52 | convolution fusion | flops 3227516928 | bytes 13631488 | tf_op jit(solution)/shard_map/tf,td->fd/dot_general | solution.py:219
  271.4 72.9 %reduce-scatter.2.cloned.1.call-done = bf16[128,2048]{1,0:T(8,128)(2,1)} async-done(((bf16[2048,2048]{1,0:T(8,128)(2,1)}), bf16[128,2048]{1,0:T(8,128)(2,1)}) %reduce-scatter.2.cloned.1.call-update) | async-done | bytes 524304 | tf_op jit(solution)/shard_map/reduce_scatter | solution.py:229
  347.5 4.0 collective-permute-start.11
  352.4 4.9 %collective-permute-start.13 = (bf16[128,512]{1,0:T(8,128)(2,1)S(1)}, bf16[128,512]{1,0:T(8,128)(2,1)S(1)}, u32[]{:S(2)}, u32[]{:S(2)}) collective-permute-start(bf16[128,512]{1,0:T(8,128)(2,1)S(1)} %bitcast.242), channel_id=1, source_target_pairs={{6,0},{0,1},{2,2},{4,3},{7,4},{1,5},{3,6},{5,7},{14,8},{8,9},{10,1... | collective-permute-start | bytes 393224 | tf_op jit(solution)/shard_map/ppermute | solution.py:69
  357.3 8.4 %convolution_bitcast_fusion.1 = f32[1,2048,768]{2,1,0:T(8,128)} fusion(bf16[1024,2048]{1,0:T(8,128)(2,1)} %bitcast_select_fusion, bf16[1024,768]{1,0:T(8,128)(2,1)S(1)} %copy-done.3), kind=kOutput, calls=%fused_computation.53 | convolution fusion | flops 3221225472 | bytes 12058624 | tf_op jit(solution)/shard_map/td,tf->df/dot_general | solution.py:225
  372.7 4.3 fusion.8
  379.4 4.4 %fusion.2 = f32[8,64,512]{2,1,0:T(8,128)} fusion(f32[512,512]{1,0:T(8,128)} %copy-done.14, f32[8,512]{1,0:T(8,128)} %get-tuple-element.43, pred[512,512]{1,0:T(8,128)(4,1)S(1)} %copy-done.23, f32[512,8,64]{0,2,1:T(8,128)S(1)} %bitcast.218), kind=kOutput, calls=%fused_computation.13 | convolution fusion | flops 277872640 | bytes 3424256 | tf_op jit(solution)/shard_map/hts,thp->shp/dot_general | solution.py:261
  385.0 23.3 %all_gather.20 = bf16[16,8,1024]{2,1,0:T(8,128)(2,1)S(1)} all-gather(bf16[1,8,1024]{2,1,0:T(8,128)(2,1)S(1)} %convert_element_type.168), channel_id=1, replica_groups=mesh['seq'=16,'expert'=4,'mp'=2] {'seq'}, dimensions={0}, use_global_device_ids=true | all-gather | bytes 278528 | tf_op jit(solution)/shard_map/all_gather | solution.py:281
  409.3 3.6 fusion.94
  423.8 3.0 copy.248
  426.8 4.0 add.297
  (249 shorter events, 104.6 us)
Async XLA Ops:
  7.2 223.9 %copy-start = (bf16[1,2048,768]{2,1,0:T(8,128)(2,1)S(1)}, bf16[1,2048,768]{2,1,0:T(8,128)(2,1)}, u32[]{:S(2)}) copy-start(bf16[1,2048,768]{2,1,0:T(8,128)(2,1)} %param.18) | copy-start | bytes 9437188
  7.2 107.1 %all-gather.4.cloned.1.call-start = ((), (), s32[]{:S(2)}) async-start(), calls=%async_computation.1 | async-start | bytes 8912896 | tf_op jit(solution)/shard_map/all_gather | solution.py:137
  8.2 24.9 %copy-start.33 = (s32[16,8]{1,0:T(8,128)}, s32[16,8]{1,0:T(8,128)S(1)}, u32[]{:S(2)}) copy-start(s32[16,8]{1,0:T(8,128)S(1)} %reshape.385) | copy-start | bytes 1540
  11.8 25.4 %copy-start.52 = (f32[8]{0:T(128)S(1)}, f32[8]{0:T(128)}, u32[]{:S(2)}) copy-start(f32[8]{0:T(128)} %param.15) | copy-start | bytes 100
  11.9 25.4 %copy-start.42 = (s32[1024]{0:T(1024)S(1)}, s32[1024]{0:T(1024)}, u32[]{:S(2)}) copy-start(s32[1024]{0:T(1024)} %param.16) | copy-start | bytes 12292
  11.9 12.8 %collective-permute-start.3 = (bf16[128,512]{1,0:T(8,128)(2,1)S(1)}, bf16[128,512]{1,0:T(8,128)(2,1)S(1)}, u32[]{:S(2)}, u32[]{:S(2)}) collective-permute-start(bf16[128,512]{1,0:T(8,128)(2,1)S(1)} %bitcast.234), channel_id=1, source_target_pairs={{0,6},{1,0},{2,2},{3,4},{4,7},{5,1},{6,3},{7,5},{8,14},{9,8},{10,1... | collective-permute-start | bytes 393224 | tf_op jit(solution)/shard_map/ppermute | solution.py:53
  18.0 6.7 %collective-permute-start = (bf16[128,512]{1,0:T(8,128)(2,1)S(1)}, bf16[128,512]{1,0:T(8,128)(2,1)S(1)}, u32[]{:S(2)}, u32[]{:S(2)}) collective-permute-start(bf16[128,512]{1,0:T(8,128)(2,1)S(1)} %bitcast.241), channel_id=1, source_target_pairs={{0,0},{1,2},{2,4},{3,6},{4,1},{5,3},{6,5},{7,7},{8,8},{9,10},{10,1... | collective-permute-start | bytes 393224 | tf_op jit(solution)/shard_map/ppermute | solution.py:53
  18.7 7.4 %collective-permute-start.1 = (bf16[128,512]{1,0:T(8,128)(2,1)S(1)}, bf16[128,512]{1,0:T(8,128)(2,1)S(1)}, u32[]{:S(2)}, u32[]{:S(2)}) collective-permute-start(bf16[128,512]{1,0:T(8,128)(2,1)S(1)} %bitcast.244), channel_id=1, source_target_pairs={{0,2},{1,4},{2,6},{3,0},{4,3},{5,5},{6,7},{7,1},{8,10},{9,12},{10,... | collective-permute-start | bytes 393224 | tf_op jit(solution)/shard_map/ppermute | solution.py:53
  22.7 5.1 %collective-permute-start.2 = (bf16[128,512]{1,0:T(8,128)(2,1)S(1)}, bf16[128,512]{1,0:T(8,128)(2,1)S(1)}, u32[]{:S(2)}, u32[]{:S(2)}) collective-permute-start(bf16[128,512]{1,0:T(8,128)(2,1)S(1)} %bitcast.247), channel_id=1, source_target_pairs={{0,4},{1,6},{2,0},{3,2},{4,5},{5,7},{6,1},{7,3},{8,12},{9,14},{10,... | collective-permute-start | bytes 393224 | tf_op jit(solution)/shard_map/ppermute | solution.py:53
  24.7 12.7 %copy-start.48 = (pred[4]{0:T(512)(128)(4,1)}, pred[4]{0:T(512)(128)(4,1)S(1)}, u32[]{:S(2)}) copy-start(pred[4]{0:T(512)(128)(4,1)S(1)} %compare_and_fusion) | copy-start | bytes 16
  24.7 12.7 %copy-start.41 = (s32[1024]{0:T(1024)}, s32[1024]{0:T(1024)S(1)}, u32[]{:S(2)}) copy-start(s32[1024]{0:T(1024)S(1)} %pad_clamp_fusion.2) | copy-start | bytes 12292
  37.2 9.4 %copy-start.18 = (bf16[1024,16]{0,1:T(8,128)(2,1)S(1)}, bf16[1024,16]{0,1:T(8,128)(2,1)}, u32[]{:S(2)}) copy-start(bf16[1024,16]{0,1:T(8,128)(2,1)} %param.13) | copy-start | bytes 98308
  37.2 185.1 %all-gather.6.cloned.1.call-start = ((), (), s32[]{:S(2)}) async-start(), calls=%async_computation.2 | async-start | bytes 8912896 | tf_op jit(solution)/shard_map/all_gather | solution.py:213
  37.3 9.3 %copy-start.43 = (f32[8]{0:T(128)}, f32[8]{0:T(128)S(1)}, u32[]{:S(2)}) copy-start(f32[8]{0:T(128)S(1)} %get-tuple-element.48) | copy-start | bytes 100
  47.4 42.4 %copy-start.17 = (bf16[1024,16]{0,1:T(8,128)(2,1)S(1)}, bf16[1024,16]{0,1:T(8,128)(2,1)}, u32[]{:S(2)}) copy-start(bf16[1024,16]{0,1:T(8,128)(2,1)} %param.14) | copy-start | bytes 98308
  88.3 12.5 %copy-start.22 = (pred[512,512]{1,0:T(8,128)(4,1)}, pred[512,512]{1,0:T(8,128)(4,1)S(1)}, u32[]{:S(2)}) copy-start(pred[512,512]{1,0:T(8,128)(4,1)S(1)} %iota_compare_fusion) | copy-start | bytes 786436
  90.1 10.7 %copy-start.12 = (f32[512,512]{1,0:T(8,128)}, f32[512,512]{1,0:T(8,128)S(1)}, u32[]{:S(2)}) copy-start(f32[512,512]{1,0:T(8,128)S(1)} %fusion.129) | copy-start | bytes 3145732
  125.1 20.5 %copy-start.49 = (pred[4]{0:T(512)(128)(4,1)S(1)}, pred[4]{0:T(512)(128)(4,1)}, u32[]{:S(2)}) copy-start(pred[4]{0:T(512)(128)(4,1)} %copy-done.48) | copy-start | bytes 16
  127.0 12.7 %collective-permute-start.5 = (bf16[128,512]{1,0:T(8,128)(2,1)S(1)}, bf16[128,512]{1,0:T(8,128)(2,1)S(1)}, u32[]{:S(2)}, u32[]{:S(2)}) collective-permute-start(bf16[128,512]{1,0:T(8,128)(2,1)S(1)} %bitcast.245), channel_id=1, source_target_pairs={{0,0},{1,2},{2,4},{3,6},{4,1},{5,3},{6,5},{7,7},{8,8},{9,10},{10,1... | collective-permute-start | bytes 393224 | tf_op jit(solution)/shard_map/ppermute | solution.py:53
  127.7 12.0 %collective-permute-start.6 = (bf16[128,512]{1,0:T(8,128)(2,1)S(1)}, bf16[128,512]{1,0:T(8,128)(2,1)S(1)}, u32[]{:S(2)}, u32[]{:S(2)}) collective-permute-start(bf16[128,512]{1,0:T(8,128)(2,1)S(1)} %bitcast.246), channel_id=1, source_target_pairs={{0,2},{1,4},{2,6},{3,0},{4,3},{5,5},{6,7},{7,1},{8,10},{9,12},{10,... | collective-permute-start | bytes 393224 | tf_op jit(solution)/shard_map/ppermute | solution.py:53
  134.7 5.0 %collective-permute-start.7 = (bf16[128,512]{1,0:T(8,128)(2,1)S(1)}, bf16[128,512]{1,0:T(8,128)(2,1)S(1)}, u32[]{:S(2)}, u32[]{:S(2)}) collective-permute-start(bf16[128,512]{1,0:T(8,128)(2,1)S(1)} %bitcast.248), channel_id=1, source_target_pairs={{0,4},{1,6},{2,0},{3,2},{4,5},{5,7},{6,1},{7,3},{8,12},{9,14},{10,... | collective-permute-start | bytes 393224 | tf_op jit(solution)/shard_map/ppermute | solution.py:53
  135.2 7.1 %collective-permute-start.8 = (bf16[128,512]{1,0:T(8,128)(2,1)S(1)}, bf16[128,512]{1,0:T(8,128)(2,1)S(1)}, u32[]{:S(2)}, u32[]{:S(2)}) collective-permute-start(bf16[128,512]{1,0:T(8,128)(2,1)S(1)} %bitcast.249), channel_id=1, source_target_pairs={{0,6},{1,0},{2,2},{3,4},{4,7},{5,1},{6,3},{7,5},{8,14},{9,8},{10,1... | collective-permute-start | bytes 393224 | tf_op jit(solution)/shard_map/ppermute | solution.py:53
  151.7 192.6 %reduce-scatter.2.cloned.1.call-start = ((), (), s32[]{:S(2)}) async-start(), calls=%async_computation.3 | async-start | bytes 8912896 | tf_op jit(solution)/shard_map/reduce_scatter | solution.py:229
  159.5 75.3 %collective-permute-start.4 = (bf16[1024,768]{1,0:T(8,128)(2,1)}, bf16[1024,768]{1,0:T(8,128)(2,1)}, u32[]{:S(2)}, u32[]{:S(2)}) collective-permute-start(bf16[1024,768]{1,0:T(8,128)(2,1)} %fusion.54), channel_id=1, source_target_pairs={{0,1},{1,0},{2,3},{3,2},{4,5},{5,4},{6,7},{7,6},{8,9},{9,8},{10,11... | collective-permute-start | bytes 4718600 | tf_op jit(solution)/shard_map/ppermute | solution.py:36
  234.5 3.7 collective-permute-start.9
  271.4 85.9 %copy-start.3 = (bf16[1024,768]{1,0:T(8,128)(2,1)S(1)}, bf16[1024,768]{1,0:T(8,128)(2,1)}, u32[]{:S(2)}) copy-start(bf16[1024,768]{1,0:T(8,128)(2,1)} %multiply_convert_fusion.1) | copy-start | bytes 4718596
  346.8 18.9 %collective-permute-start.10 = (bf16[128,512]{1,0:T(8,128)(2,1)S(1)}, bf16[128,512]{1,0:T(8,128)(2,1)S(1)}, u32[]{:S(2)}, u32[]{:S(2)}) collective-permute-start(bf16[128,512]{1,0:T(8,128)(2,1)S(1)} %bitcast.235), channel_id=1, source_target_pairs={{0,0},{2,1},{4,2},{6,3},{1,4},{3,5},{5,6},{7,7},{8,8},{10,9},{12,1... | collective-permute-start | bytes 393224 | tf_op jit(solution)/shard_map/ppermute | solution.py:69
  347.5 18.4 %collective-permute-start.11 = (bf16[128,512]{1,0:T(8,128)(2,1)S(1)}, bf16[128,512]{1,0:T(8,128)(2,1)S(1)}, u32[]{:S(2)}, u32[]{:S(2)}) collective-permute-start(bf16[128,512]{1,0:T(8,128)(2,1)S(1)} %bitcast.237), channel_id=1, source_target_pairs={{2,0},{4,1},{6,2},{0,3},{3,4},{5,5},{7,6},{1,7},{10,8},{12,9},{14,... | collective-permute-start | bytes 393224 | tf_op jit(solution)/shard_map/ppermute | solution.py:69
  351.5 14.6 %collective-permute-start.12 = (bf16[128,512]{1,0:T(8,128)(2,1)S(1)}, bf16[128,512]{1,0:T(8,128)(2,1)S(1)}, u32[]{:S(2)}, u32[]{:S(2)}) collective-permute-start(bf16[128,512]{1,0:T(8,128)(2,1)S(1)} %bitcast.239), channel_id=1, source_target_pairs={{4,0},{6,1},{0,2},{2,3},{5,4},{7,5},{1,6},{3,7},{12,8},{14,9},{8,1... | collective-permute-start | bytes 393224 | tf_op jit(solution)/shard_map/ppermute | solution.py:69
  352.4 14.0 %collective-permute-start.13 = (bf16[128,512]{1,0:T(8,128)(2,1)S(1)}, bf16[128,512]{1,0:T(8,128)(2,1)S(1)}, u32[]{:S(2)}, u32[]{:S(2)}) collective-permute-start(bf16[128,512]{1,0:T(8,128)(2,1)S(1)} %bitcast.242), channel_id=1, source_target_pairs={{6,0},{0,1},{2,2},{4,3},{7,4},{1,5},{3,6},{5,7},{14,8},{8,9},{10,1... | collective-permute-start | bytes 393224 | tf_op jit(solution)/shard_map/ppermute | solution.py:69
  369.6 7.5 %copy-start.2 = (f32[1024,512]{1,0:T(8,128)}, f32[1024,512]{1,0:T(8,128)S(1)}, u32[]{:S(2)}) copy-start(f32[1024,512]{1,0:T(8,128)S(1)} %bitcast_add_fusion) | copy-start | bytes 6291460
  379.4 29.8 %copy-start.15 = (f32[512,512]{1,0:T(8,128)S(1)}, f32[512,512]{1,0:T(8,128)}, u32[]{:S(2)}) copy-start(f32[512,512]{1,0:T(8,128)} %copy-done.14) | copy-start | bytes 3145732
  (39 other events, 139.4 us)
Sparse Core Ops, SparseCore 0:
  37.3 73.3 all-gather.3
  151.8 70.4 all-gather.5
  258.6 85.6 reduce-scatter.1

commit v7 on v6

--- a/solution.py
+++ b/solution.py
@@ -232,6 +232,7 @@
         scatter_dimension=0,
         tiled=True,
     )
+    up_grad, down_grad, back_rows = lax.optimization_barrier((up_grad, down_grad, back_rows))
     returned = give_back(back_rows, exp_index, exp_count, mp_count)
     position = my_slice % exp_count
     chosen_by_shift = jnp.take(chosen, (position + jnp.arange(exp_count)) % exp_count, axis=0)

time: 444 us -> 441 us (level)
  the two profiles are of different devices: /device:TPU:0 before, /device:TPU:32 now
where the time goes in v7:
time: 441 us; the launch traced here: 434 us
  waiting for transfers between devices  150 us (34%)
  matrix products  78.9 us (18%)
  local copies, waits for them, and re-layouts  67.2 us (15%)
  blocking collectives  49.8 us (11%)
  other arithmetic  43.3 us (10%)
  starting transfers between devices  29.6 us (7%)
  between operations  15.5 us (4%)
    reduce_scatter x1, waiting for transfers between devices, per_device(): lax.psum_scatter(spread_rows, 'seq', scatter_dimension=0, tiled=True)  70.7 us
    all_gather x1, waiting for transfers between devices, per_device(): h_all = lax.all_gather(h_block, 'seq', axis=0)  62.3 us
    all_gather x1, blocking collectives, per_device(): lax.all_gather(jnp.concatenate([flat_state, level_lanes], axis=1), 'seq')  26.6 us
    all_gather x1, blocking collectives, per_device(): adjoint_all = lax.all_gather(flat_adjoint.astype(jnp.bfloat16), 'seq')  23.1 us
    ppermute x8, starting transfers between devices, dispatch(): received.append(lax.ppermute(send, ('expert', 'mp'), pairs))  19.5 us
    gather x2, local copies, waits for them, and re-layouts, compact(): jnp.take(blocks, source, axis=0, mode='clip')  12.4 us
    select_n x3, other arithmetic, compact(): jnp.where(used[:, None, None], jnp.take(blocks, source, axis=0, mode='cli...  9.81 us
    ppermute x4, starting transfers between devices, give_back(): received.append(lax.ppermute(send, ('expert', 'mp'), pairs))  9.67 us
  transfers between devices with their start and end apart: 17, of which 9 were waited for; matrix products, arithmetic and copies ran while one was open for 20% of the time, Pallas kernels for 0%

profile of v7, /device:TPU:32, one launch (start us, length us, event | category | flops | bytes accessed | tf_op | source)
XLA Modules:
  0.0 433.8 jit_solution(7215188198076434894)
XLA Ops:
  8.7 2.8 convolution_convert_fusion.2
  11.5 3.3 constant_dynamic-slice_fusion.11
  15.5 5.5 %collective-permute-start.2 = (bf16[128,512]{1,0:T(8,128)(2,1)S(1)}, bf16[128,512]{1,0:T(8,128)(2,1)S(1)}, u32[]{:S(2)}, u32[]{:S(2)}) collective-permute-start(bf16[128,512]{1,0:T(8,128)(2,1)S(1)} %bitcast.241), channel_id=1, source_target_pairs={{0,4},{1,6},{2,0},{3,2},{4,5},{5,7},{6,1},{7,3},{8,12},{9,14},{10,... | collective-permute-start | bytes 393224 | tf_op jit(solution)/shard_map/ppermute | solution.py:53
  25.0 2.9 collective-permute-done.1
  61.2 26.6 %all-gather = f32[128,1152]{1,0:T(8,128)S(1)} all-gather(f32[8,1152]{1,0:T(8,128)S(1)} %pad_maximum_fusion.2), channel_id=2, replica_groups=mesh['seq'=16,'expert'=4,'mp'=2] {'seq'}, dimensions={0}, use_global_device_ids=true | all-gather | bytes 626688 | tf_op jit(solution)/shard_map/all_gather | solution.py:194
  94.6 4.3 fusion.45
  102.2 2.7 fusion.47
  108.3 2.8 maximum_add_fusion
  111.1 2.9 copy.231
  114.9 3.2 add_convert_fusion
  118.1 6.2 %gather_fusion.1 = bf16[8,128,2048]{2,1,0:T(8,128)(2,1)} fusion(bf16[16,128,2048]{2,1,0:T(8,128)(2,1)} %all-gather.4.cloned.1.call-done, s32[1024]{0:T(1024)S(1)} %pad_clamp_fusion.1), kind=kCustom, calls=%fused_computation.3 | custom fusion | bytes 8388640 | tf_op jit(solution)/shard_map/jit(_take)/gather | solution.py:93
  124.3 4.6 %bitcast_select_fusion.1 = bf16[1024,2048]{1,0:T(8,128)(2,1)} fusion(bf16[8,128,2048]{2,1,0:T(8,128)(2,1)} %gather_fusion.1, pred[1024]{0:T(1024)(128)(4,1)S(1)} %broadcast_bitcast_fusion), kind=kLoop, calls=%fused_computation.20 | loop fusion | flops 2097152 | bytes 8389632 | tf_op jit(solution)/shard_map/jit(_where)/select_n | solution.py:93
  131.5 5.1 %collective-permute-start.6 = (bf16[128,512]{1,0:T(8,128)(2,1)S(1)}, bf16[128,512]{1,0:T(8,128)(2,1)S(1)}, u32[]{:S(2)}, u32[]{:S(2)}) collective-permute-start(bf16[128,512]{1,0:T(8,128)(2,1)S(1)} %bitcast.244), channel_id=1, source_target_pairs={{0,4},{1,6},{2,0},{3,2},{4,5},{5,7},{6,1},{7,3},{8,12},{9,14},{10,... | collective-permute-start | bytes 393224 | tf_op jit(solution)/shard_map/ppermute | solution.py:53
  140.5 3.0 collective-permute-done.5
  154.4 7.8 %fusion.54 = bf16[1024,768]{1,0:T(8,128)(2,1)} fusion(bf16[1024,2048]{1,0:T(8,128)(2,1)} %bitcast_select_fusion.1, bf16[1,768,2048]{2,1,0:T(8,128)(2,1)} %param.19), kind=kOutput, calls=%fused_computation.73 | convolution fusion | flops 3222011904 | bytes 8912896 | tf_op jit(solution)/shard_map/td,fd->tf/dot_general | solution.py:221
  162.2 62.3 %all-gather.6.cloned.1.call-done = bf16[16,128,2048]{2,1,0:T(8,128)(2,1)} async-done(((bf16[1,128,2048]{2,1,0:T(8,128)(2,1)}), bf16[16,128,2048]{2,1,0:T(8,128)(2,1)}) %all-gather.6.cloned.1.call-update) | async-done | bytes 8388624 | tf_op jit(solution)/shard_map/all_gather | solution.py:213
  224.4 6.2 %gather_fusion.2 = bf16[8,128,2048]{2,1,0:T(8,128)(2,1)} fusion(bf16[16,128,2048]{2,1,0:T(8,128)(2,1)} %all-gather.6.cloned.1.call-done, s32[1024]{0:T(1024)S(1)} %pad_clamp_fusion.1), kind=kCustom, calls=%fused_computation.4 | custom fusion | bytes 8388640 | tf_op jit(solution)/shard_map/jit(_take)/gather | solution.py:93
  233.2 3.4 fusion.57
  236.9 3.4 collective-permute-done.9
  240.3 5.2 %multiply_convert_fusion.1 = bf16[1024,768]{1,0:T(8,128)(2,1)} fusion(bf16[1024,768]{1,0:T(8,128)(2,1)} %collective-permute-done.8, bf16[1024,768]{1,0:T(8,128)(2,1)} %fusion.54, bf16[1024,768]{1,0:T(8,128)(2,1)S(1)} %collective-permute-done.9, bf16[1024,768]{1,0:T(8,128)(2,1)S(1)} %fusion.57), kind=kLoop, calls=%fused_computation.62 | loop fusion | flops 11796480 | bytes 7864320 | tf_op jit(solution)/shard_map/convert_element_type | solution.py:224
  245.5 3.8 gather_fusion.3
  251.4 9.2 %convolution_convert_fusion = bf16[2048,2048]{1,0:T(8,128)(2,1)} fusion(bf16[2048,768]{1,0:T(8,128)(2,1)S(1)} %bitcast.221, bf16[1,2048,768]{2,1,0:T(8,128)(2,1)S(1)} %copy-done), kind=kOutput, calls=%fused_computation.12 | convolution fusion | flops 6446645248 | bytes 14680064 | tf_op jit(solution)/shard_map/tf,df->td/dot_general | solution.py:227
  264.7 5.5 %fusion.186 = f32[2048,768]{1,0:T(8,128)} fusion(bf16[1024,2048]{1,0:T(8,128)(2,1)S(1)} %bitcast_select_fusion, bf16[1024,768]{1,0:T(8,128)(2,1)S(1)} %copy-done.3), kind=kOutput, calls=%fused_computation.285 | convolution fusion | flops 3221225472 | bytes 12058624 | tf_op jit(solution)/shard_map/td,tf->df/dot_general | solution.py:225
  270.2 5.6 %fusion.60 = f32[768,2048]{1,0:T(8,128)} fusion(bf16[1024,2048]{1,0:T(8,128)(2,1)S(1)} %copy-done.5, bf16[1024,768]{1,0:T(8,128)(2,1)S(1)} %copy-done.12, bf16[1024,768]{1,0:T(8,128)(2,1)S(1)} %copy-done.10), kind=kOutput, calls=%fused_computation.75 | convolution fusion | flops 3227516928 | bytes 13631488 | tf_op jit(solution)/shard_map/tf,td->fd/dot_general | solution.py:219
  275.7 70.7 %reduce-scatter.2.cloned.1.call-done = bf16[128,2048]{1,0:T(8,128)(2,1)} async-done(((bf16[2048,2048]{1,0:T(8,128)(2,1)}), bf16[128,2048]{1,0:T(8,128)(2,1)}) %reduce-scatter.2.cloned.1.call-update) | async-done | bytes 524304 | tf_op jit(solution)/shard_map/reduce_scatter | solution.py:229
  349.7 3.7 collective-permute-start.12
  355.3 3.4 collective-permute-start.10
  370.9 3.4 fusion.8
  381.3 4.0 fusion.2
  394.0 23.1 %all_gather.20 = bf16[16,8,1024]{2,1,0:T(8,128)(2,1)S(1)} all-gather(bf16[1,8,1024]{2,1,0:T(8,128)(2,1)S(1)} %convert_element_type.169), channel_id=1, replica_groups=mesh['seq'=16,'expert'=4,'mp'=2] {'seq'}, dimensions={0}, use_global_device_ids=true | all-gather | bytes 278528 | tf_op jit(solution)/shard_map/all_gather | solution.py:282
  419.8 3.0 copy.248
  422.8 4.0 add.297
  (247 shorter events, 114.9 us)
Async XLA Ops:
  7.2 226.0 %copy-start = (bf16[1,2048,768]{2,1,0:T(8,128)(2,1)S(1)}, bf16[1,2048,768]{2,1,0:T(8,128)(2,1)}, u32[]{:S(2)}) copy-start(bf16[1,2048,768]{2,1,0:T(8,128)(2,1)} %param.18) | copy-start | bytes 9437188
  7.2 110.9 %all-gather.4.cloned.1.call-start = ((), (), s32[]{:S(2)}) async-start(), calls=%async_computation.1 | async-start | bytes 8912896 | tf_op jit(solution)/shard_map/all_gather | solution.py:137
  14.8 10.1 %collective-permute-start.3 = (bf16[128,512]{1,0:T(8,128)(2,1)S(1)}, bf16[128,512]{1,0:T(8,128)(2,1)S(1)}, u32[]{:S(2)}, u32[]{:S(2)}) collective-permute-start(bf16[128,512]{1,0:T(8,128)(2,1)S(1)} %bitcast.240), channel_id=1, source_target_pairs={{0,6},{1,0},{2,2},{3,4},{4,7},{5,1},{6,3},{7,5},{8,14},{9,8},{10,1... | collective-permute-start | bytes 393224 | tf_op jit(solution)/shard_map/ppermute | solution.py:53
  15.5 9.4 %collective-permute-start.2 = (bf16[128,512]{1,0:T(8,128)(2,1)S(1)}, bf16[128,512]{1,0:T(8,128)(2,1)S(1)}, u32[]{:S(2)}, u32[]{:S(2)}) collective-permute-start(bf16[128,512]{1,0:T(8,128)(2,1)S(1)} %bitcast.241), channel_id=1, source_target_pairs={{0,4},{1,6},{2,0},{3,2},{4,5},{5,7},{6,1},{7,3},{8,12},{9,14},{10,... | collective-permute-start | bytes 393224 | tf_op jit(solution)/shard_map/ppermute | solution.py:53
  21.0 6.9 %collective-permute-start.1 = (bf16[128,512]{1,0:T(8,128)(2,1)S(1)}, bf16[128,512]{1,0:T(8,128)(2,1)S(1)}, u32[]{:S(2)}, u32[]{:S(2)}) collective-permute-start(bf16[128,512]{1,0:T(8,128)(2,1)S(1)} %bitcast.242), channel_id=1, source_target_pairs={{0,2},{1,4},{2,6},{3,0},{4,3},{5,5},{6,7},{7,1},{8,10},{9,12},{10,... | collective-permute-start | bytes 393224 | tf_op jit(solution)/shard_map/ppermute | solution.py:53
  23.0 6.3 %collective-permute-start = (bf16[128,512]{1,0:T(8,128)(2,1)S(1)}, bf16[128,512]{1,0:T(8,128)(2,1)S(1)}, u32[]{:S(2)}, u32[]{:S(2)}) collective-permute-start(bf16[128,512]{1,0:T(8,128)(2,1)S(1)} %bitcast.245), channel_id=1, source_target_pairs={{0,0},{1,2},{2,4},{3,6},{4,1},{5,3},{6,5},{7,7},{8,8},{9,10},{10,1... | collective-permute-start | bytes 393224 | tf_op jit(solution)/shard_map/ppermute | solution.py:53
  24.9 9.6 %copy-start.48 = (pred[4]{0:T(512)(128)(4,1)}, pred[4]{0:T(512)(128)(4,1)S(1)}, u32[]{:S(2)}) copy-start(pred[4]{0:T(512)(128)(4,1)S(1)} %compare_and_fusion) | copy-start | bytes 16
  25.0 17.6 %copy-start.39 = (s32[1024]{0:T(1024)}, s32[1024]{0:T(1024)S(1)}, u32[]{:S(2)}) copy-start(s32[1024]{0:T(1024)S(1)} %pad_clamp_fusion.2) | copy-start | bytes 12292
  36.6 10.4 %copy-start.52 = (f32[8]{0:T(128)S(1)}, f32[8]{0:T(128)}, u32[]{:S(2)}) copy-start(f32[8]{0:T(128)} %param.15) | copy-start | bytes 100
  36.6 10.4 %copy-start.42 = (s32[1024]{0:T(1024)S(1)}, s32[1024]{0:T(1024)}, u32[]{:S(2)}) copy-start(s32[1024]{0:T(1024)} %param.16) | copy-start | bytes 12292
  38.7 185.8 %all-gather.6.cloned.1.call-start = ((), (), s32[]{:S(2)}) async-start(), calls=%async_computation.2 | async-start | bytes 8912896 | tf_op jit(solution)/shard_map/all_gather | solution.py:213
  42.6 13.2 %copy-start.18 = (bf16[1024,16]{0,1:T(8,128)(2,1)S(1)}, bf16[1024,16]{0,1:T(8,128)(2,1)}, u32[]{:S(2)}) copy-start(bf16[1024,16]{0,1:T(8,128)(2,1)} %param.13) | copy-start | bytes 98308
  47.0 9.6 %copy-start.43 = (f32[8]{0:T(128)}, f32[8]{0:T(128)S(1)}, u32[]{:S(2)}) copy-start(f32[8]{0:T(128)S(1)} %get-tuple-element.54) | copy-start | bytes 100
  53.9 40.0 %copy-start.17 = (bf16[1024,16]{0,1:T(8,128)(2,1)S(1)}, bf16[1024,16]{0,1:T(8,128)(2,1)}, u32[]{:S(2)}) copy-start(bf16[1024,16]{0,1:T(8,128)(2,1)} %param.14) | copy-start | bytes 98308
  92.4 12.5 %copy-start.22 = (pred[512,512]{1,0:T(8,128)(4,1)}, pred[512,512]{1,0:T(8,128)(4,1)S(1)}, u32[]{:S(2)}) copy-start(pred[512,512]{1,0:T(8,128)(4,1)S(1)} %iota_compare_fusion) | copy-start | bytes 786436
  94.2 10.7 %copy-start.15 = (f32[512,512]{1,0:T(8,128)}, f32[512,512]{1,0:T(8,128)S(1)}, u32[]{:S(2)}) copy-start(f32[512,512]{1,0:T(8,128)S(1)} %fusion.130) | copy-start | bytes 3145732
  128.9 19.3 %copy-start.49 = (pred[4]{0:T(512)(128)(4,1)S(1)}, pred[4]{0:T(512)(128)(4,1)}, u32[]{:S(2)}) copy-start(pred[4]{0:T(512)(128)(4,1)} %copy-done.48) | copy-start | bytes 16
  130.8 9.7 %collective-permute-start.7 = (bf16[128,512]{1,0:T(8,128)(2,1)S(1)}, bf16[128,512]{1,0:T(8,128)(2,1)S(1)}, u32[]{:S(2)}, u32[]{:S(2)}) collective-permute-start(bf16[128,512]{1,0:T(8,128)(2,1)S(1)} %bitcast.243), channel_id=1, source_target_pairs={{0,6},{1,0},{2,2},{3,4},{4,7},{5,1},{6,3},{7,5},{8,14},{9,8},{10,1... | collective-permute-start | bytes 393224 | tf_op jit(solution)/shard_map/ppermute | solution.py:53
  131.5 9.0 %collective-permute-start.6 = (bf16[128,512]{1,0:T(8,128)(2,1)S(1)}, bf16[128,512]{1,0:T(8,128)(2,1)S(1)}, u32[]{:S(2)}, u32[]{:S(2)}) collective-permute-start(bf16[128,512]{1,0:T(8,128)(2,1)S(1)} %bitcast.244), channel_id=1, source_target_pairs={{0,4},{1,6},{2,0},{3,2},{4,5},{5,7},{6,1},{7,3},{8,12},{9,14},{10,... | collective-permute-start | bytes 393224 | tf_op jit(solution)/shard_map/ppermute | solution.py:53
  136.6 6.9 %collective-permute-start.5 = (bf16[128,512]{1,0:T(8,128)(2,1)S(1)}, bf16[128,512]{1,0:T(8,128)(2,1)S(1)}, u32[]{:S(2)}, u32[]{:S(2)}) collective-permute-start(bf16[128,512]{1,0:T(8,128)(2,1)S(1)} %bitcast.246), channel_id=1, source_target_pairs={{0,2},{1,4},{2,6},{3,0},{4,3},{5,5},{6,7},{7,1},{8,10},{9,12},{10,... | collective-permute-start | bytes 393224 | tf_op jit(solution)/shard_map/ppermute | solution.py:53
  138.6 6.3 %collective-permute-start.4 = (bf16[128,512]{1,0:T(8,128)(2,1)S(1)}, bf16[128,512]{1,0:T(8,128)(2,1)S(1)}, u32[]{:S(2)}, u32[]{:S(2)}) collective-permute-start(bf16[128,512]{1,0:T(8,128)(2,1)S(1)} %bitcast.247), channel_id=1, source_target_pairs={{0,0},{1,2},{2,4},{3,6},{4,1},{5,3},{6,5},{7,7},{8,8},{9,10},{10,1... | collective-permute-start | bytes 393224 | tf_op jit(solution)/shard_map/ppermute | solution.py:53
  154.3 192.1 %reduce-scatter.2.cloned.1.call-start = ((), (), s32[]{:S(2)}) async-start(), calls=%async_computation.3 | async-start | bytes 8912896 | tf_op jit(solution)/shard_map/reduce_scatter | solution.py:229
  162.2 74.7 %collective-permute-start.8 = (bf16[1024,768]{1,0:T(8,128)(2,1)}, bf16[1024,768]{1,0:T(8,128)(2,1)}, u32[]{:S(2)}, u32[]{:S(2)}) collective-permute-start(bf16[1024,768]{1,0:T(8,128)(2,1)} %fusion.54), channel_id=1, source_target_pairs={{0,1},{1,0},{2,3},{3,2},{4,5},{5,4},{6,7},{7,6},{8,9},{9,8},{10,11... | collective-permute-start | bytes 4718600 | tf_op jit(solution)/shard_map/ppermute | solution.py:36
  236.6 3.7 collective-permute-start.9
  349.0 10.4 %collective-permute-start.13 = (bf16[128,512]{1,0:T(8,128)(2,1)S(1)}, bf16[128,512]{1,0:T(8,128)(2,1)S(1)}, u32[]{:S(2)}, u32[]{:S(2)}) collective-permute-start(bf16[128,512]{1,0:T(8,128)(2,1)S(1)} %bitcast.232), channel_id=1, source_target_pairs={{6,0},{0,1},{2,2},{4,3},{7,4},{1,5},{3,6},{5,7},{14,8},{8,9},{10,1... | collective-permute-start | bytes 393224 | tf_op jit(solution)/shard_map/ppermute | solution.py:69
  349.7 9.9 %collective-permute-start.12 = (bf16[128,512]{1,0:T(8,128)(2,1)S(1)}, bf16[128,512]{1,0:T(8,128)(2,1)S(1)}, u32[]{:S(2)}, u32[]{:S(2)}) collective-permute-start(bf16[128,512]{1,0:T(8,128)(2,1)S(1)} %bitcast.234), channel_id=1, source_target_pairs={{4,0},{6,1},{0,2},{2,3},{5,4},{7,5},{1,6},{3,7},{12,8},{14,9},{8,1... | collective-permute-start | bytes 393224 | tf_op jit(solution)/shard_map/ppermute | solution.py:69
  353.4 8.4 %collective-permute-start.11 = (bf16[128,512]{1,0:T(8,128)(2,1)S(1)}, bf16[128,512]{1,0:T(8,128)(2,1)S(1)}, u32[]{:S(2)}, u32[]{:S(2)}) collective-permute-start(bf16[128,512]{1,0:T(8,128)(2,1)S(1)} %bitcast.236), channel_id=1, source_target_pairs={{2,0},{4,1},{6,2},{0,3},{3,4},{5,5},{7,6},{1,7},{10,8},{12,9},{14,... | collective-permute-start | bytes 393224 | tf_op jit(solution)/shard_map/ppermute | solution.py:69
  355.3 9.2 %collective-permute-start.10 = (bf16[128,512]{1,0:T(8,128)(2,1)S(1)}, bf16[128,512]{1,0:T(8,128)(2,1)S(1)}, u32[]{:S(2)}, u32[]{:S(2)}) collective-permute-start(bf16[128,512]{1,0:T(8,128)(2,1)S(1)} %bitcast.238), channel_id=1, source_target_pairs={{0,0},{2,1},{4,2},{6,3},{1,4},{3,5},{5,6},{7,7},{8,8},{10,9},{12,1... | collective-permute-start | bytes 393224 | tf_op jit(solution)/shard_map/ppermute | solution.py:69
  390.2 26.9 %copy-start.32 = (f32[16,8]{1,0:T(8,128)S(1)}, f32[16,8]{1,0:T(8,128)}, u32[]{:S(2)}) copy-start(f32[16,8]{1,0:T(8,128)} %exponential_select_fusion) | copy-start | bytes 1540
  390.2 27.2 %copy-start.30 = (f32[1024,8]{0,1:T(8,128)S(1)}, f32[1024,8]{0,1:T(8,128)}, u32[]{:S(2)}) copy-start(f32[1024,8]{0,1:T(8,128)} %get-tuple-element.42) | copy-start | bytes 98308
  390.2 27.2 %copy-start.45 = (f32[8]{0:T(128)S(1)}, f32[8]{0:T(128)}, u32[]{:S(2)}) copy-start(f32[8]{0:T(128)} %copy-done.43) | copy-start | bytes 100
  419.8 7.0 %copy-start.1 = (bf16[1,2048,768]{2,1,0:T(8,128)(2,1)S(1)}, bf16[1,2048,768]{2,1,0:T(8,128)(2,1)}, u32[]{:S(2)}) copy-start(bf16[1,2048,768]{2,1,0:T(8,128)(2,1)} %param.18) | copy-start | bytes 9437188
  (38 other events, 137.2 us)
Sparse Core Ops, SparseCore 0:
  38.8 74.8 all-gather.3
  154.5 69.9 all-gather.5
  260.7 85.6 reduce-scatter.1

commit v8 on v7

--- a/solution.py
+++ b/solution.py
@@ -140,7 +140,6 @@
     select = ((slot_of[None, :] == jnp.arange(slot_total)[:, None]) & present[None, :]).astype(
         jnp.bfloat16
     )
-    g_rows = compact(select, g_all, half_width)
     input_scale = jnp.sqrt(1.0 - jnp.exp(-2.0 * head_decay_speed))
     cum_level = jnp.cumsum(
         -head_decay_speed[None, :]
@@ -202,7 +201,7 @@
     mixed_out = (activations.astype(jnp.float32) + outputs.reshape(tokens, slice_width)).astype(
         jnp.bfloat16
     )
-    g_rows, mixed_out = lax.optimization_barrier((g_rows, mixed_out))
+    g_all, mixed_out = lax.optimization_barrier((g_all, mixed_out))
     h_pick = jnp.einsum(
         "eb,brf->erf",
         chosen,
@@ -211,15 +210,17 @@
     ).astype(jnp.bfloat16)
     h_block = dispatch(h_pick, exp_index, exp_count, mp_count, my_slice)
     h_all = lax.all_gather(h_block, "seq", axis=0)
+    g_rows = compact(select, g_all, half_width)
+    down_local = expert_down_weight[0]
+    act_grad = mp_sum(
+        jnp.einsum("td,fd->tf", g_rows, down_local, preferred_element_type=jnp.float32)
+    )
+    g_rows, act_grad, h_all = lax.optimization_barrier((g_rows, act_grad, h_all))
     x_rows = compact(select, h_all, half_width)
     up_local = expert_up_weight[0]
-    down_local = expert_down_weight[0]
     pre_act = mp_sum(jnp.dot(x_rows, up_local, preferred_element_type=jnp.float32))
     activation = jax.nn.silu(pre_act).astype(jnp.bfloat16)
     down_grad = jnp.einsum("tf,td->fd", activation, g_rows, preferred_element_type=jnp.float32)
-    act_grad = mp_sum(
-        jnp.einsum("td,fd->tf", g_rows, down_local, preferred_element_type=jnp.float32)
-    )
     sigmoid_pre = jax.nn.sigmoid(pre_act)
     pre_grad = (act_grad * sigmoid_pre * (1.0 + pre_act * (1.0 - sigmoid_pre))).astype(jnp.bfloat16)
     up_grad = jnp.einsum("td,tf->df", x_rows, pre_grad, preferred_element_type=jnp.float32)

time: 441 us -> 425 us (0.964)
  waiting for transfers between devices: 150 us -> 138 us
    all_gather x1, waiting for transfers between devices: 62.3 us -> 50.3 us  [per_device(): h_all = lax.all_gather(h_block, 'seq', axis=0)]
    select_n x3 -> x4, other arithmetic: 9.81 us -> 10.9 us  [compact(): jnp.where(used[:, None, None], jnp.take(blocks, source, axis=0, mode='cli...]
  transfers between devices with their start and end apart: 17 -> 17, of which waited for: 9 -> 10; matrix products, arithmetic and copies ran while one was open for 20% -> 20% of each run, Pallas kernels for 0% -> 0%
where the time goes in v8:
time: 425 us; the launch traced here: 419 us
  waiting for transfers between devices  138 us (32%)
  matrix products  75.6 us (18%)
  local copies, waits for them, and re-layouts  67.3 us (16%)
  blocking collectives  49.7 us (12%)
  other arithmetic  43.1 us (10%)
  starting transfers between devices  29.5 us (7%)
  between operations  15.5 us (4%)
    reduce_scatter x1, waiting for transfers between devices, per_device(): lax.psum_scatter(spread_rows, 'seq', scatter_dimension=0, tiled=True)  70.5 us
    all_gather x1, waiting for transfers between devices, per_device(): h_all = lax.all_gather(h_block, 'seq', axis=0)  50.3 us
    all_gather x1, blocking collectives, per_device(): lax.all_gather(jnp.concatenate([flat_state, level_lanes], axis=1), 'seq')  26.6 us
    all_gather x1, blocking collectives, per_device(): adjoint_all = lax.all_gather(flat_adjoint.astype(jnp.bfloat16), 'seq')  23.1 us
    ppermute x8, starting transfers between devices, dispatch(): received.append(lax.ppermute(send, ('expert', 'mp'), pairs))  19.4 us
    gather x2, local copies, waits for them, and re-layouts, compact(): jnp.take(blocks, source, axis=0, mode='clip')  12.4 us
    select_n x4, other arithmetic, compact(): jnp.where(used[:, None, None], jnp.take(blocks, source, axis=0, mode='cli...  10.9 us
    ppermute x4, starting transfers between devices, give_back(): received.append(lax.ppermute(send, ('expert', 'mp'), pairs))  9.6 us
  transfers between devices with their start and end apart: 17, of which 10 were waited for; matrix products, arithmetic and copies ran while one was open for 20% of the time, Pallas kernels for 0%

profile of v8, /device:TPU:32, one launch (start us, length us, event | category | flops | bytes accessed | tf_op | source)
XLA Modules:
  0.0 418.6 jit_solution(11156837047288317723)
XLA Ops:
  8.8 2.8 convolution_convert_fusion.2
  11.6 3.3 constant_dynamic-slice_fusion.11
  15.6 5.5 %collective-permute-start.2 = (bf16[128,512]{1,0:T(8,128)(2,1)S(1)}, bf16[128,512]{1,0:T(8,128)(2,1)S(1)}, u32[]{:S(2)}, u32[]{:S(2)}) collective-permute-start(bf16[128,512]{1,0:T(8,128)(2,1)S(1)} %bitcast.243), channel_id=1, source_target_pairs={{0,4},{1,6},{2,0},{3,2},{4,5},{5,7},{6,1},{7,3},{8,12},{9,14},{10,... | collective-permute-start | bytes 393224 | tf_op jit(solution)/shard_map/ppermute | solution.py:53
  25.1 2.9 collective-permute-done.1
  59.9 26.6 %all-gather = f32[128,1152]{1,0:T(8,128)S(1)} all-gather(f32[8,1152]{1,0:T(8,128)S(1)} %pad_maximum_fusion.2), channel_id=2, replica_groups=mesh['seq'=16,'expert'=4,'mp'=2] {'seq'}, dimensions={0}, use_global_device_ids=true | all-gather | bytes 626688 | tf_op jit(solution)/shard_map/all_gather | solution.py:193
  93.2 4.2 %fusion.45 = f32[8,512,64]{1,2,0:T(8,128)S(1)} fusion(bf16[512,8,64]{0,2,1:T(8,128)(2,1)} %bitcast.230, f32[512,512]{1,0:T(8,128)S(1)} %fusion.137, f32[8,512]{1,0:T(8,128)} %get-tuple-element.55, pred[512,512]{1,0:T(8,128)(4,1)S(1)} %iota_compare_fusion), kind=kOutput, calls=%fused_computation.54 | convolution fusion | flops 283115520 | bytes 2899968 | tf_op jit(solution)/shard_map/hts,shp->thp/dot_general | solution.py:175
  100.7 2.7 fusion.47
  106.8 2.8 maximum_add_fusion
  109.6 2.9 copy.232
  112.5 3.2 add_convert_fusion
  119.5 4.9 %collective-permute-start.7 = (bf16[128,512]{1,0:T(8,128)(2,1)S(1)}, bf16[128,512]{1,0:T(8,128)(2,1)S(1)}, u32[]{:S(2)}, u32[]{:S(2)}) collective-permute-start(bf16[128,512]{1,0:T(8,128)(2,1)S(1)} %bitcast.246), channel_id=1, source_target_pairs={{0,4},{1,6},{2,0},{3,2},{4,5},{5,7},{6,1},{7,3},{8,12},{9,14},{10,... | collective-permute-start | bytes 393224 | tf_op jit(solution)/shard_map/ppermute | solution.py:53
  128.4 3.0 collective-permute-done.6
  143.4 6.2 %gather_fusion.1 = bf16[8,128,2048]{2,1,0:T(8,128)(2,1)} fusion(bf16[16,128,2048]{2,1,0:T(8,128)(2,1)} %all-gather.4.cloned.1.call-done, s32[1024]{0:T(1024)S(1)} %pad_clamp_fusion.1), kind=kCustom, calls=%fused_computation.3 | custom fusion | bytes 8388640 | tf_op jit(solution)/shard_map/jit(_take)/gather | solution.py:93
  149.6 2.9 broadcast_select_fusion.1
  153.1 3.5 fusion.54
  156.7 2.8 bitcast_select_fusion.1
  162.1 50.3 %all-gather.6.cloned.1.call-done = bf16[16,128,2048]{2,1,0:T(8,128)(2,1)} async-done(((bf16[1,128,2048]{2,1,0:T(8,128)(2,1)}), bf16[16,128,2048]{2,1,0:T(8,128)(2,1)}) %all-gather.6.cloned.1.call-update) | async-done | bytes 8388624 | tf_op jit(solution)/shard_map/all_gather | solution.py:212
  212.3 6.2 %gather_fusion.2 = bf16[8,128,2048]{2,1,0:T(8,128)(2,1)} fusion(bf16[16,128,2048]{2,1,0:T(8,128)(2,1)} %all-gather.6.cloned.1.call-done, s32[1024]{0:T(1024)S(1)} %pad_clamp_fusion.1), kind=kCustom, calls=%fused_computation.4 | custom fusion | bytes 8388640 | tf_op jit(solution)/shard_map/jit(_take)/gather | solution.py:93
  221.1 3.4 fusion.57
  224.8 3.4 collective-permute-done.9
  230.6 3.8 gather_fusion.3
  236.6 9.0 %convolution_convert_fusion = bf16[2048,2048]{1,0:T(8,128)(2,1)} fusion(bf16[2048,768]{1,0:T(8,128)(2,1)S(1)} %bitcast.223, bf16[1,2048,768]{2,1,0:T(8,128)(2,1)S(1)} %copy-done), kind=kOutput, calls=%fused_computation.12 | convolution fusion | flops 6446645248 | bytes 14680064 | tf_op jit(solution)/shard_map/tf,df->td/dot_general | solution.py:228
  249.7 5.5 %fusion.186 = f32[2048,768]{1,0:T(8,128)} fusion(bf16[1024,2048]{1,0:T(8,128)(2,1)S(1)} %bitcast_select_fusion, bf16[1024,768]{1,0:T(8,128)(2,1)S(1)} %copy-done.4), kind=kOutput, calls=%fused_computation.287 | convolution fusion | flops 3221225472 | bytes 12058624 | tf_op jit(solution)/shard_map/td,tf->df/dot_general | solution.py:226
  255.2 5.6 %fusion.60 = f32[768,2048]{1,0:T(8,128)} fusion(bf16[1024,2048]{1,0:T(8,128)(2,1)S(1)} %copy-done.7, bf16[1024,768]{1,0:T(8,128)(2,1)S(1)} %copy-done.13, bf16[1024,768]{1,0:T(8,128)(2,1)S(1)} %copy-done.11), kind=kOutput, calls=%fused_computation.77 | convolution fusion | flops 3227516928 | bytes 13631488 | tf_op jit(solution)/shard_map/tf,td->fd/dot_general | solution.py:223
  260.7 70.5 %reduce-scatter.2.cloned.1.call-done = bf16[128,2048]{1,0:T(8,128)(2,1)} async-done(((bf16[2048,2048]{1,0:T(8,128)(2,1)}), bf16[128,2048]{1,0:T(8,128)(2,1)}) %reduce-scatter.2.cloned.1.call-update) | async-done | bytes 524304 | tf_op jit(solution)/shard_map/reduce_scatter | solution.py:230
  334.5 3.7 collective-permute-start.12
  340.1 3.3 collective-permute-start.10
  355.7 3.4 fusion.8
  366.1 4.0 fusion.2
  378.8 23.1 %all_gather.20 = bf16[16,8,1024]{2,1,0:T(8,128)(2,1)S(1)} all-gather(bf16[1,8,1024]{2,1,0:T(8,128)(2,1)S(1)} %convert_element_type.169), channel_id=1, replica_groups=mesh['seq'=16,'expert'=4,'mp'=2] {'seq'}, dimensions={0}, use_global_device_ids=true | all-gather | bytes 278528 | tf_op jit(solution)/shard_map/all_gather | solution.py:283
  404.6 3.0 copy.249
  407.6 4.0 add.297
  (251 shorter events, 120.8 us)
Async XLA Ops:
  7.2 213.9 %copy-start = (bf16[1,2048,768]{2,1,0:T(8,128)(2,1)S(1)}, bf16[1,2048,768]{2,1,0:T(8,128)(2,1)}, u32[]{:S(2)}) copy-start(bf16[1,2048,768]{2,1,0:T(8,128)(2,1)} %param.18) | copy-start | bytes 9437188
  7.2 108.5 %all-gather.4.cloned.1.call-start = ((), (), s32[]{:S(2)}) async-start(), calls=%async_computation.1 | async-start | bytes 8912896 | tf_op jit(solution)/shard_map/all_gather | solution.py:137
  8.2 26.4 %copy-start.34 = (s32[16,8]{1,0:T(8,128)}, s32[16,8]{1,0:T(8,128)S(1)}, u32[]{:S(2)}) copy-start(s32[16,8]{1,0:T(8,128)S(1)} %reshape.415) | copy-start | bytes 1540
  14.9 10.1 %collective-permute-start.3 = (bf16[128,512]{1,0:T(8,128)(2,1)S(1)}, bf16[128,512]{1,0:T(8,128)(2,1)S(1)}, u32[]{:S(2)}, u32[]{:S(2)}) collective-permute-start(bf16[128,512]{1,0:T(8,128)(2,1)S(1)} %bitcast.242), channel_id=1, source_target_pairs={{0,6},{1,0},{2,2},{3,4},{4,7},{5,1},{6,3},{7,5},{8,14},{9,8},{10,1... | collective-permute-start | bytes 393224 | tf_op jit(solution)/shard_map/ppermute | solution.py:53
  15.6 9.4 %collective-permute-start.2 = (bf16[128,512]{1,0:T(8,128)(2,1)S(1)}, bf16[128,512]{1,0:T(8,128)(2,1)S(1)}, u32[]{:S(2)}, u32[]{:S(2)}) collective-permute-start(bf16[128,512]{1,0:T(8,128)(2,1)S(1)} %bitcast.243), channel_id=1, source_target_pairs={{0,4},{1,6},{2,0},{3,2},{4,5},{5,7},{6,1},{7,3},{8,12},{9,14},{10,... | collective-permute-start | bytes 393224 | tf_op jit(solution)/shard_map/ppermute | solution.py:53
  21.1 6.9 %collective-permute-start.1 = (bf16[128,512]{1,0:T(8,128)(2,1)S(1)}, bf16[128,512]{1,0:T(8,128)(2,1)S(1)}, u32[]{:S(2)}, u32[]{:S(2)}) collective-permute-start(bf16[128,512]{1,0:T(8,128)(2,1)S(1)} %bitcast.244), channel_id=1, source_target_pairs={{0,2},{1,4},{2,6},{3,0},{4,3},{5,5},{6,7},{7,1},{8,10},{9,12},{10,... | collective-permute-start | bytes 393224 | tf_op jit(solution)/shard_map/ppermute | solution.py:53
  23.1 6.3 %collective-permute-start = (bf16[128,512]{1,0:T(8,128)(2,1)S(1)}, bf16[128,512]{1,0:T(8,128)(2,1)S(1)}, u32[]{:S(2)}, u32[]{:S(2)}) collective-permute-start(bf16[128,512]{1,0:T(8,128)(2,1)S(1)} %bitcast.247), channel_id=1, source_target_pairs={{0,0},{1,2},{2,4},{3,6},{4,1},{5,3},{6,5},{7,7},{8,8},{9,10},{10,1... | collective-permute-start | bytes 393224 | tf_op jit(solution)/shard_map/ppermute | solution.py:53
  25.0 16.3 %copy-start.48 = (pred[4]{0:T(512)(128)(4,1)}, pred[4]{0:T(512)(128)(4,1)S(1)}, u32[]{:S(2)}) copy-start(pred[4]{0:T(512)(128)(4,1)S(1)} %compare_and_fusion) | copy-start | bytes 16
  25.1 16.3 %copy-start.41 = (s32[1024]{0:T(1024)}, s32[1024]{0:T(1024)S(1)}, u32[]{:S(2)}) copy-start(s32[1024]{0:T(1024)S(1)} %pad_clamp_fusion.2) | copy-start | bytes 12292
  36.6 9.1 %copy-start.42 = (s32[1024]{0:T(1024)S(1)}, s32[1024]{0:T(1024)}, u32[]{:S(2)}) copy-start(s32[1024]{0:T(1024)} %param.16) | copy-start | bytes 12292
  38.7 173.6 %all-gather.6.cloned.1.call-start = ((), (), s32[]{:S(2)}) async-start(), calls=%async_computation.2 | async-start | bytes 8912896 | tf_op jit(solution)/shard_map/all_gather | solution.py:212
  41.4 13.2 %copy-start.19 = (bf16[1024,16]{0,1:T(8,128)(2,1)S(1)}, bf16[1024,16]{0,1:T(8,128)(2,1)}, u32[]{:S(2)}) copy-start(bf16[1024,16]{0,1:T(8,128)(2,1)} %param.13) | copy-start | bytes 98308
  45.7 9.6 %copy-start.43 = (f32[8]{0:T(128)}, f32[8]{0:T(128)S(1)}, u32[]{:S(2)}) copy-start(f32[8]{0:T(128)S(1)} %get-tuple-element.60) | copy-start | bytes 100
  52.6 39.8 %copy-start.18 = (bf16[1024,16]{0,1:T(8,128)(2,1)S(1)}, bf16[1024,16]{0,1:T(8,128)(2,1)}, u32[]{:S(2)}) copy-start(bf16[1024,16]{0,1:T(8,128)(2,1)} %param.14) | copy-start | bytes 98308
  91.0 12.5 %copy-start.23 = (pred[512,512]{1,0:T(8,128)(4,1)}, pred[512,512]{1,0:T(8,128)(4,1)S(1)}, u32[]{:S(2)}) copy-start(pred[512,512]{1,0:T(8,128)(4,1)S(1)} %iota_compare_fusion) | copy-start | bytes 786436
  92.8 10.7 %copy-start.16 = (f32[512,512]{1,0:T(8,128)}, f32[512,512]{1,0:T(8,128)S(1)}, u32[]{:S(2)}) copy-start(f32[512,512]{1,0:T(8,128)S(1)} %fusion.130) | copy-start | bytes 3145732
  115.7 20.4 %copy-start.49 = (pred[4]{0:T(512)(128)(4,1)S(1)}, pred[4]{0:T(512)(128)(4,1)}, u32[]{:S(2)}) copy-start(pred[4]{0:T(512)(128)(4,1)} %copy-done.48) | copy-start | bytes 16
  118.8 23.5 %copy-start.35 = (s32[16,8]{1,0:T(8,128)S(1)}, s32[16,8]{1,0:T(8,128)}, u32[]{:S(2)}) copy-start(s32[16,8]{1,0:T(8,128)} %copy-done.34) | copy-start | bytes 1540
  118.8 9.6 %collective-permute-start.8 = (bf16[128,512]{1,0:T(8,128)(2,1)S(1)}, bf16[128,512]{1,0:T(8,128)(2,1)S(1)}, u32[]{:S(2)}, u32[]{:S(2)}) collective-permute-start(bf16[128,512]{1,0:T(8,128)(2,1)S(1)} %bitcast.245), channel_id=1, source_target_pairs={{0,6},{1,0},{2,2},{3,4},{4,7},{5,1},{6,3},{7,5},{8,14},{9,8},{10,1... | collective-permute-start | bytes 393224 | tf_op jit(solution)/shard_map/ppermute | solution.py:53
  119.5 8.9 %collective-permute-start.7 = (bf16[128,512]{1,0:T(8,128)(2,1)S(1)}, bf16[128,512]{1,0:T(8,128)(2,1)S(1)}, u32[]{:S(2)}, u32[]{:S(2)}) collective-permute-start(bf16[128,512]{1,0:T(8,128)(2,1)S(1)} %bitcast.246), channel_id=1, source_target_pairs={{0,4},{1,6},{2,0},{3,2},{4,5},{5,7},{6,1},{7,3},{8,12},{9,14},{10,... | collective-permute-start | bytes 393224 | tf_op jit(solution)/shard_map/ppermute | solution.py:53
  124.5 6.9 %collective-permute-start.6 = (bf16[128,512]{1,0:T(8,128)(2,1)S(1)}, bf16[128,512]{1,0:T(8,128)(2,1)S(1)}, u32[]{:S(2)}, u32[]{:S(2)}) collective-permute-start(bf16[128,512]{1,0:T(8,128)(2,1)S(1)} %bitcast.248), channel_id=1, source_target_pairs={{0,2},{1,4},{2,6},{3,0},{4,3},{5,5},{6,7},{7,1},{8,10},{9,12},{10,... | collective-permute-start | bytes 393224 | tf_op jit(solution)/shard_map/ppermute | solution.py:53
  126.4 6.3 %collective-permute-start.5 = (bf16[128,512]{1,0:T(8,128)(2,1)S(1)}, bf16[128,512]{1,0:T(8,128)(2,1)S(1)}, u32[]{:S(2)}, u32[]{:S(2)}) collective-permute-start(bf16[128,512]{1,0:T(8,128)(2,1)S(1)} %bitcast.249), channel_id=1, source_target_pairs={{0,0},{1,2},{2,4},{3,6},{4,1},{5,3},{6,5},{7,7},{8,8},{9,10},{10,1... | collective-permute-start | bytes 393224 | tf_op jit(solution)/shard_map/ppermute | solution.py:53
  142.2 189.0 %reduce-scatter.2.cloned.1.call-start = ((), (), s32[]{:S(2)}) async-start(), calls=%async_computation.3 | async-start | bytes 8912896 | tf_op jit(solution)/shard_map/reduce_scatter | solution.py:230
  156.6 3.5 collective-permute-start.4
  224.5 3.7 collective-permute-start.9
  333.8 10.3 %collective-permute-start.13 = (bf16[128,512]{1,0:T(8,128)(2,1)S(1)}, bf16[128,512]{1,0:T(8,128)(2,1)S(1)}, u32[]{:S(2)}, u32[]{:S(2)}) collective-permute-start(bf16[128,512]{1,0:T(8,128)(2,1)S(1)} %bitcast.234), channel_id=1, source_target_pairs={{6,0},{0,1},{2,2},{4,3},{7,4},{1,5},{3,6},{5,7},{14,8},{8,9},{10,1... | collective-permute-start | bytes 393224 | tf_op jit(solution)/shard_map/ppermute | solution.py:69
  334.5 9.8 %collective-permute-start.12 = (bf16[128,512]{1,0:T(8,128)(2,1)S(1)}, bf16[128,512]{1,0:T(8,128)(2,1)S(1)}, u32[]{:S(2)}, u32[]{:S(2)}) collective-permute-start(bf16[128,512]{1,0:T(8,128)(2,1)S(1)} %bitcast.236), channel_id=1, source_target_pairs={{4,0},{6,1},{0,2},{2,3},{5,4},{7,5},{1,6},{3,7},{12,8},{14,9},{8,1... | collective-permute-start | bytes 393224 | tf_op jit(solution)/shard_map/ppermute | solution.py:69
  338.2 8.4 %collective-permute-start.11 = (bf16[128,512]{1,0:T(8,128)(2,1)S(1)}, bf16[128,512]{1,0:T(8,128)(2,1)S(1)}, u32[]{:S(2)}, u32[]{:S(2)}) collective-permute-start(bf16[128,512]{1,0:T(8,128)(2,1)S(1)} %bitcast.238), channel_id=1, source_target_pairs={{2,0},{4,1},{6,2},{0,3},{3,4},{5,5},{7,6},{1,7},{10,8},{12,9},{14,... | collective-permute-start | bytes 393224 | tf_op jit(solution)/shard_map/ppermute | solution.py:69
  340.1 9.2 %collective-permute-start.10 = (bf16[128,512]{1,0:T(8,128)(2,1)S(1)}, bf16[128,512]{1,0:T(8,128)(2,1)S(1)}, u32[]{:S(2)}, u32[]{:S(2)}) collective-permute-start(bf16[128,512]{1,0:T(8,128)(2,1)S(1)} %bitcast.240), channel_id=1, source_target_pairs={{0,0},{2,1},{4,2},{6,3},{1,4},{3,5},{5,6},{7,7},{8,8},{10,9},{12,1... | collective-permute-start | bytes 393224 | tf_op jit(solution)/shard_map/ppermute | solution.py:69
  375.0 26.9 %copy-start.33 = (f32[16,8]{1,0:T(8,128)S(1)}, f32[16,8]{1,0:T(8,128)}, u32[]{:S(2)}) copy-start(f32[16,8]{1,0:T(8,128)} %exponential_select_fusion) | copy-start | bytes 1540
  375.0 27.2 %copy-start.31 = (f32[1024,8]{0,1:T(8,128)S(1)}, f32[1024,8]{0,1:T(8,128)}, u32[]{:S(2)}) copy-start(f32[1024,8]{0,1:T(8,128)} %get-tuple-element.48) | copy-start | bytes 98308
  375.0 27.2 %copy-start.45 = (f32[8]{0:T(128)S(1)}, f32[8]{0:T(128)}, u32[]{:S(2)}) copy-start(f32[8]{0:T(128)} %copy-done.43) | copy-start | bytes 100
  (39 other events, 152.0 us)
Sparse Core Ops, SparseCore 0:
  38.9 74.7 all-gather.3
  142.3 69.9 all-gather.5
  245.8 85.3 reduce-scatter.1

commit v9 on v8

--- a/solution.py
+++ b/solution.py
@@ -25,6 +25,26 @@
     exponent = jnp.sum(jnp.where(between[:, :, None], level_all[None], 0.0), axis=1)
     weight = jnp.where(valid[:, None], jnp.exp(exponent), 0.0)
     return jnp.sum(weight[:, :, None] * values_all.astype(jnp.float32), axis=0)
+
+
+def torus_gather(value, count):
+    side = 4
+    if count != side * side:
+        return lax.all_gather(value, "seq")
+    own = lax.axis_index("seq")
+    row, col = own // side, own % side
+    steps = jnp.arange(side)
+    got = [value]
+    for shift in range(1, side):
+        pairs = [(r * side + c, r * side + (c + shift) % side) for r in range(side) for c in range(side)]
+        got.append(lax.ppermute(value, "seq", pairs))
+    line = jnp.take(jnp.stack(got), (col - steps) % side, axis=0)
+    got = [line]
+    for shift in range(1, side):
+        pairs = [(r * side + c, ((r + shift) % side) * side + c) for r in range(side) for c in range(side)]
+        got.append(lax.ppermute(line, "seq", pairs))
+    whole = jnp.take(jnp.stack(got), (row - steps) % side, axis=0)
+    return whole.reshape((count,) + value.shape)
 
 
 def mp_sum(part):
@@ -280,7 +300,7 @@
             precision=highest,
         )
     flat_adjoint = adjoint.reshape(heads_dev, HEAD * STATE)
-    adjoint_all = lax.all_gather(flat_adjoint.astype(jnp.bfloat16), "seq")
+    adjoint_all = torus_gather(flat_adjoint.astype(jnp.bfloat16), seq_count)
     later_adjoint = carried_sum(adjoint_all, level_all, seq_index, False)
     later_adjoint = later_adjoint.reshape(heads_dev, HEAD, STATE)
     scan_grad = jnp.concatenate(back_pieces, axis=0) + jnp.exp(cum_level[-1][None, :] - cum_level)[

time: 425 us -> 420 us (0.988)
  the two profiles are of different devices: /device:TPU:32 before, /device:TPU:34 now
where the time goes in v9:
time: 420 us; the launch traced here: 413 us
  waiting for transfers between devices  141 us (34%)
  matrix products  76.8 us (18%)
  local copies, waits for them, and re-layouts  69.5 us (17%)
  other arithmetic  46.1 us (11%)
  starting transfers between devices  37.6 us (9%)
  blocking collectives  26.1 us (6%)
  between operations  15.6 us (4%)
    reduce_scatter x1, waiting for transfers between devices, per_device(): lax.psum_scatter(spread_rows, 'seq', scatter_dimension=0, tiled=True)  70.1 us
    all_gather x1, waiting for transfers between devices, per_device(): h_all = lax.all_gather(h_block, 'seq', axis=0)  50.2 us
    all_gather x1, blocking collectives, per_device(): lax.all_gather(jnp.concatenate([flat_state, level_lanes], axis=1), 'seq')  26.1 us
    ppermute x8, starting transfers between devices, dispatch(): received.append(lax.ppermute(send, ('expert', 'mp'), pairs))  19.6 us
    gather x2, local copies, waits for them, and re-layouts, compact(): jnp.take(blocks, source, axis=0, mode='clip')  12.4 us
    select_n x4, other arithmetic, compact(): jnp.where(used[:, None, None], jnp.take(blocks, source, axis=0, mode='cli...  10.9 us
    ppermute x4, starting transfers between devices, give_back(): received.append(lax.ppermute(send, ('expert', 'mp'), pairs))  9.65 us
    dot_general x1, matrix products, per_device(): jnp.einsum('tf,df->td', shard_grad, up_local, preferred_element_type=jnp....  9.09 us
  transfers between devices with their start and end apart: 23, of which 13 were waited for; matrix products, arithmetic and copies ran while one was open for 24% of the time, Pallas kernels for 0%

profile of v9, /device:TPU:34, one launch (start us, length us, event | category | flops | bytes accessed | tf_op | source)
XLA Modules:
  0.0 412.8 jit_solution(13617350955125921227)
XLA Ops:
  8.8 2.8 convolution_convert_fusion.2
  11.5 3.3 constant_dynamic-slice_fusion.11
  16.2 4.8 %collective-permute-start.2 = (bf16[128,512]{1,0:T(8,128)(2,1)S(1)}, bf16[128,512]{1,0:T(8,128)(2,1)}, u32[]{:S(2)}, u32[]{:S(2)}) collective-permute-start(bf16[128,512]{1,0:T(8,128)(2,1)S(1)} %bitcast.248), channel_id=1, source_target_pairs={{0,4},{1,6},{2,0},{3,2},{4,5},{5,7},{6,1},{7,3},{8,12},{9,14},{10,... | collective-permute-start | bytes 393224 | tf_op jit(solution)/shard_map/ppermute | solution.py:73
  61.9 26.1 %all-gather = f32[128,1152]{1,0:T(8,128)S(1)} all-gather(f32[8,1152]{1,0:T(8,128)S(1)} %pad_maximum_fusion.4), channel_id=2, replica_groups=mesh['seq'=16,'expert'=4,'mp'=2] {'seq'}, dimensions={0}, use_global_device_ids=true | all-gather | bytes 626688 | tf_op jit(solution)/shard_map/all_gather | solution.py:213
  94.7 4.2 %fusion.45 = f32[8,512,64]{1,2,0:T(8,128)S(1)} fusion(bf16[512,8,64]{0,2,1:T(8,128)(2,1)} %bitcast.243, f32[512,512]{1,0:T(8,128)S(1)} %fusion.137, f32[8,512]{1,0:T(8,128)} %get-tuple-element.55, pred[512,512]{1,0:T(8,128)(4,1)S(1)} %iota_compare_fusion), kind=kOutput, calls=%fused_computation.56 | convolution fusion | flops 283115520 | bytes 2899968 | tf_op jit(solution)/shard_map/hts,shp->thp/dot_general | solution.py:195
  99.0 2.7 fusion.92
  102.3 2.7 fusion.47
  108.4 2.8 maximum_add_fusion
  111.2 2.9 copy.236
  114.0 3.2 add_convert_fusion
  121.0 5.1 %collective-permute-start.7 = (bf16[128,512]{1,0:T(8,128)(2,1)S(1)}, bf16[128,512]{1,0:T(8,128)(2,1)S(1)}, u32[]{:S(2)}, u32[]{:S(2)}) collective-permute-start(bf16[128,512]{1,0:T(8,128)(2,1)S(1)} %bitcast.259), channel_id=1, source_target_pairs={{0,4},{1,6},{2,0},{3,2},{4,5},{5,7},{6,1},{7,3},{8,12},{9,14},{10,... | collective-permute-start | bytes 393224 | tf_op jit(solution)/shard_map/ppermute | solution.py:73
  130.1 3.0 collective-permute-done.6
  145.1 6.2 %gather_fusion.1 = bf16[8,128,2048]{2,1,0:T(8,128)(2,1)} fusion(bf16[16,128,2048]{2,1,0:T(8,128)(2,1)} %all-gather.4.cloned.1.call-done, s32[1024]{0:T(1024)S(1)} %pad_clamp_fusion.3), kind=kCustom, calls=%fused_computation.3 | custom fusion | bytes 8388640 | tf_op jit(solution)/shard_map/jit(_take)/gather | solution.py:113
  151.3 2.9 broadcast_select_fusion.1
  154.9 3.5 fusion.54
  158.5 2.7 bitcast_select_fusion.1
  163.8 50.2 %all-gather.6.cloned.1.call-done = bf16[16,128,2048]{2,1,0:T(8,128)(2,1)} async-done(((bf16[1,128,2048]{2,1,0:T(8,128)(2,1)}), bf16[16,128,2048]{2,1,0:T(8,128)(2,1)}) %all-gather.6.cloned.1.call-update) | async-done | bytes 8388624 | tf_op jit(solution)/shard_map/all_gather | solution.py:232
  214.0 6.2 %gather_fusion.2 = bf16[8,128,2048]{2,1,0:T(8,128)(2,1)} fusion(bf16[16,128,2048]{2,1,0:T(8,128)(2,1)} %all-gather.6.cloned.1.call-done, s32[1024]{0:T(1024)S(1)} %pad_clamp_fusion.3), kind=kCustom, calls=%fused_computation.4 | custom fusion | bytes 8388640 | tf_op jit(solution)/shard_map/jit(_take)/gather | solution.py:113
  222.8 3.4 fusion.57
  226.5 3.4 collective-permute-done.9
  232.3 3.8 gather_fusion.3
  238.3 9.1 %convolution_convert_fusion = bf16[2048,2048]{1,0:T(8,128)(2,1)} fusion(bf16[2048,768]{1,0:T(8,128)(2,1)S(1)} %bitcast.236, bf16[1,2048,768]{2,1,0:T(8,128)(2,1)S(1)} %copy-done), kind=kOutput, calls=%fused_computation.14 | convolution fusion | flops 6446645248 | bytes 14680064 | tf_op jit(solution)/shard_map/tf,df->td/dot_general | solution.py:248
  251.6 5.5 %fusion.192 = f32[2048,768]{1,0:T(8,128)} fusion(bf16[1024,2048]{1,0:T(8,128)(2,1)S(1)} %bitcast_select_fusion, bf16[1024,768]{1,0:T(8,128)(2,1)S(1)} %copy-done.4), kind=kOutput, calls=%fused_computation.319 | convolution fusion | flops 3221225472 | bytes 12058624 | tf_op jit(solution)/shard_map/td,tf->df/dot_general | solution.py:246
  257.1 5.6 %fusion.60 = f32[768,2048]{1,0:T(8,128)} fusion(bf16[1024,2048]{1,0:T(8,128)(2,1)S(1)} %copy-done.7, bf16[1024,768]{1,0:T(8,128)(2,1)S(1)} %copy-done.12, bf16[1024,768]{1,0:T(8,128)(2,1)S(1)} %copy-done.10), kind=kOutput, calls=%fused_computation.79 | convolution fusion | flops 3227516928 | bytes 13631488 | tf_op jit(solution)/shard_map/tf,td->fd/dot_general | solution.py:243
  262.6 70.1 %reduce-scatter.2.cloned.1.call-done = bf16[128,2048]{1,0:T(8,128)(2,1)} async-done(((bf16[2048,2048]{1,0:T(8,128)(2,1)}), bf16[128,2048]{1,0:T(8,128)(2,1)}) %reduce-scatter.2.cloned.1.call-update) | async-done | bytes 524304 | tf_op jit(solution)/shard_map/reduce_scatter | solution.py:250
  336.0 3.7 collective-permute-start.12
  341.7 3.4 collective-permute-start.10
  357.2 4.3 %fusion.8 = f32[8,64,512]{2,1,0:T(8,128)} fusion(f32[512,512]{1,0:T(8,128)} %copy-done.15, f32[8,512]{1,0:T(8,128)S(1)} %copy-done.40, pred[512,512]{1,0:T(8,128)(4,1)S(1)} %copy-done.24, f32[512,8,64]{0,2,1:T(8,128)S(1)} %bitcast.231), kind=kOutput, calls=%fused_computation.18 | convolution fusion | flops 277872640 | bytes 3424256 | tf_op jit(solution)/shard_map/hts,thp->shp/dot_general | solution.py:283
  363.2 4.4 %fusion.2 = f32[8,64,512]{2,1,0:T(8,128)} fusion(f32[512,512]{1,0:T(8,128)} %copy-done.13, f32[8,512]{1,0:T(8,128)S(1)} %copy-done.37, pred[512,512]{1,0:T(8,128)(4,1)S(1)} %copy-done.24, f32[512,8,64]{0,2,1:T(8,128)S(1)} %bitcast.227), kind=kOutput, calls=%fused_computation.15 | convolution fusion | flops 277872640 | bytes 3424256 | tf_op jit(solution)/shard_map/hts,thp->shp/dot_general | solution.py:283
  374.5 3.5 fusion.83
  398.8 3.0 copy.254
  401.8 4.0 add.371
  (285 shorter events, 134.7 us)
Async XLA Ops:
  7.2 215.6 %copy-start = (bf16[1,2048,768]{2,1,0:T(8,128)(2,1)S(1)}, bf16[1,2048,768]{2,1,0:T(8,128)(2,1)}, u32[]{:S(2)}) copy-start(bf16[1,2048,768]{2,1,0:T(8,128)(2,1)} %param.18) | copy-start | bytes 9437188
  7.2 110.0 %all-gather.4.cloned.1.call-start = ((), (), s32[]{:S(2)}) async-start(), calls=%async_computation.1 | async-start | bytes 8912896 | tf_op jit(solution)/shard_map/all_gather | solution.py:157
  14.9 11.3 %collective-permute-start.3 = (bf16[128,512]{1,0:T(8,128)(2,1)S(1)}, bf16[128,512]{1,0:T(8,128)(2,1)}, u32[]{:S(2)}, u32[]{:S(2)}) collective-permute-start(bf16[128,512]{1,0:T(8,128)(2,1)S(1)} %bitcast.247), channel_id=1, source_target_pairs={{0,6},{1,0},{2,2},{3,4},{4,7},{5,1},{6,3},{7,5},{8,14},{9,8},{10,1... | collective-permute-start | bytes 393224 | tf_op jit(solution)/shard_map/ppermute | solution.py:73
  16.2 10.0 %collective-permute-start.2 = (bf16[128,512]{1,0:T(8,128)(2,1)S(1)}, bf16[128,512]{1,0:T(8,128)(2,1)}, u32[]{:S(2)}, u32[]{:S(2)}) collective-permute-start(bf16[128,512]{1,0:T(8,128)(2,1)S(1)} %bitcast.248), channel_id=1, source_target_pairs={{0,4},{1,6},{2,0},{3,2},{4,5},{5,7},{6,1},{7,3},{8,12},{9,14},{10,... | collective-permute-start | bytes 393224 | tf_op jit(solution)/shard_map/ppermute | solution.py:73
  21.1 7.0 %collective-permute-start.1 = (bf16[128,512]{1,0:T(8,128)(2,1)S(1)}, bf16[128,512]{1,0:T(8,128)(2,1)}, u32[]{:S(2)}, u32[]{:S(2)}) collective-permute-start(bf16[128,512]{1,0:T(8,128)(2,1)S(1)} %bitcast.249), channel_id=1, source_target_pairs={{0,2},{1,4},{2,6},{3,0},{4,3},{5,5},{6,7},{7,1},{8,10},{9,12},{10,... | collective-permute-start | bytes 393224 | tf_op jit(solution)/shard_map/ppermute | solution.py:73
  23.7 6.6 %collective-permute-start = (bf16[128,512]{1,0:T(8,128)(2,1)}, bf16[128,512]{1,0:T(8,128)(2,1)}, u32[]{:S(2)}, u32[]{:S(2)}) collective-permute-start(bf16[128,512]{1,0:T(8,128)(2,1)} %bitcast.216), channel_id=1, source_target_pairs={{0,0},{1,2},{2,4},{3,6},{4,1},{5,3},{6,5},{7,7},{8,8},{9,10},{10,1... | collective-permute-start | bytes 393224 | tf_op jit(solution)/shard_map/ppermute | solution.py:73
  26.1 17.2 %copy-start.45 = (pred[4]{0:T(512)(128)(4,1)}, pred[4]{0:T(512)(128)(4,1)S(1)}, u32[]{:S(2)}) copy-start(pred[4]{0:T(512)(128)(4,1)S(1)} %get-tuple-element.62) | copy-start | bytes 16
  26.2 17.2 %copy-start.43 = (s32[1024]{0:T(1024)}, s32[1024]{0:T(1024)S(1)}, u32[]{:S(2)}) copy-start(s32[1024]{0:T(1024)S(1)} %pad_clamp_fusion.4) | copy-start | bytes 12292
  40.7 173.3 %all-gather.6.cloned.1.call-start = ((), (), s32[]{:S(2)}) async-start(), calls=%async_computation.2 | async-start | bytes 8912896 | tf_op jit(solution)/shard_map/all_gather | solution.py:232
  43.3 13.2 %copy-start.19 = (bf16[1024,16]{0,1:T(8,128)(2,1)S(1)}, bf16[1024,16]{0,1:T(8,128)(2,1)}, u32[]{:S(2)}) copy-start(bf16[1024,16]{0,1:T(8,128)(2,1)} %param.13) | copy-start | bytes 98308
  54.6 39.4 %copy-start.18 = (bf16[1024,16]{0,1:T(8,128)(2,1)S(1)}, bf16[1024,16]{0,1:T(8,128)(2,1)}, u32[]{:S(2)}) copy-start(bf16[1024,16]{0,1:T(8,128)(2,1)} %param.14) | copy-start | bytes 98308
  92.5 12.5 %copy-start.23 = (pred[512,512]{1,0:T(8,128)(4,1)}, pred[512,512]{1,0:T(8,128)(4,1)S(1)}, u32[]{:S(2)}) copy-start(pred[512,512]{1,0:T(8,128)(4,1)S(1)} %iota_compare_fusion) | copy-start | bytes 786436
  117.2 20.6 %copy-start.46 = (pred[4]{0:T(512)(128)(4,1)S(1)}, pred[4]{0:T(512)(128)(4,1)}, u32[]{:S(2)}) copy-start(pred[4]{0:T(512)(128)(4,1)} %copy-done.45) | copy-start | bytes 16
  120.3 23.7 %copy-start.35 = (s32[16,8]{1,0:T(8,128)S(1)}, s32[16,8]{1,0:T(8,128)}, u32[]{:S(2)}) copy-start(s32[16,8]{1,0:T(8,128)} %copy-done.34) | copy-start | bytes 1540
  120.3 9.7 %collective-permute-start.8 = (bf16[128,512]{1,0:T(8,128)(2,1)S(1)}, bf16[128,512]{1,0:T(8,128)(2,1)S(1)}, u32[]{:S(2)}, u32[]{:S(2)}) collective-permute-start(bf16[128,512]{1,0:T(8,128)(2,1)S(1)} %bitcast.258), channel_id=1, source_target_pairs={{0,6},{1,0},{2,2},{3,4},{4,7},{5,1},{6,3},{7,5},{8,14},{9,8},{10,1... | collective-permute-start | bytes 393224 | tf_op jit(solution)/shard_map/ppermute | solution.py:73
  121.0 9.0 %collective-permute-start.7 = (bf16[128,512]{1,0:T(8,128)(2,1)S(1)}, bf16[128,512]{1,0:T(8,128)(2,1)S(1)}, u32[]{:S(2)}, u32[]{:S(2)}) collective-permute-start(bf16[128,512]{1,0:T(8,128)(2,1)S(1)} %bitcast.259), channel_id=1, source_target_pairs={{0,4},{1,6},{2,0},{3,2},{4,5},{5,7},{6,1},{7,3},{8,12},{9,14},{10,... | collective-permute-start | bytes 393224 | tf_op jit(solution)/shard_map/ppermute | solution.py:73
  126.2 6.9 %collective-permute-start.6 = (bf16[128,512]{1,0:T(8,128)(2,1)S(1)}, bf16[128,512]{1,0:T(8,128)(2,1)S(1)}, u32[]{:S(2)}, u32[]{:S(2)}) collective-permute-start(bf16[128,512]{1,0:T(8,128)(2,1)S(1)} %bitcast.260), channel_id=1, source_target_pairs={{0,2},{1,4},{2,6},{3,0},{4,3},{5,5},{6,7},{7,1},{8,10},{9,12},{10,... | collective-permute-start | bytes 393224 | tf_op jit(solution)/shard_map/ppermute | solution.py:73
  128.1 6.3 %collective-permute-start.5 = (bf16[128,512]{1,0:T(8,128)(2,1)S(1)}, bf16[128,512]{1,0:T(8,128)(2,1)S(1)}, u32[]{:S(2)}, u32[]{:S(2)}) collective-permute-start(bf16[128,512]{1,0:T(8,128)(2,1)S(1)} %bitcast.261), channel_id=1, source_target_pairs={{0,0},{1,2},{2,4},{3,6},{4,1},{5,3},{6,5},{7,7},{8,8},{9,10},{10,1... | collective-permute-start | bytes 393224 | tf_op jit(solution)/shard_map/ppermute | solution.py:73
  143.9 188.8 %reduce-scatter.2.cloned.1.call-start = ((), (), s32[]{:S(2)}) async-start(), calls=%async_computation.3 | async-start | bytes 8912896 | tf_op jit(solution)/shard_map/reduce_scatter | solution.py:250
  158.3 3.5 collective-permute-start.4
  226.2 3.7 collective-permute-start.9
  335.3 11.5 %collective-permute-start.13 = (bf16[128,512]{1,0:T(8,128)(2,1)S(1)}, bf16[128,512]{1,0:T(8,128)(2,1)S(1)}, u32[]{:S(2)}, u32[]{:S(2)}) collective-permute-start(bf16[128,512]{1,0:T(8,128)(2,1)S(1)} %bitcast.250), channel_id=1, source_target_pairs={{6,0},{0,1},{2,2},{4,3},{7,4},{1,5},{3,6},{5,7},{14,8},{8,9},{10,1... | collective-permute-start | bytes 393224 | tf_op jit(solution)/shard_map/ppermute | solution.py:89
  336.0 11.0 %collective-permute-start.12 = (bf16[128,512]{1,0:T(8,128)(2,1)S(1)}, bf16[128,512]{1,0:T(8,128)(2,1)S(1)}, u32[]{:S(2)}, u32[]{:S(2)}) collective-permute-start(bf16[128,512]{1,0:T(8,128)(2,1)S(1)} %bitcast.252), channel_id=1, source_target_pairs={{4,0},{6,1},{0,2},{2,3},{5,4},{7,5},{1,6},{3,7},{12,8},{14,9},{8,1... | collective-permute-start | bytes 393224 | tf_op jit(solution)/shard_map/ppermute | solution.py:89
  339.7 8.4 %collective-permute-start.11 = (bf16[128,512]{1,0:T(8,128)(2,1)S(1)}, bf16[128,512]{1,0:T(8,128)(2,1)S(1)}, u32[]{:S(2)}, u32[]{:S(2)}) collective-permute-start(bf16[128,512]{1,0:T(8,128)(2,1)S(1)} %bitcast.254), channel_id=1, source_target_pairs={{2,0},{4,1},{6,2},{0,3},{3,4},{5,5},{7,6},{1,7},{10,8},{12,9},{14,... | collective-permute-start | bytes 393224 | tf_op jit(solution)/shard_map/ppermute | solution.py:89
  341.7 9.2 %collective-permute-start.10 = (bf16[128,512]{1,0:T(8,128)(2,1)S(1)}, bf16[128,512]{1,0:T(8,128)(2,1)S(1)}, u32[]{:S(2)}, u32[]{:S(2)}) collective-permute-start(bf16[128,512]{1,0:T(8,128)(2,1)S(1)} %bitcast.256), channel_id=1, source_target_pairs={{0,0},{2,1},{4,2},{6,3},{1,4},{3,5},{5,6},{7,7},{8,8},{10,9},{12,1... | collective-permute-start | bytes 393224 | tf_op jit(solution)/shard_map/ppermute | solution.py:89
  363.2 11.4 %copy-start.16 = (f32[512,512]{1,0:T(8,128)S(1)}, f32[512,512]{1,0:T(8,128)}, u32[]{:S(2)}) copy-start(f32[512,512]{1,0:T(8,128)} %copy-done.15) | copy-start | bytes 3145732
  369.5 17.2 %collective-permute-start.16 = (bf16[8,1024]{1,0:T(8,128)(2,1)S(1)}, bf16[8,1024]{1,0:T(8,128)(2,1)S(1)}, u32[]{:S(2)}, u32[]{:S(2)}) collective-permute-start(bf16[8,1024]{1,0:T(8,128)(2,1)S(1)} %convert_element_type.174), channel_id=1, source_target_pairs={{0,24},{8,0},{16,8},{24,16},{32,56},{40,32},{48,40},{56,48},{64,88... | collective-permute-start | bytes 49160 | tf_op jit(solution)/shard_map/ppermute | solution.py:40
  370.4 16.3 %collective-permute-start.15 = (bf16[8,1024]{1,0:T(8,128)(2,1)S(1)}, bf16[8,1024]{1,0:T(8,128)(2,1)S(1)}, u32[]{:S(2)}, u32[]{:S(2)}) collective-permute-start(bf16[8,1024]{1,0:T(8,128)(2,1)S(1)} %convert_element_type.174), channel_id=1, source_target_pairs={{0,16},{8,24},{16,0},{24,8},{32,48},{40,56},{48,32},{56,40},{64,80... | collective-permute-start | bytes 49160 | tf_op jit(solution)/shard_map/ppermute | solution.py:40
  372.5 14.2 %collective-permute-start.14 = (bf16[8,1024]{1,0:T(8,128)(2,1)S(1)}, bf16[8,1024]{1,0:T(8,128)(2,1)S(1)}, u32[]{:S(2)}, u32[]{:S(2)}) collective-permute-start(bf16[8,1024]{1,0:T(8,128)(2,1)S(1)} %convert_element_type.174), channel_id=1, source_target_pairs={{0,8},{8,16},{16,24},{24,0},{32,40},{40,48},{48,56},{56,32},{64,72... | collective-permute-start | bytes 49160 | tf_op jit(solution)/shard_map/ppermute | solution.py:40
  387.5 4.3 %collective-permute-start.19 = (bf16[4,8,1024]{2,1,0:T(8,128)(2,1)S(1)}, bf16[4,8,1024]{2,1,0:T(8,128)(2,1)S(1)}, u32[]{:S(2)}, u32[]{:S(2)}) collective-permute-start(bf16[4,8,1024]{2,1,0:T(8,128)(2,1)S(1)} %broadcast_select_fusion.3), channel_id=1, source_target_pairs={{0,96},{8,104},{16,112},{24,120},{32,0},{40,8},{48,16},{56,24},{64... | collective-permute-start | bytes 196616 | tf_op jit(solution)/shard_map/ppermute | solution.py:45
  388.4 5.8 %collective-permute-start.18 = (bf16[4,8,1024]{2,1,0:T(8,128)(2,1)S(1)}, bf16[4,8,1024]{2,1,0:T(8,128)(2,1)S(1)}, u32[]{:S(2)}, u32[]{:S(2)}) collective-permute-start(bf16[4,8,1024]{2,1,0:T(8,128)(2,1)S(1)} %broadcast_select_fusion.3), channel_id=1, source_target_pairs={{0,64},{8,72},{16,80},{24,88},{32,96},{40,104},{48,112},{56,120},{... | collective-permute-start | bytes 196616 | tf_op jit(solution)/shard_map/ppermute | solution.py:45
  389.8 5.5 %collective-permute-start.17 = (bf16[4,8,1024]{2,1,0:T(8,128)(2,1)S(1)}, bf16[4,8,1024]{2,1,0:T(8,128)(2,1)S(1)}, u32[]{:S(2)}, u32[]{:S(2)}) collective-permute-start(bf16[4,8,1024]{2,1,0:T(8,128)(2,1)S(1)} %broadcast_select_fusion.3), channel_id=1, source_target_pairs={{0,32},{8,40},{16,48},{24,56},{32,64},{40,72},{48,80},{56,88},{64,... | collective-permute-start | bytes 196616 | tf_op jit(solution)/shard_map/ppermute | solution.py:45
  (50 other events, 253.9 us)
Sparse Core Ops, SparseCore 0:
  40.8 73.7 all-gather.3
  144.0 69.9 all-gather.5
  247.5 85.1 reduce-scatter.1

commit v10 on v9

--- a/solution.py
+++ b/solution.py
@@ -210,7 +210,7 @@
         )
     flat_state = carry_state.reshape(heads_dev, HEAD * STATE)
     level_lanes = jnp.broadcast_to(cum_level[-1][:, None], (heads_dev, 128))
-    joined_all = lax.all_gather(jnp.concatenate([flat_state, level_lanes], axis=1), "seq")
+    joined_all = torus_gather(jnp.concatenate([flat_state, level_lanes], axis=1), seq_count)
     state_all = joined_all[:, :, : HEAD * STATE]
     level_all = joined_all[:, :, HEAD * STATE]
     incoming = carried_sum(state_all, level_all, seq_index, True)

time: 420 us -> 428 us (1.019)
  blocking collectives: 26.1 us -> 0 us
  waiting for transfers between devices: 141 us -> 156 us
  starting transfers between devices: 37.6 us -> 46.3 us
    all_gather x1 -> x0, blocking collectives: 26.1 us -> none  [per_device(): lax.all_gather(jnp.concatenate([flat_state, level_lanes], axis=1), 'seq')]
    ppermute x3 -> x6, waiting for transfers between devices: 4.81 us -> 16.1 us  [torus_gather(): got.append(lax.ppermute(line, 'seq', pairs))]
    ppermute x3 -> x6, starting transfers between devices: 2.89 us -> 7.92 us  [torus_gather(): got.append(lax.ppermute(line, 'seq', pairs))]
    ppermute x3 -> x6, starting transfers between devices: 5.01 us -> 9.84 us  [torus_gather(): got.append(lax.ppermute(value, 'seq', pairs))]
  transfers between devices with their start and end apart: 23 -> 29, of which waited for: 13 -> 16; matrix products, arithmetic and copies ran while one was open for 24% -> 25% of each run, Pallas kernels for 0% -> 0%
where the time goes in v10:
time: 428 us; the launch traced here: 420 us
  waiting for transfers between devices  156 us (36%)
  matrix products  79.7 us (19%)
  local copies, waits for them, and re-layouts  72.3 us (17%)
  other arithmetic  50.1 us (12%)
  starting transfers between devices  46.3 us (11%)
  between operations  15.5 us (4%)
    reduce_scatter x1, waiting for transfers between devices, per_device(): lax.psum_scatter(spread_rows, 'seq', scatter_dimension=0, tiled=True)  70.7 us
    all_gather x1, waiting for transfers between devices, per_device(): h_all = lax.all_gather(h_block, 'seq', axis=0)  51.9 us
    ppermute x8, starting transfers between devices, dispatch(): received.append(lax.ppermute(send, ('expert', 'mp'), pairs))  18.3 us
    ppermute x6, waiting for transfers between devices, torus_gather(): got.append(lax.ppermute(line, 'seq', pairs))  16.1 us
    gather x2, local copies, waits for them, and re-layouts, compact(): jnp.take(blocks, source, axis=0, mode='clip')  12.4 us
    select_n x4, other arithmetic, compact(): jnp.where(used[:, None, None], jnp.take(blocks, source, axis=0, mode='cli...  10.6 us
    ppermute x6, starting transfers between devices, torus_gather(): got.append(lax.ppermute(value, 'seq', pairs))  9.84 us
    ppermute x4, starting transfers between devices, give_back(): received.append(lax.ppermute(send, ('expert', 'mp'), pairs))  9.84 us
  transfers between devices with their start and end apart: 29, of which 16 were waited for; matrix products, arithmetic and copies ran while one was open for 25% of the time, Pallas kernels for 0%

profile of v10, /device:TPU:34, one launch (start us, length us, event | category | flops | bytes accessed | tf_op | source)
XLA Modules:
  0.0 420.3 jit_solution(2800640357597257331)
XLA Ops:
  8.8 2.8 convolution_convert_fusion.2
  11.6 3.3 constant_dynamic-slice_fusion.11
  16.3 4.8 %collective-permute-start.2 = (bf16[128,512]{1,0:T(8,128)(2,1)S(1)}, bf16[128,512]{1,0:T(8,128)(2,1)}, u32[]{:S(2)}, u32[]{:S(2)}) collective-permute-start(bf16[128,512]{1,0:T(8,128)(2,1)S(1)} %bitcast.260), channel_id=1, source_target_pairs={{0,4},{1,6},{2,0},{3,2},{4,5},{5,7},{6,1},{7,3},{8,12},{9,14},{10,... | collective-permute-start | bytes 393224 | tf_op jit(solution)/shard_map/ppermute | solution.py:73
  70.9 4.2 fusion.45
  79.3 2.7 fusion.47
  89.4 3.0 collective-permute-start.9
  95.1 5.4 %collective-permute-done.9 = f32[4,8,1152]{2,1,0:T(8,128)S(1)} collective-permute-done((f32[4,8,1152]{2,1,0:T(8,128)S(1)}, f32[4,8,1152]{2,1,0:T(8,128)S(1)}, u32[]{:S(2)}, u32[]{:S(2)}) %collective-permute-start.9) | collective-permute-done | bytes 147488 | tf_op jit(solution)/shard_map/ppermute | solution.py:45
  100.5 3.3 collective-permute-done.8
  114.9 3.9 maximum_add_fusion
  118.8 2.9 copy.236
  121.7 3.2 add_convert_fusion
  128.7 3.2 collective-permute-start.13
  136.4 3.8 collective-permute-done.12
  151.8 6.2 %gather_fusion.3 = bf16[8,128,2048]{2,1,0:T(8,128)(2,1)} fusion(bf16[16,128,2048]{2,1,0:T(8,128)(2,1)} %all-gather.3.cloned.1.call-done, s32[1024]{0:T(1024)S(1)} %pad_clamp_fusion.1), kind=kCustom, calls=%fused_computation.5 | custom fusion | bytes 8388640 | tf_op jit(solution)/shard_map/jit(_take)/gather | solution.py:113
  161.2 3.5 fusion.54
  165.0 2.8 bitcast_select_fusion.1
  170.3 51.9 %all-gather.5.cloned.1.call-done = bf16[16,128,2048]{2,1,0:T(8,128)(2,1)} async-done(((bf16[1,128,2048]{2,1,0:T(8,128)(2,1)}), bf16[16,128,2048]{2,1,0:T(8,128)(2,1)}) %all-gather.5.cloned.1.call-update) | async-done | bytes 8388624 | tf_op jit(solution)/shard_map/all_gather | solution.py:232
  222.2 6.2 %gather_fusion.4 = bf16[8,128,2048]{2,1,0:T(8,128)(2,1)} fusion(bf16[16,128,2048]{2,1,0:T(8,128)(2,1)} %all-gather.5.cloned.1.call-done, s32[1024]{0:T(1024)S(1)} %pad_clamp_fusion.1), kind=kCustom, calls=%fused_computation.6 | custom fusion | bytes 8388640 | tf_op jit(solution)/shard_map/jit(_take)/gather | solution.py:113
  231.0 3.4 fusion.57
  234.6 3.4 collective-permute-done.15
  240.4 3.8 gather_fusion.5
  246.4 9.0 %convolution_convert_fusion = bf16[2048,2048]{1,0:T(8,128)(2,1)} fusion(bf16[2048,768]{1,0:T(8,128)(2,1)S(1)} %bitcast.247, bf16[1,2048,768]{2,1,0:T(8,128)(2,1)S(1)} %copy-done), kind=kOutput, calls=%fused_computation.16 | convolution fusion | flops 6446645248 | bytes 14680064 | tf_op jit(solution)/shard_map/tf,df->td/dot_general | solution.py:248
  258.9 5.5 %fusion.193 = f32[2048,768]{1,0:T(8,128)} fusion(bf16[1024,2048]{1,0:T(8,128)(2,1)S(1)} %bitcast_select_fusion, bf16[1024,768]{1,0:T(8,128)(2,1)S(1)} %copy-done.4), kind=kOutput, calls=%fused_computation.327 | convolution fusion | flops 3221225472 | bytes 12058624 | tf_op jit(solution)/shard_map/td,tf->df/dot_general | solution.py:246
  264.4 5.6 %fusion.60 = f32[768,2048]{1,0:T(8,128)} fusion(bf16[1024,2048]{1,0:T(8,128)(2,1)S(1)} %copy-done.7, bf16[1024,768]{1,0:T(8,128)(2,1)S(1)} %copy-done.12, bf16[1024,768]{1,0:T(8,128)(2,1)S(1)} %copy-done.10), kind=kOutput, calls=%fused_computation.81 | convolution fusion | flops 3227516928 | bytes 13631488 | tf_op jit(solution)/shard_map/tf,td->fd/dot_general | solution.py:243
  269.9 70.7 %reduce-scatter.2.cloned.1.call-done = bf16[128,2048]{1,0:T(8,128)(2,1)} async-done(((bf16[2048,2048]{1,0:T(8,128)(2,1)}), bf16[128,2048]{1,0:T(8,128)(2,1)}) %reduce-scatter.2.cloned.1.call-update) | async-done | bytes 524304 | tf_op jit(solution)/shard_map/reduce_scatter | solution.py:250
  343.9 3.6 collective-permute-start.18
  349.5 3.6 collective-permute-start.16
  365.1 4.3 %fusion.8 = f32[8,64,512]{2,1,0:T(8,128)} fusion(f32[512,512]{1,0:T(8,128)} %copy-done.15, f32[8,512]{1,0:T(8,128)S(1)} %copy-done.41, pred[512,512]{1,0:T(8,128)(4,1)S(1)} %copy-done.25, f32[512,8,64]{0,2,1:T(8,128)S(1)} %bitcast.242), kind=kOutput, calls=%fused_computation.20 | convolution fusion | flops 277872640 | bytes 3424256 | tf_op jit(solution)/shard_map/hts,thp->shp/dot_general | solution.py:283
  371.1 4.4 %fusion.2 = f32[8,64,512]{2,1,0:T(8,128)} fusion(f32[512,512]{1,0:T(8,128)} %copy-done.13, f32[8,512]{1,0:T(8,128)S(1)} %copy-done.38, pred[512,512]{1,0:T(8,128)(4,1)S(1)} %copy-done.25, f32[512,8,64]{0,2,1:T(8,128)S(1)} %bitcast.238), kind=kOutput, calls=%fused_computation.17 | convolution fusion | flops 277872640 | bytes 3424256 | tf_op jit(solution)/shard_map/hts,thp->shp/dot_general | solution.py:283
  382.3 3.5 fusion.83
  406.5 3.1 copy.254
  409.6 4.0 add.380
  (313 shorter events, 160.0 us)
Async XLA Ops:
  7.2 223.8 %copy-start = (bf16[1,2048,768]{2,1,0:T(8,128)(2,1)S(1)}, bf16[1,2048,768]{2,1,0:T(8,128)(2,1)}, u32[]{:S(2)}) copy-start(bf16[1,2048,768]{2,1,0:T(8,128)(2,1)} %param.18) | copy-start | bytes 9437188
  7.2 117.7 %all-gather.3.cloned.1.call-start = ((), (), s32[]{:S(2)}) async-start(), calls=%async_computation.1 | async-start | bytes 8912896 | tf_op jit(solution)/shard_map/all_gather | solution.py:157
  14.9 25.9 %copy-start.61 = (f32[8]{0:T(128)S(1)}, f32[8]{0:T(128)}, u32[]{:S(2)}) copy-start(f32[8]{0:T(128)} %param.15) | copy-start | bytes 100
  14.9 25.9 %copy-start.49 = (s32[1024]{0:T(1024)S(1)}, s32[1024]{0:T(1024)}, u32[]{:S(2)}) copy-start(s32[1024]{0:T(1024)} %param.16) | copy-start | bytes 12292
  14.9 11.3 %collective-permute-start.3 = (bf16[128,512]{1,0:T(8,128)(2,1)S(1)}, bf16[128,512]{1,0:T(8,128)(2,1)}, u32[]{:S(2)}, u32[]{:S(2)}) collective-permute-start(bf16[128,512]{1,0:T(8,128)(2,1)S(1)} %bitcast.259), channel_id=1, source_target_pairs={{0,6},{1,0},{2,2},{3,4},{4,7},{5,1},{6,3},{7,5},{8,14},{9,8},{10,1... | collective-permute-start | bytes 393224 | tf_op jit(solution)/shard_map/ppermute | solution.py:73
  16.3 10.0 %collective-permute-start.2 = (bf16[128,512]{1,0:T(8,128)(2,1)S(1)}, bf16[128,512]{1,0:T(8,128)(2,1)}, u32[]{:S(2)}, u32[]{:S(2)}) collective-permute-start(bf16[128,512]{1,0:T(8,128)(2,1)S(1)} %bitcast.260), channel_id=1, source_target_pairs={{0,4},{1,6},{2,0},{3,2},{4,5},{5,7},{6,1},{7,3},{8,12},{9,14},{10,... | collective-permute-start | bytes 393224 | tf_op jit(solution)/shard_map/ppermute | solution.py:73
  21.1 7.0 %collective-permute-start.1 = (bf16[128,512]{1,0:T(8,128)(2,1)S(1)}, bf16[128,512]{1,0:T(8,128)(2,1)}, u32[]{:S(2)}, u32[]{:S(2)}) collective-permute-start(bf16[128,512]{1,0:T(8,128)(2,1)S(1)} %bitcast.261), channel_id=1, source_target_pairs={{0,2},{1,4},{2,6},{3,0},{4,3},{5,5},{6,7},{7,1},{8,10},{9,12},{10,... | collective-permute-start | bytes 393224 | tf_op jit(solution)/shard_map/ppermute | solution.py:73
  23.7 6.6 %collective-permute-start = (bf16[128,512]{1,0:T(8,128)(2,1)}, bf16[128,512]{1,0:T(8,128)(2,1)}, u32[]{:S(2)}, u32[]{:S(2)}) collective-permute-start(bf16[128,512]{1,0:T(8,128)(2,1)} %bitcast.227), channel_id=1, source_target_pairs={{0,0},{1,2},{2,4},{3,6},{4,1},{5,3},{6,5},{7,7},{8,8},{9,10},{10,1... | collective-permute-start | bytes 393224 | tf_op jit(solution)/shard_map/ppermute | solution.py:73
  40.7 181.5 %all-gather.5.cloned.1.call-start = ((), (), s32[]{:S(2)}) async-start(), calls=%async_computation.2 | async-start | bytes 8912896 | tf_op jit(solution)/shard_map/all_gather | solution.py:232
  55.6 30.9 %collective-permute-start.6 = (f32[8,1152]{1,0:T(8,128)S(1)}, f32[8,1152]{1,0:T(8,128)S(1)}, u32[]{:S(2)}, u32[]{:S(2)}) collective-permute-start(f32[8,1152]{1,0:T(8,128)S(1)} %get-tuple-element.47), channel_id=1, source_target_pairs={{0,24},{8,0},{16,8},{24,16},{32,56},{40,32},{48,40},{56,48},{64,88... | collective-permute-start | bytes 110600 | tf_op jit(solution)/shard_map/ppermute | solution.py:40
  56.2 30.4 %collective-permute-start.5 = (f32[8,1152]{1,0:T(8,128)S(1)}, f32[8,1152]{1,0:T(8,128)S(1)}, u32[]{:S(2)}, u32[]{:S(2)}) collective-permute-start(f32[8,1152]{1,0:T(8,128)S(1)} %get-tuple-element.47), channel_id=1, source_target_pairs={{0,16},{8,24},{16,0},{24,8},{32,48},{40,56},{48,32},{56,40},{64,80... | collective-permute-start | bytes 110600 | tf_op jit(solution)/shard_map/ppermute | solution.py:40
  58.6 28.0 %collective-permute-start.4 = (f32[8,1152]{1,0:T(8,128)S(1)}, f32[8,1152]{1,0:T(8,128)S(1)}, u32[]{:S(2)}, u32[]{:S(2)}) collective-permute-start(f32[8,1152]{1,0:T(8,128)S(1)} %get-tuple-element.47), channel_id=1, source_target_pairs={{0,8},{8,16},{16,24},{24,0},{32,40},{40,48},{48,56},{56,32},{64,72... | collective-permute-start | bytes 110600 | tf_op jit(solution)/shard_map/ppermute | solution.py:40
  89.4 11.1 %collective-permute-start.9 = (f32[4,8,1152]{2,1,0:T(8,128)S(1)}, f32[4,8,1152]{2,1,0:T(8,128)S(1)}, u32[]{:S(2)}, u32[]{:S(2)}) collective-permute-start(f32[4,8,1152]{2,1,0:T(8,128)S(1)} %broadcast_select_fusion.3), channel_id=1, source_target_pairs={{0,96},{8,104},{16,112},{24,120},{32,0},{40,8},{48,16},{56,24},{64... | collective-permute-start | bytes 442376 | tf_op jit(solution)/shard_map/ppermute | solution.py:45
  92.4 11.4 %collective-permute-start.8 = (f32[4,8,1152]{2,1,0:T(8,128)S(1)}, f32[4,8,1152]{2,1,0:T(8,128)S(1)}, u32[]{:S(2)}, u32[]{:S(2)}) collective-permute-start(f32[4,8,1152]{2,1,0:T(8,128)S(1)} %broadcast_select_fusion.3), channel_id=1, source_target_pairs={{0,64},{8,72},{16,80},{24,88},{32,96},{40,104},{48,112},{56,120},{... | collective-permute-start | bytes 442376 | tf_op jit(solution)/shard_map/ppermute | solution.py:45
  93.1 13.4 %collective-permute-start.7 = (f32[4,8,1152]{2,1,0:T(8,128)S(1)}, f32[4,8,1152]{2,1,0:T(8,128)S(1)}, u32[]{:S(2)}, u32[]{:S(2)}) collective-permute-start(f32[4,8,1152]{2,1,0:T(8,128)S(1)} %broadcast_select_fusion.3), channel_id=1, source_target_pairs={{0,32},{8,40},{16,48},{24,56},{32,64},{40,72},{48,80},{56,88},{64,... | collective-permute-start | bytes 442376 | tf_op jit(solution)/shard_map/ppermute | solution.py:45
  128.0 8.4 %collective-permute-start.14 = (bf16[128,512]{1,0:T(8,128)(2,1)S(1)}, bf16[128,512]{1,0:T(8,128)(2,1)S(1)}, u32[]{:S(2)}, u32[]{:S(2)}) collective-permute-start(bf16[128,512]{1,0:T(8,128)(2,1)S(1)} %bitcast.270), channel_id=1, source_target_pairs={{0,6},{1,0},{2,2},{3,4},{4,7},{5,1},{6,3},{7,5},{8,14},{9,8},{10,1... | collective-permute-start | bytes 393224 | tf_op jit(solution)/shard_map/ppermute | solution.py:73
  128.7 7.7 %collective-permute-start.13 = (bf16[128,512]{1,0:T(8,128)(2,1)S(1)}, bf16[128,512]{1,0:T(8,128)(2,1)S(1)}, u32[]{:S(2)}, u32[]{:S(2)}) collective-permute-start(bf16[128,512]{1,0:T(8,128)(2,1)S(1)} %bitcast.271), channel_id=1, source_target_pairs={{0,4},{1,6},{2,0},{3,2},{4,5},{5,7},{6,1},{7,3},{8,12},{9,14},{10,... | collective-permute-start | bytes 393224 | tf_op jit(solution)/shard_map/ppermute | solution.py:73
  131.9 8.3 %collective-permute-start.12 = (bf16[128,512]{1,0:T(8,128)(2,1)S(1)}, bf16[128,512]{1,0:T(8,128)(2,1)S(1)}, u32[]{:S(2)}, u32[]{:S(2)}) collective-permute-start(bf16[128,512]{1,0:T(8,128)(2,1)S(1)} %bitcast.272), channel_id=1, source_target_pairs={{0,2},{1,4},{2,6},{3,0},{4,3},{5,5},{6,7},{7,1},{8,10},{9,12},{10,... | collective-permute-start | bytes 393224 | tf_op jit(solution)/shard_map/ppermute | solution.py:73
  134.4 6.7 %collective-permute-start.11 = (bf16[128,512]{1,0:T(8,128)(2,1)S(1)}, bf16[128,512]{1,0:T(8,128)(2,1)S(1)}, u32[]{:S(2)}, u32[]{:S(2)}) collective-permute-start(bf16[128,512]{1,0:T(8,128)(2,1)S(1)} %bitcast.273), channel_id=1, source_target_pairs={{0,0},{1,2},{2,4},{3,6},{4,1},{5,3},{6,5},{7,7},{8,8},{9,10},{10,1... | collective-permute-start | bytes 393224 | tf_op jit(solution)/shard_map/ppermute | solution.py:73
  150.6 190.1 %reduce-scatter.2.cloned.1.call-start = ((), (), s32[]{:S(2)}) async-start(), calls=%async_computation.3 | async-start | bytes 8912896 | tf_op jit(solution)/shard_map/reduce_scatter | solution.py:250
  164.7 3.7 collective-permute-start.10
  234.4 3.5 collective-permute-start.15
  343.2 10.0 %collective-permute-start.19 = (bf16[128,512]{1,0:T(8,128)(2,1)S(1)}, bf16[128,512]{1,0:T(8,128)(2,1)S(1)}, u32[]{:S(2)}, u32[]{:S(2)}) collective-permute-start(bf16[128,512]{1,0:T(8,128)(2,1)S(1)} %bitcast.262), channel_id=1, source_target_pairs={{6,0},{0,1},{2,2},{4,3},{7,4},{1,5},{3,6},{5,7},{14,8},{8,9},{10,1... | collective-permute-start | bytes 393224 | tf_op jit(solution)/shard_map/ppermute | solution.py:89
  343.9 9.5 %collective-permute-start.18 = (bf16[128,512]{1,0:T(8,128)(2,1)S(1)}, bf16[128,512]{1,0:T(8,128)(2,1)S(1)}, u32[]{:S(2)}, u32[]{:S(2)}) collective-permute-start(bf16[128,512]{1,0:T(8,128)(2,1)S(1)} %bitcast.264), channel_id=1, source_target_pairs={{4,0},{6,1},{0,2},{2,3},{5,4},{7,5},{1,6},{3,7},{12,8},{14,9},{8,1... | collective-permute-start | bytes 393224 | tf_op jit(solution)/shard_map/ppermute | solution.py:89
  347.6 8.4 %collective-permute-start.17 = (bf16[128,512]{1,0:T(8,128)(2,1)S(1)}, bf16[128,512]{1,0:T(8,128)(2,1)S(1)}, u32[]{:S(2)}, u32[]{:S(2)}) collective-permute-start(bf16[128,512]{1,0:T(8,128)(2,1)S(1)} %bitcast.266), channel_id=1, source_target_pairs={{2,0},{4,1},{6,2},{0,3},{3,4},{5,5},{7,6},{1,7},{10,8},{12,9},{14,... | collective-permute-start | bytes 393224 | tf_op jit(solution)/shard_map/ppermute | solution.py:89
  349.5 9.2 %collective-permute-start.16 = (bf16[128,512]{1,0:T(8,128)(2,1)S(1)}, bf16[128,512]{1,0:T(8,128)(2,1)S(1)}, u32[]{:S(2)}, u32[]{:S(2)}) collective-permute-start(bf16[128,512]{1,0:T(8,128)(2,1)S(1)} %bitcast.268), channel_id=1, source_target_pairs={{0,0},{2,1},{4,2},{6,3},{1,4},{3,5},{5,6},{7,7},{8,8},{10,9},{12,1... | collective-permute-start | bytes 393224 | tf_op jit(solution)/shard_map/ppermute | solution.py:89
  377.4 17.1 %collective-permute-start.22 = (bf16[8,1024]{1,0:T(8,128)(2,1)S(1)}, bf16[8,1024]{1,0:T(8,128)(2,1)S(1)}, u32[]{:S(2)}, u32[]{:S(2)}) collective-permute-start(bf16[8,1024]{1,0:T(8,128)(2,1)S(1)} %convert_element_type.174), channel_id=1, source_target_pairs={{0,24},{8,0},{16,8},{24,16},{32,56},{40,32},{48,40},{56,48},{64,88... | collective-permute-start | bytes 49160 | tf_op jit(solution)/shard_map/ppermute | solution.py:40
  378.3 16.2 %collective-permute-start.21 = (bf16[8,1024]{1,0:T(8,128)(2,1)S(1)}, bf16[8,1024]{1,0:T(8,128)(2,1)S(1)}, u32[]{:S(2)}, u32[]{:S(2)}) collective-permute-start(bf16[8,1024]{1,0:T(8,128)(2,1)S(1)} %convert_element_type.174), channel_id=1, source_target_pairs={{0,16},{8,24},{16,0},{24,8},{32,48},{40,56},{48,32},{56,40},{64,80... | collective-permute-start | bytes 49160 | tf_op jit(solution)/shard_map/ppermute | solution.py:40
  380.4 14.1 %collective-permute-start.20 = (bf16[8,1024]{1,0:T(8,128)(2,1)S(1)}, bf16[8,1024]{1,0:T(8,128)(2,1)S(1)}, u32[]{:S(2)}, u32[]{:S(2)}) collective-permute-start(bf16[8,1024]{1,0:T(8,128)(2,1)S(1)} %convert_element_type.174), channel_id=1, source_target_pairs={{0,8},{8,16},{16,24},{24,0},{32,40},{40,48},{48,56},{56,32},{64,72... | collective-permute-start | bytes 49160 | tf_op jit(solution)/shard_map/ppermute | solution.py:40
  395.3 4.3 %collective-permute-start.25 = (bf16[4,8,1024]{2,1,0:T(8,128)(2,1)S(1)}, bf16[4,8,1024]{2,1,0:T(8,128)(2,1)S(1)}, u32[]{:S(2)}, u32[]{:S(2)}) collective-permute-start(bf16[4,8,1024]{2,1,0:T(8,128)(2,1)S(1)} %broadcast_select_fusion.4), channel_id=1, source_target_pairs={{0,96},{8,104},{16,112},{24,120},{32,0},{40,8},{48,16},{56,24},{64... | collective-permute-start | bytes 196616 | tf_op jit(solution)/shard_map/ppermute | solution.py:45
  396.2 5.8 %collective-permute-start.24 = (bf16[4,8,1024]{2,1,0:T(8,128)(2,1)S(1)}, bf16[4,8,1024]{2,1,0:T(8,128)(2,1)S(1)}, u32[]{:S(2)}, u32[]{:S(2)}) collective-permute-start(bf16[4,8,1024]{2,1,0:T(8,128)(2,1)S(1)} %broadcast_select_fusion.4), channel_id=1, source_target_pairs={{0,64},{8,72},{16,80},{24,88},{32,96},{40,104},{48,112},{56,120},{... | collective-permute-start | bytes 196616 | tf_op jit(solution)/shard_map/ppermute | solution.py:45
  397.6 5.5 %collective-permute-start.23 = (bf16[4,8,1024]{2,1,0:T(8,128)(2,1)S(1)}, bf16[4,8,1024]{2,1,0:T(8,128)(2,1)S(1)}, u32[]{:S(2)}, u32[]{:S(2)}) collective-permute-start(bf16[4,8,1024]{2,1,0:T(8,128)(2,1)S(1)} %broadcast_select_fusion.4), channel_id=1, source_target_pairs={{0,32},{8,40},{16,48},{24,56},{32,64},{40,72},{48,80},{56,88},{64,... | collective-permute-start | bytes 196616 | tf_op jit(solution)/shard_map/ppermute | solution.py:45
  (60 other events, 423.4 us)
Sparse Core Ops, SparseCore 0:
  40.9 79.3 all-gather.2
  150.7 71.4 all-gather.4
  255.5 85.0 reduce-scatter.1
